TPU v7x, 32 devices: a whole 2x2x4 slice. The times are simulated.
32 devices in a mesh: kvh: 2 (over x), seq: 16 (over z, y, core).
Axes of the slice: x: 2, y: 2, z: 4, core: 2. Of those that a mesh axis runs over, the one named last changes fastest.
Arguments:
- queries: bfloat16 [6144, 2048], P('seq', 'kvh'), may hold values from -180 to 180
- own_kv: bfloat16 [6144, 512], P('seq', 'kvh'), may hold values from -7 to 7
- library: bfloat16 [48, 128, 512], P('seq', None, 'kvh'), may hold values from -6 to 6
- fresh_kv: bfloat16 [16, 16, 64, 512], P('seq', None, 'kvh'), may hold values from -6 to 6
- retrieved: int32 [16, 16], P('seq'), may hold values from 0 to 47, as said below
- stretch_slot: int32 [48], replicated, may hold values from 0 to 47, as said below
- stretch_len: int32 [48], replicated, may hold values from 32 to 128
- recompute_pos: int32 [16, 16, 64], P('seq'), may hold values from 0 to 127, as said below
Outputs:
- attended: bfloat16 [6144, 2048], P('seq', 'kvh')
Inputs may be any that keep to these rules, and one draw needn't show every extreme that they name: The 16 rows r[c, j] = stretch_slot[retrieved[c, j]] of one context have distinct owners r[c, j] // 3. `stretch_slot`: each library row is named once. `recompute_pos`: position i of a stretch's list lies in [i * 2, (i + 1) * 2).
All inputs are finite; a program needn't handle non-finite values.
Results may differ from a plain program's by a relative error of at most 0.0049.
Values may be sent and summed in bfloat16 or wider, within the bound.
No kernel may reach another device: no remote copies, remote signals or barrier semaphores. Data moves between devices by JAX's collectives and lax.ppermute only.
A program may use at most 64 MiB of HBM per device.

v0:
```python
import jax
import jax.numpy as jnp
from jax import lax
from jax.sharding import PartitionSpec as P

HD = 128
CL = 128
NCH = 16


def lookup(table, indices):
    hits = indices[..., None] == jnp.arange(table.shape[0], dtype=jnp.int32)
    return jnp.sum(jnp.where(hits, table, 0), axis=-1)


def project_keys(query_head, key_block):
    return lax.dot_general(
        query_head, key_block, (((1,), (1,)), ((), ())), preferred_element_type=jnp.float32
    )


def per_device(
    queries, own_kv, library, fresh_kv, retrieved, stretch_slot, stretch_len, recompute_pos
):
    wanted = lookup(stretch_slot, retrieved[0])
    piece = lax.all_gather(library, "seq", axis=0, tiled=True)
    count = piece.shape[0]
    inside = (wanted >= 0) & (wanted < count)
    taken = piece[jnp.clip(wanted, 0, count - 1)]
    blocks = jnp.where(inside[:, None, None], taken, jnp.zeros((), piece.dtype))
    fresh = lax.all_to_all(fresh_kv, "kvh", split_axis=3, concat_axis=2, tiled=True)
    limits = lookup(stretch_len, wanted)
    stretch_index = jnp.arange(NCH, dtype=jnp.int32)[:, None]
    blocks = blocks.at[stretch_index, recompute_pos[0]].set(fresh[0])
    span = NCH * CL
    key_rows = jnp.concatenate([blocks[:, :, :HD].reshape(span, HD), own_kv[:, :HD]], 0)
    value_rows = jnp.concatenate([blocks[:, :, HD:].reshape(span, HD), own_kv[:, HD:]], 0)
    row_count = queries.shape[0]
    column = jnp.arange(span + row_count, dtype=jnp.int32)
    row_index = jnp.arange(row_count, dtype=jnp.int32)
    owner_stretch = jnp.minimum(column // CL, NCH - 1)
    column_limit = jnp.sum(
        jnp.where(owner_stretch[:, None] == jnp.arange(NCH, dtype=jnp.int32), limits[None, :], 0), 1
    )
    visible = jnp.where(
        column[None, :] < span,
        (column % CL)[None, :] < column_limit[None, :],
        (column - span)[None, :] <= row_index[:, None],
    )
    score_scale = HD ** (-0.5)
    outputs = []
    for group_head in range(queries.shape[1] // HD):
        query_head = queries[:, group_head * HD : (group_head + 1) * HD]
        scores = project_keys(query_head, key_rows)
        scores = jnp.where(visible, scores * score_scale, -jnp.inf)
        highest = jnp.max(scores, axis=1, keepdims=True)
        expo = jnp.exp(scores - highest)
        weights = (expo / jnp.sum(expo, axis=1, keepdims=True)).astype(jnp.bfloat16)
        mixed = jnp.dot(weights, value_rows, preferred_element_type=jnp.float32)
        outputs.append(mixed.astype(jnp.bfloat16))
    return jnp.concatenate(outputs, 1)


def solution(mesh):
    placed = (
        P("seq", "kvh"),
        P("seq", "kvh"),
        P("seq", None, "kvh"),
        P("seq", None, "kvh", None),
        P("seq", None),
        P(),
        P(),
        P("seq", None, None),
    )
    return jax.shard_map(
        per_device, mesh=mesh, in_specs=placed, out_specs=P("seq", "kvh"), check_vma=False
    )
```

profile of v0, /device:TPU:0, one launch (start us, length us, event | category | flops | bytes accessed | tf_op | source)
XLA Modules:
  0.0 96.4 jit_solution(6478403487636148404)
XLA Ops:
  6.6 0.0 all-gather.2.cloned.1.call-start
  6.6 0.7 all-gather.2.cloned.1.call-update
  7.3 2.9 %copy.17 = bf16[1,16,32,512]{2,1,0,3:T(8,128)(2,1)S(1)} copy(bf16[1,16,32,512]{3,2,1,0:T(8,128)(2,1)} %param.11) | data formatting | bytes 1048576 | tf_op args[3]
  10.2 2.8 %reshape.137 = bf16[2,2,65536]{2,1,0:T(2,128)(2,1)} reshape(bf16[512,1,16,32]{3,2,1,0:T(8,128)(2,1)S(1)} %bitcast.51) | data formatting | bytes 1048576
  13.0 4.2 %all-to-all-start = ((bf16[2,2,65536]{2,1,0:T(2,128)(2,1)}), bf16[2,2,65536]{2,1,0:T(2,128)(2,1)S(1)}, u32[]{:S(2)}, u32[]{:S(2)}) async-start(bf16[2,2,65536]{2,1,0:T(2,128)(2,1)} %reshape.137), calls=%async_computation | async-start | bytes 1048576 | tf_op jit(solution)/shard_map/all_to_all | solution.py:31
  17.2 0.0 copy-done.2
  17.2 0.1 multiply_reduce_fusion
  17.3 0.1 and_reduce_fusion
  17.4 0.0 copy-done.6
  17.4 0.2 select_reduce_fusion.2
  17.6 0.2 select_reduce_fusion.1
  17.8 0.1 select_reduce_fusion
  18.0 0.1 reshape.130
  18.1 7.9 %all-to-all-done = bf16[2,2,65536]{2,1,0:T(2,128)(2,1)S(1)} async-done(((bf16[2,2,65536]{2,1,0:T(2,128)(2,1)}), bf16[2,2,65536]{2,1,0:T(2,128)(2,1)S(1)}, u32[]{:S(2)}, u32[]{:S(2)}) %all-to-all-start) | async-done | bytes 524320 | tf_op jit(solution)/shard_map/all_to_all | solution.py:31
  25.9 1.0 %reshape.138 = bf16[512,1,16,32]{3,2,1,0:T(8,128)(2,1)S(1)} reshape(bf16[2,2,65536]{2,1,0:T(2,128)(2,1)S(1)} %all-to-all-done) | data formatting | bytes 1048576
  26.9 1.8 %copy.21 = bf16[1,16,32,2,256]{4,3,2,1,0:T(2,128)(2,1)S(1)} copy(bf16[1,16,32,2,256]{2,1,4,3,0:T(8,128)(2,1)S(1)} %bitcast.50) | data formatting | bytes 1048576 | tf_op jit(solution)/shard_map/all_to_all | solution.py:31
  28.8 0.1 copy.19
  28.9 29.0 %all-gather.2.cloned.1.call-done = bf16[48,128,256]{2,1,0:T(8,128)(2,1)} async-done(((bf16[3,128,256]{2,1,0:T(8,128)(2,1)}), bf16[48,128,256]{2,1,0:T(8,128)(2,1)}) %all-gather.2.cloned.1.call-update) | async-done | bytes 3145744 | tf_op jit(solution)/shard_map/all_gather | solution.py:26
  57.9 2.5 %gather_fusion = bf16[16,128,256]{2,1,0:T(8,128)(2,1)S(1)} fusion(bf16[48,128,256]{2,1,0:T(8,128)(2,1)} %all-gather.2.cloned.1.call-done, s32[1024]{0:T(1024)S(1)} %pad_clamp_fusion), kind=kCustom, calls=%fused_computation | custom fusion | bytes 2097216 | tf_op jit(solution)/shard_map/gather | solution.py:29
  60.4 0.1 broadcast_select_fusion
  60.5 0.0 copy-start.4
  60.5 5.7 %scatter_fusion = bf16[2048,256]{1,0:T(8,128)(2,1)S(1)} fusion(bf16[2048,256]{1,0:T(8,128)(2,1)S(1)} %bitcast.48, s32[1024]{0:T(1024)S(1)} %reshape.130, bf16[1024,256]{1,0:T(8,128)(2,1)S(1)} %bitcast.52), kind=kCustom, calls=%fused_computation.1 | custom fusion | bytes 1576960
  66.2 0.2 fusion.65
  66.4 1.2 %fusion.67 = (f32[384]{0:T(512)S(1)}, f32[384,2432]{0,1:T(8,128)S(1)}) fusion(bf16[384,1024]{1,0:T(8,128)(2,1)S(1)} %copy-done.4, bf16[384,128]{1,0:T(8,128)(2,1)S(1)} %get-tuple-element.8, bf16[2048,128]{1,0:T(8,128)(2,1)S(1)} %bitcast.62, s32[2432]{0:T(1024)S(1)} %iota_add_fusion, pred[2432]{0:T(1024)(128)(4,1)S(1)} %get-tuple-element.25, ...), kind=kOutput, calls=%fused_computation.118 | convolution fusion | flops 244989568 | bytes 4476416 | tf_op jit(solution)/shard_map/dot_general | solution.py:17
  67.6 1.2 %fusion.68 = (f32[384]{0:T(512)S(1)}, f32[384,2432]{0,1:T(8,128)S(1)}) fusion(bf16[384,1024]{1,0:T(8,128)(2,1)S(1)} %copy-done.4, bf16[384,128]{1,0:T(8,128)(2,1)S(1)} %get-tuple-element.8, bf16[2048,128]{1,0:T(8,128)(2,1)S(1)} %bitcast.63, s32[2432]{0:T(1024)S(1)} %iota_add_fusion, pred[2432]{0:T(1024)(128)(4,1)S(1)} %get-tuple-element.25, ...), kind=kOutput, calls=%fused_computation.119 | convolution fusion | flops 244989568 | bytes 4476416 | tf_op jit(solution)/shard_map/dot_general | solution.py:17
  68.8 1.2 %fusion.69 = (f32[384]{0:T(512)S(1)}, f32[384,2432]{0,1:T(8,128)S(1)}) fusion(bf16[384,1024]{1,0:T(8,128)(2,1)S(1)} %copy-done.4, bf16[384,128]{1,0:T(8,128)(2,1)S(1)} %get-tuple-element.8, bf16[2048,128]{1,0:T(8,128)(2,1)S(1)} %bitcast.64, s32[2432]{0:T(1024)S(1)} %iota_add_fusion, pred[2432]{0:T(1024)(128)(4,1)S(1)} %get-tuple-element.25, ...), kind=kOutput, calls=%fused_computation.120 | convolution fusion | flops 244989568 | bytes 4476416 | tf_op jit(solution)/shard_map/dot_general | solution.py:17
  70.1 1.2 %fusion.70 = (f32[384]{0:T(512)S(1)}, f32[384,2432]{0,1:T(8,128)S(1)}) fusion(bf16[384,1024]{1,0:T(8,128)(2,1)S(1)} %copy-done.4, bf16[384,128]{1,0:T(8,128)(2,1)S(1)} %get-tuple-element.8, bf16[2048,128]{1,0:T(8,128)(2,1)S(1)} %bitcast.65, s32[2432]{0:T(1024)S(1)} %iota_add_fusion, pred[2432]{0:T(1024)(128)(4,1)S(1)} %get-tuple-element.25, ...), kind=kOutput, calls=%fused_computation.121 | convolution fusion | flops 244989568 | bytes 4476416 | tf_op jit(solution)/shard_map/dot_general | solution.py:17
  71.3 1.2 %fusion.71 = (f32[384]{0:T(512)S(1)}, f32[384,2432]{0,1:T(8,128)S(1)}) fusion(bf16[384,1024]{1,0:T(8,128)(2,1)S(1)} %copy-done.4, bf16[384,128]{1,0:T(8,128)(2,1)S(1)} %get-tuple-element.8, bf16[2048,128]{1,0:T(8,128)(2,1)S(1)} %bitcast.66, s32[2432]{0:T(1024)S(1)} %iota_add_fusion, pred[2432]{0:T(1024)(128)(4,1)S(1)} %get-tuple-element.25, ...), kind=kOutput, calls=%fused_computation.122 | convolution fusion | flops 244989568 | bytes 4476416 | tf_op jit(solution)/shard_map/dot_general | solution.py:17
  72.5 1.2 %fusion.72 = (f32[384]{0:T(512)S(1)}, f32[384,2432]{0,1:T(8,128)S(1)}) fusion(bf16[384,1024]{1,0:T(8,128)(2,1)S(1)} %copy-done.4, bf16[384,128]{1,0:T(8,128)(2,1)S(1)} %get-tuple-element.8, bf16[2048,128]{1,0:T(8,128)(2,1)S(1)} %bitcast.67, s32[2432]{0:T(1024)S(1)} %iota_add_fusion, pred[2432]{0:T(1024)(128)(4,1)S(1)} %get-tuple-element.25, ...), kind=kOutput, calls=%fused_computation.123 | convolution fusion | flops 244989568 | bytes 4476416 | tf_op jit(solution)/shard_map/dot_general | solution.py:17
  73.7 1.2 %fusion.73 = (f32[384]{0:T(512)S(1)}, f32[384,2432]{0,1:T(8,128)S(1)}) fusion(bf16[384,1024]{1,0:T(8,128)(2,1)S(1)} %copy-done.4, bf16[384,128]{1,0:T(8,128)(2,1)S(1)} %get-tuple-element.8, bf16[2048,128]{1,0:T(8,128)(2,1)S(1)} %bitcast.68, s32[2432]{0:T(1024)S(1)} %iota_add_fusion, pred[2432]{0:T(1024)(128)(4,1)S(1)} %get-tuple-element.25, ...), kind=kOutput, calls=%fused_computation.124 | convolution fusion | flops 244989568 | bytes 4476416 | tf_op jit(solution)/shard_map/dot_general | solution.py:17
  74.9 1.2 %fusion.74 = (f32[384]{0:T(512)S(1)}, f32[384,2432]{0,1:T(8,128)S(1)}) fusion(bf16[384,1024]{1,0:T(8,128)(2,1)S(1)} %copy-done.4, bf16[384,128]{1,0:T(8,128)(2,1)S(1)} %get-tuple-element.8, bf16[2048,128]{1,0:T(8,128)(2,1)S(1)} %bitcast.69, s32[2432]{0:T(1024)S(1)} %iota_add_fusion, pred[2432]{0:T(1024)(128)(4,1)S(1)} %get-tuple-element.25, ...), kind=kOutput, calls=%fused_computation.125 | convolution fusion | flops 244989568 | bytes 4476416 | tf_op jit(solution)/shard_map/dot_general | solution.py:17
  76.1 0.6 fusion.17
  76.7 0.6 fusion.18
  77.4 0.9 fusion.41
  78.3 1.1 %fusion.42 = bf16[384,1024]{0,1:T(8,128)(2,1)S(1)} fusion(bf16[384,1024]{0,1:T(8,128)(2,1)S(1)} %fusion.41, f32[384,2432]{0,1:T(8,128)S(1)} %get-tuple-element.12, f32[384]{0:T(512)S(1)} %fusion.18, f32[384]{0:T(512)S(1)} %get-tuple-element.11, bf16[384,128]{1,0:T(8,128)(2,1)S(1)} %get-tuple-element.7, bf16[2048,128]{1,0:T(8,128)(2,1)S(1)} %bitcast.55), kind=kOutput, calls=%fused_computation.69 | convolution fusion | flops 243171328 | bytes 4460544 | tf_op jit(solution)/shard_map/dot_general | solution.py:59
  79.3 0.6 fusion.19
  80.0 0.9 fusion.43
  80.9 0.6 fusion.20
  81.5 0.9 fusion.44
  82.4 0.6 fusion.21
  83.0 0.9 fusion.45
  83.9 0.6 fusion.22
  84.5 0.9 fusion.46
  85.4 0.6 fusion.23
  86.0 0.9 fusion.47
  86.9 0.6 fusion.24
  87.5 0.9 fusion.48
  88.4 1.2 %copy.20 = bf16[384,1024]{1,0:T(8,128)(2,1)} copy(bf16[384,1024]{0,1:T(8,128)(2,1)S(1)} %fusion.48) | data formatting | bytes 1572864 | tf_op jit(solution)/shard_map/concatenate | solution.py:61
  (23 shorter events, 0.1 us)
Async XLA Ops:
  6.5 10.7 %copy-start.2 = (s32[2]{0:T(128)S(1)}, s32[2]{0:T(128)}, u32[]{:S(2)}) copy-start(s32[2]{0:T(128)} %constant.61) | copy-start | bytes 28
  6.5 10.8 %copy-start.3 = (s32[2]{0:T(128)S(1)}, s32[2]{0:T(128)}, u32[]{:S(2)}) copy-start(s32[2]{0:T(128)} %constant.64) | copy-start | bytes 28
  6.5 10.7 %copy-start.1 = (s32[1,16,64]{2,1,0:T(8,128)S(1)}, s32[1,16,64]{2,1,0:T(8,128)}, u32[]{:S(2)}) copy-start(s32[1,16,64]{2,1,0:T(8,128)} %param.15) | copy-start | bytes 12292
  6.5 10.9 %copy-start.5 = (s32[48]{0:T(128)S(1)}, s32[48]{0:T(128)}, u32[]{:S(2)}) copy-start(s32[48]{0:T(128)} %param.13) | copy-start | bytes 580
  6.5 10.9 %copy-start.6 = (s32[1,16]{1,0:T(1,128)S(1)}, s32[1,16]{1,0:T(1,128)}, u32[]{:S(2)}) copy-start(s32[1,16]{1,0:T(1,128)} %param.12) | copy-start | bytes 196
  6.5 11.0 %copy-start.7 = (s32[48]{0:T(128)S(1)}, s32[48]{0:T(128)}, u32[]{:S(2)}) copy-start(s32[48]{0:T(128)} %param.14) | copy-start | bytes 580
  6.6 11.5 %copy-start = (bf16[384,256]{1,0:T(8,128)(2,1)S(1)}, bf16[384,256]{1,0:T(8,128)(2,1)}, u32[]{:S(2)}) copy-start(bf16[384,256]{1,0:T(8,128)(2,1)} %param.9) | copy-start | bytes 589828
  6.6 51.3 %all-gather.2.cloned.1.call-start = ((), (), s32[]{:S(2)}) async-start(), calls=%async_computation.1 | async-start | bytes 3342336 | tf_op jit(solution)/shard_map/all_gather | solution.py:26
  13.0 12.9 %all-to-all-start = ((bf16[2,2,65536]{2,1,0:T(2,128)(2,1)}), bf16[2,2,65536]{2,1,0:T(2,128)(2,1)S(1)}, u32[]{:S(2)}, u32[]{:S(2)}) async-start(bf16[2,2,65536]{2,1,0:T(2,128)(2,1)} %reshape.137), calls=%async_computation | async-start | bytes 1048576 | tf_op jit(solution)/shard_map/all_to_all | solution.py:31
  60.5 5.9 %copy-start.4 = (bf16[384,1024]{1,0:T(8,128)(2,1)S(1)}, bf16[384,1024]{1,0:T(8,128)(2,1)}, u32[]{:S(2)}) copy-start(bf16[384,1024]{1,0:T(8,128)(2,1)} %param.8) | copy-start | bytes 2359300
Sparse Core Ops, SparseCore 0:
  9.7 48.1 all-gather.1
where the time goes:
time: 96.6 us; the launch traced here: 96.4 us
  waiting for transfers between devices  37.5 us (39%)
  local copies, waits for them, and re-layouts  18.2 us (19%)
  matrix products  16.9 us (17%)
  between operations  13.7 us (14%)
  other arithmetic  5.87 us (6%)
  starting transfers between devices  4.24 us (4%)
    all_gather x1, waiting for transfers between devices, per_device(): piece = lax.all_gather(library, 'seq', axis=0, tiled=True)  29 us
    unnamed x21, local copies, waits for them, and re-layouts  12.5 us
    dot_general x8, matrix products, project_keys(): lax.dot_general(query_head, key_block, (((1,), (1,)), ((), ())), preferre...  9.68 us
    all_to_all x1, waiting for transfers between devices, per_device(): lax.all_to_all(fresh_kv, 'kvh', split_axis=3, concat_axis=2, tiled=True)  7.86 us
    dot_general x8, matrix products, per_device(): mixed = jnp.dot(weights, value_rows, preferred_element_type=jnp.float32)  7.19 us
    reduce_sum x8, other arithmetic, per_device(): weights = (expo / jnp.sum(expo, axis=1, keepdims=True)).astype(jnp.bfloat16)  5.06 us
    all_to_all x1, starting transfers between devices, per_device(): lax.all_to_all(fresh_kv, 'kvh', split_axis=3, concat_axis=2, tiled=True)  4.21 us
    gather x1, local copies, waits for them, and re-layouts, per_device(): taken = piece[jnp.clip(wanted, 0, count - 1)]  2.5 us
  transfers between devices with their start and end apart: 2, of which 2 were waited for; matrix products, arithmetic and copies ran while one was open for 10% of the time, Pallas kernels for 0%

commit v1 on v0

v1 whole, which is shorter than its diff:
```python
import functools

import jax
import jax.numpy as jnp
from jax import lax
from jax.experimental import pallas as pl
from jax.experimental.pallas import tpu as pltpu
from jax.sharding import PartitionSpec as P

HD = 128
CL = 128
TR = 128


def lookup(table, indices):
    hits = indices[..., None] == jnp.arange(table.shape[0], dtype=jnp.int32)
    return jnp.sum(jnp.where(hits, table, 0), axis=-1)


def attend_kernel(owner_ref, bias_ref, pos_ref, recv_ref, fresh_ref, own_ref, q_ref, out_ref, kb_ref, vb_ref):
    nch, nrec = pos_ref.shape
    rows = q_ref.shape[0]
    scale = HD ** (-0.5)

    @pl.when(pl.program_id(0) == 0)
    def _():
        def build(j, carry):
            lib = recv_ref[owner_ref[j]]
            where_at = pos_ref[pl.ds(j, 1), :]
            pick = lax.broadcasted_iota(jnp.int32, (CL, nrec), 0) == where_at
            up = jnp.dot(pick.astype(jnp.bfloat16), fresh_ref[j], preferred_element_type=jnp.float32)
            hit = jnp.max(pick.astype(jnp.float32), axis=1, keepdims=True) > 0
            block = jnp.where(hit, up.astype(jnp.bfloat16), lib)
            at = pl.ds(pl.multiple_of(j * CL, CL), CL)
            kb_ref[at, :] = block[:, :HD]
            vb_ref[at, :] = block[:, HD:]
            return carry

        lax.fori_loop(0, nch, build, 0)

    dims = (((1,), (1,)), ((), ()))
    for t in range(rows // TR):
        qt = q_ref[t * TR:(t + 1) * TR, :]
        s1 = lax.dot_general(qt, kb_ref[...], dims, preferred_element_type=jnp.float32)
        s1 = s1 * scale + bias_ref[...]
        kk = (t + 1) * TR
        s2 = lax.dot_general(qt, own_ref[:kk, :HD], dims, preferred_element_type=jnp.float32) * scale
        row = lax.broadcasted_iota(jnp.int32, (TR, kk), 0) + t * TR
        col = lax.broadcasted_iota(jnp.int32, (TR, kk), 1)
        s2 = jnp.where(col <= row, s2, -jnp.inf)
        top = jnp.maximum(jnp.max(s1, axis=1, keepdims=True), jnp.max(s2, axis=1, keepdims=True))
        e1 = jnp.exp(s1 - top)
        e2 = jnp.exp(s2 - top)
        inv = 1.0 / (jnp.sum(e1, axis=1, keepdims=True) + jnp.sum(e2, axis=1, keepdims=True))
        w1 = (e1 * inv).astype(jnp.bfloat16)
        w2 = (e2 * inv).astype(jnp.bfloat16)
        mixed = jnp.dot(w1, vb_ref[...], preferred_element_type=jnp.float32)
        mixed = mixed + jnp.dot(w2, own_ref[:kk, HD:], preferred_element_type=jnp.float32)
        out_ref[t * TR:(t + 1) * TR, :] = mixed.astype(out_ref.dtype)


def attend(owner, bias, pos, recv, fresh, own_kv, queries):
    rows, width = queries.shape
    heads = width // HD
    nch, nrec = pos.shape
    span = nch * CL
    keys = span + rows
    flops = 4 * heads * rows * keys * HD + 2 * nch * CL * nrec * 2 * HD
    bytes_accessed = 2 * (recv.size + fresh.size + own_kv.size + 2 * queries.size) + 4 * (bias.size + pos.size)

    def full(shape):
        return pl.BlockSpec(shape, lambda g, o: (0,) * len(shape))

    grid_spec = pltpu.PrefetchScalarGridSpec(
        num_scalar_prefetch=1,
        grid=(heads,),
        in_specs=[
            full(bias.shape),
            full(pos.shape),
            full(recv.shape),
            full(fresh.shape),
            full(own_kv.shape),
            pl.BlockSpec((rows, HD), lambda g, o: (0, g)),
        ],
        out_specs=pl.BlockSpec((rows, HD), lambda g, o: (0, g)),
        scratch_shapes=[pltpu.VMEM((span, HD), jnp.bfloat16), pltpu.VMEM((span, HD), jnp.bfloat16)],
    )
    return pl.pallas_call(
        attend_kernel,
        grid_spec=grid_spec,
        out_shape=jax.ShapeDtypeStruct(queries.shape, queries.dtype),
        compiler_params=pltpu.CompilerParams(dimension_semantics=("arbitrary",)),
        cost_estimate=pl.CostEstimate(
            flops=flops, bytes_accessed=bytes_accessed, transcendentals=heads * rows * keys
        ),
    )(owner, bias, pos, recv, fresh, own_kv, queries)


def per_device(
    n_seq, n_kvh, queries, own_kv, library, fresh_kv, retrieved, stretch_slot, stretch_len, recompute_pos
):
    per_owner = library.shape[0]
    wanted = lookup(stretch_slot, retrieved[0])
    owner = wanted // per_owner
    local = wanted % per_owner
    limits = lookup(stretch_len, wanted)

    devices = jnp.arange(n_seq, dtype=jnp.int32)
    request = jnp.sum(jnp.where(owner[None, :] == devices[:, None], local[None, :], 0), axis=1)
    asked = lax.all_to_all(request.reshape(n_seq, 1), "seq", 0, 0, tiled=True).reshape(n_seq)
    send = jnp.broadcast_to(library[0], (n_seq,) + library.shape[1:])
    for k in range(1, per_owner):
        send = jnp.where((asked == k)[:, None, None], library[k], send)
    recv = lax.all_to_all(send, "seq", 0, 0, tiled=True)

    me = lax.axis_index("kvh")
    width = own_kv.shape[1]
    tokens = fresh_kv.shape[2]
    fresh_local = fresh_kv[0]
    pos_local = recompute_pos[0]
    pieces = [lax.dynamic_slice_in_dim(fresh_local, me * width, width, 2)]
    places = [lax.dynamic_slice_in_dim(pos_local, me * tokens, tokens, 1)]
    for shift in range(1, n_kvh):
        target = lax.rem(me + shift, n_kvh)
        piece = lax.dynamic_slice_in_dim(fresh_local, target * width, width, 2)
        pairs = [(i, (i + shift) % n_kvh) for i in range(n_kvh)]
        pieces.append(lax.ppermute(piece, "kvh", pairs))
        source = lax.rem(me + n_kvh - shift, n_kvh)
        places.append(lax.dynamic_slice_in_dim(pos_local, source * tokens, tokens, 1))
    fresh = jnp.concatenate(pieces, 1)
    pos = jnp.concatenate(places, 1)

    column = jnp.arange(CL, dtype=jnp.int32)
    bias = jnp.where(column[None, :] < limits[:, None], 0.0, -jnp.inf).astype(jnp.float32)
    bias = bias.reshape(1, -1)
    return attend(owner, bias, pos, recv, fresh, own_kv, queries)


def solution(mesh):
    placed = (
        P("seq", "kvh"),
        P("seq", "kvh"),
        P("seq", None, "kvh"),
        P("seq", None, "kvh", None),
        P("seq", None),
        P(),
        P(),
        P("seq", None, None),
    )
    body = functools.partial(per_device, mesh.shape["seq"], mesh.shape["kvh"])
    return jax.shard_map(body, mesh=mesh, in_specs=placed, out_specs=P("seq", "kvh"), check_vma=False)
```

time: 96.6 us -> 71.7 us (0.74)
  the two profiles are of different devices: /device:TPU:0 before, /device:TPU:9 now
where the time goes in v1:
time: 71.7 us; the launch traced here: 71.4 us
  Pallas kernels  24.7 us (34%)
  waiting for transfers between devices  24.2 us (34%)
  starting transfers between devices  13.3 us (19%)
  local copies, waits for them, and re-layouts  4.54 us (6%)
  other arithmetic  4.51 us (6%)
    pallas_call x1, Pallas kernels, attend(): pl.pallas_call(attend_kernel, grid_spec=grid_spec, out_shape=jax.ShapeDty...  24.7 us
    all_to_all x1, waiting for transfers between devices, per_device(): recv = lax.all_to_all(send, 'seq', 0, 0, tiled=True)  16.4 us
    all_to_all x1, starting transfers between devices, per_device(): lax.all_to_all(request.reshape(n_seq, 1), 'seq', 0, 0, tiled=True)  6.61 us
    all_to_all x1, starting transfers between devices, per_device(): recv = lax.all_to_all(send, 'seq', 0, 0, tiled=True)  5.41 us
    ppermute x1, waiting for transfers between devices, per_device(): pieces.append(lax.ppermute(piece, 'kvh', pairs))  4.15 us
    all_to_all x1, waiting for transfers between devices, per_device(): lax.all_to_all(request.reshape(n_seq, 1), 'seq', 0, 0, tiled=True)  3.7 us
    unnamed x14, local copies, waits for them, and re-layouts  2.82 us
  transfers between devices with their start and end apart: 3, of which 3 were waited for; matrix products, arithmetic and copies ran while one was open for 5% of the time, Pallas kernels for 0%

profile of v1, /device:TPU:9, one launch (start us, length us, event | category | flops | bytes accessed | tf_op | source)
XLA Modules:
  0.0 71.4 jit_solution(11104192458894731970)
XLA Ops:
  0.0 0.0 copy-start.3
  0.0 0.0 copy-start.4
  0.0 0.7 copy-done.3
  0.7 0.0 copy-done.4
  0.7 0.2 select_reduce_fusion.2
  0.9 0.0 copy-start.6
  0.9 0.6 copy-done.6
  1.5 0.1 select_reduce_fusion
  1.6 0.7 copy.11
  2.3 6.6 %all-to-all-start = ((s32[16,1,1]{2,1,0:T(1,128)}), s32[16,1,1]{2,1,0:T(1,128)S(1)}, u32[]{:S(2)}, u32[]{:S(2)}) async-start(s32[16,1,1]{2,1,0:T(1,128)} %copy.11), calls=%async_computation | async-start | bytes 16384 | tf_op jit(solution)/shard_map/all_to_all | solution.py:110
  8.9 0.9 %slice_bitcast_fusion.2 = (bf16[128,256]{1,0:T(8,128)(2,1)S(1)}, bf16[128,256]{1,0:T(8,128)(2,1)S(1)}, bf16[128,256]{1,0:T(8,128)(2,1)S(1)}) fusion(bf16[3,128,256]{2,1,0:T(8,128)(2,1)} %param.10), kind=kLoop, calls=%fused_computation.6 | loop fusion | bytes 393216 | tf_op jit(solution)/shard_map/squeeze | solution.py:113
  9.8 3.7 %all-to-all-done = s32[16,1,1]{2,1,0:T(1,128)S(1)} async-done(((s32[16,1,1]{2,1,0:T(1,128)}), s32[16,1,1]{2,1,0:T(1,128)S(1)}, u32[]{:S(2)}, u32[]{:S(2)}) %all-to-all-start) | async-done | bytes 96 | tf_op jit(solution)/shard_map/all_to_all | solution.py:110
  13.5 0.7 compare_reduce_fusion.1
  14.2 1.2 %select_select_fusion = bf16[16,128,256]{2,1,0:T(8,128)(2,1)} fusion(pred[16]{0:T(512)(128)(4,1)S(1)} %get-tuple-element.6, pred[16]{0:T(512)(128)(4,1)S(1)} %get-tuple-element.5, bf16[128,256]{1,0:T(8,128)(2,1)S(1)} %get-tuple-element.10, bf16[128,256]{1,0:T(8,128)(2,1)S(1)} %get-tuple-element.11, bf16[128,256]{1,0:T(8,128)(2,1)S(1)} %get-tuple-element.9), kind=kLoop, calls=%fused_computation | loop fusion | flops 1048576 | bytes 1245216 | tf_op jit(solution)/shard_map/jit(_where)/select_n | solution.py:113
  15.3 0.0 copy-start.1
  15.4 5.4 %all-to-all-start.1 = ((bf16[16,128,256]{2,1,0:T(8,128)(2,1)}), bf16[16,128,256]{2,1,0:T(8,128)(2,1)S(1)}, u32[]{:S(2)}, u32[]{:S(2)}) async-start(bf16[16,128,256]{2,1,0:T(8,128)(2,1)} %select_select_fusion), calls=%async_computation.1 | async-start | bytes 2097152 | tf_op jit(solution)/shard_map/all_to_all | solution.py:114
  20.8 0.0 copy-done.1
  20.8 0.0 copy-start.2
  20.8 1.3 %collective-permute-start = (bf16[16,32,256]{2,1,0:T(8,128)(2,1)S(1)}, bf16[16,32,256]{2,1,0:T(8,128)(2,1)S(1)}, u32[]{:S(2)}, u32[]{:S(2)}) collective-permute-start(bf16[16,32,256]{2,1,0:T(8,128)(2,1)S(1)} %get-tuple-element.8), channel_id=1, source_target_pairs={{0,16},{16,0},{1,17},{17,1},{2,18},{18,2},{3,19},{19,3},{4,20},{20... | collective-permute-start | bytes 786440 | tf_op jit(solution)/shard_map/ppermute | solution.py:127
  22.1 0.0 copy-done.2
  22.1 0.0 copy-start.5
  22.1 0.1 dynamic-slice_bitcast_fusion.3
  22.2 0.6 copy-done.5
  22.8 0.2 select_reduce_fusion.1
  22.9 0.7 pad_add_fusion.pos_ref
  23.6 0.7 fusion
  24.3 4.1 %collective-permute-done = bf16[16,32,256]{2,1,0:T(8,128)(2,1)S(1)} collective-permute-done((bf16[16,32,256]{2,1,0:T(8,128)(2,1)S(1)}, bf16[16,32,256]{2,1,0:T(8,128)(2,1)S(1)}, u32[]{:S(2)}, u32[]{:S(2)}) %collective-permute-start) | collective-permute-done | bytes 262176 | tf_op jit(solution)/shard_map/ppermute | solution.py:127
  28.4 0.8 %pad_maximum_fusion.fresh_ref = bf16[16,64,256]{2,1,0:T(8,128)(2,1)} fusion(bf16[16,32,256]{2,1,0:T(8,128)(2,1)S(1)} %collective-permute-done, bf16[16,32,256]{2,1,0:T(8,128)(2,1)S(1)} %get-tuple-element.7), kind=kLoop, calls=%fused_computation.1 | loop fusion | flops 1048576 | bytes 1048576 | tf_op jit(solution)/shard_map/concatenate | solution.py:130
  29.3 16.4 %all-to-all-done.1.recv_ref = bf16[16,128,256]{2,1,0:T(8,128)(2,1)S(1)} async-done(((bf16[16,128,256]{2,1,0:T(8,128)(2,1)}), bf16[16,128,256]{2,1,0:T(8,128)(2,1)S(1)}, u32[]{:S(2)}, u32[]{:S(2)}) %all-to-all-start.1) | async-done | bytes 1048608 | tf_op jit(solution)/shard_map/all_to_all | solution.py:114
  45.6 0.0 copy-start
  45.6 1.0 %copy-done = bf16[16,128,256]{2,1,0:T(8,128)(2,1)} copy-done((bf16[16,128,256]{2,1,0:T(8,128)(2,1)}, bf16[16,128,256]{2,1,0:T(8,128)(2,1)S(1)}, u32[]{:S(2)}) %copy-start) | copy-done | bytes 1048600
  46.6 24.7 %shard_map.82 = bf16[384,1024]{1,0:T(8,128)(2,1)} custom-call(s32[16]{0:T(128)} %copy-done.6, f32[1,2048]{1,0:T(1,128)} %bitcast.17, s32[16,64]{1,0:T(8,128)} %pad_add_fusion.pos_ref, bf16[16,128,256]{2,1,0:T(8,128)(2,1)} %copy-done, bf16[16,64,256]{2,1,0:T(8,128)(2,1)} %pad_maximum_fusion.fresh_ref, bf16[384,256]{1,0:T(8,128)(2,1)} %own_ref.1, ...), custom_call_target="tpu_custom_call" | custom-call | flops 3892314112 | bytes 3354624 | tf_op jit(solution)/shard_map/pallas_call | solution.py:88
  (2 shorter events, 0.1 us)
Async XLA Ops:
  0.0 0.7 copy-start.3
  0.0 0.7 copy-start.4
  0.9 0.6 copy-start.6
  2.3 11.2 %all-to-all-start = ((s32[16,1,1]{2,1,0:T(1,128)}), s32[16,1,1]{2,1,0:T(1,128)S(1)}, u32[]{:S(2)}, u32[]{:S(2)}) async-start(s32[16,1,1]{2,1,0:T(1,128)} %copy.11), calls=%async_computation | async-start | bytes 16384 | tf_op jit(solution)/shard_map/all_to_all | solution.py:110
  15.3 5.4 %copy-start.1 = (bf16[1,16,32,512]{3,2,1,0:T(8,128)(2,1)S(1)}, bf16[1,16,32,512]{3,2,1,0:T(8,128)(2,1)}, u32[]{:S(2)}) copy-start(bf16[1,16,32,512]{3,2,1,0:T(8,128)(2,1)} %param.11) | copy-start | bytes 1572868
  15.4 30.3 %all-to-all-start.1 = ((bf16[16,128,256]{2,1,0:T(8,128)(2,1)}), bf16[16,128,256]{2,1,0:T(8,128)(2,1)S(1)}, u32[]{:S(2)}, u32[]{:S(2)}) async-start(bf16[16,128,256]{2,1,0:T(8,128)(2,1)} %select_select_fusion), calls=%async_computation.1 | async-start | bytes 2097152 | tf_op jit(solution)/shard_map/all_to_all | solution.py:114
  20.8 1.3 %copy-start.2 = (s32[1,16,64]{2,1,0:T(8,128)S(1)}, s32[1,16,64]{2,1,0:T(8,128)}, u32[]{:S(2)}) copy-start(s32[1,16,64]{2,1,0:T(8,128)} %param.15) | copy-start | bytes 12292
  20.8 7.6 %collective-permute-start = (bf16[16,32,256]{2,1,0:T(8,128)(2,1)S(1)}, bf16[16,32,256]{2,1,0:T(8,128)(2,1)S(1)}, u32[]{:S(2)}, u32[]{:S(2)}) collective-permute-start(bf16[16,32,256]{2,1,0:T(8,128)(2,1)S(1)} %get-tuple-element.8), channel_id=1, source_target_pairs={{0,16},{16,0},{1,17},{17,1},{2,18},{18,2},{3,19},{19,3},{4,20},{20... | collective-permute-start | bytes 786440 | tf_op jit(solution)/shard_map/ppermute | solution.py:127
  22.1 0.7 copy-start.5
  45.6 1.0 %copy-start = (bf16[16,128,256]{2,1,0:T(8,128)(2,1)}, bf16[16,128,256]{2,1,0:T(8,128)(2,1)S(1)}, u32[]{:S(2)}) copy-start(bf16[16,128,256]{2,1,0:T(8,128)(2,1)S(1)} %all-to-all-done.1.recv_ref) | copy-start | bytes 3145732

commit v2 on v1

--- a/solution.py
+++ b/solution.py
@@ -9,7 +9,6 @@
 
 HD = 128
 CL = 128
-TR = 128
 
 
 def lookup(table, indices):
@@ -17,7 +16,9 @@
     return jnp.sum(jnp.where(hits, table, 0), axis=-1)
 
 
-def attend_kernel(owner_ref, bias_ref, pos_ref, recv_ref, fresh_ref, own_ref, q_ref, out_ref, kb_ref, vb_ref):
+def attend_kernel(
+    owner_ref, bias_ref, pos_ref, recv_ref, fresh_ref, own_ref, q_ref, out_ref, kt_ref, vb_ref, ot_ref
+):
     nch, nrec = pos_ref.shape
     rows = q_ref.shape[0]
     scale = HD ** (-0.5)
@@ -32,31 +33,28 @@
             hit = jnp.max(pick.astype(jnp.float32), axis=1, keepdims=True) > 0
             block = jnp.where(hit, up.astype(jnp.bfloat16), lib)
             at = pl.ds(pl.multiple_of(j * CL, CL), CL)
-            kb_ref[at, :] = block[:, :HD]
+            kt_ref[:, at] = block[:, :HD].T
             vb_ref[at, :] = block[:, HD:]
             return carry
 
         lax.fori_loop(0, nch, build, 0)
+        ot_ref[...] = own_ref[:, :HD].T
 
-    dims = (((1,), (1,)), ((), ()))
-    for t in range(rows // TR):
-        qt = q_ref[t * TR:(t + 1) * TR, :]
-        s1 = lax.dot_general(qt, kb_ref[...], dims, preferred_element_type=jnp.float32)
-        s1 = s1 * scale + bias_ref[...]
-        kk = (t + 1) * TR
-        s2 = lax.dot_general(qt, own_ref[:kk, :HD], dims, preferred_element_type=jnp.float32) * scale
-        row = lax.broadcasted_iota(jnp.int32, (TR, kk), 0) + t * TR
-        col = lax.broadcasted_iota(jnp.int32, (TR, kk), 1)
-        s2 = jnp.where(col <= row, s2, -jnp.inf)
-        top = jnp.maximum(jnp.max(s1, axis=1, keepdims=True), jnp.max(s2, axis=1, keepdims=True))
-        e1 = jnp.exp(s1 - top)
-        e2 = jnp.exp(s2 - top)
-        inv = 1.0 / (jnp.sum(e1, axis=1, keepdims=True) + jnp.sum(e2, axis=1, keepdims=True))
-        w1 = (e1 * inv).astype(jnp.bfloat16)
-        w2 = (e2 * inv).astype(jnp.bfloat16)
-        mixed = jnp.dot(w1, vb_ref[...], preferred_element_type=jnp.float32)
-        mixed = mixed + jnp.dot(w2, own_ref[:kk, HD:], preferred_element_type=jnp.float32)
-        out_ref[t * TR:(t + 1) * TR, :] = mixed.astype(out_ref.dtype)
+    q = q_ref[...]
+    s1 = jnp.dot(q, kt_ref[...], preferred_element_type=jnp.float32) * scale + bias_ref[...]
+    s2 = jnp.dot(q, ot_ref[...], preferred_element_type=jnp.float32) * scale
+    row = lax.broadcasted_iota(jnp.int32, (rows, rows), 0)
+    col = lax.broadcasted_iota(jnp.int32, (rows, rows), 1)
+    s2 = jnp.where(col <= row, s2, -jnp.inf)
+    top = jnp.maximum(jnp.max(s1, axis=1, keepdims=True), jnp.max(s2, axis=1, keepdims=True))
+    e1 = jnp.exp(s1 - top)
+    e2 = jnp.exp(s2 - top)
+    inv = 1.0 / (jnp.sum(e1, axis=1, keepdims=True) + jnp.sum(e2, axis=1, keepdims=True))
+    w1 = (e1 * inv).astype(jnp.bfloat16)
+    w2 = (e2 * inv).astype(jnp.bfloat16)
+    mixed = jnp.dot(w1, vb_ref[...], preferred_element_type=jnp.float32)
+    mixed = mixed + jnp.dot(w2, own_ref[:, HD:], preferred_element_type=jnp.float32)
+    out_ref[...] = mixed.astype(out_ref.dtype)
 
 
 def attend(owner, bias, pos, recv, fresh, own_kv, queries):
@@ -83,7 +81,11 @@
             pl.BlockSpec((rows, HD), lambda g, o: (0, g)),
         ],
         out_specs=pl.BlockSpec((rows, HD), lambda g, o: (0, g)),
-        scratch_shapes=[pltpu.VMEM((span, HD), jnp.bfloat16), pltpu.VMEM((span, HD), jnp.bfloat16)],
+        scratch_shapes=[
+            pltpu.VMEM((HD, span), jnp.bfloat16),
+            pltpu.VMEM((span, HD), jnp.bfloat16),
+            pltpu.VMEM((HD, rows), jnp.bfloat16),
+        ],
     )
     return pl.pallas_call(
         attend_kernel,

time: 71.7 us -> 74.4 us (1.038)
  the two profiles are of different devices: /device:TPU:9 before, /device:TPU:0 now
where the time goes in v2:
time: 74.4 us; the launch traced here: 73 us
  Pallas kernels  27.5 us (37%)
  waiting for transfers between devices  23.7 us (32%)
  starting transfers between devices  12.7 us (17%)
  local copies, waits for them, and re-layouts  4.54 us (6%)
  other arithmetic  4.51 us (6%)
    pallas_call x1, Pallas kernels, attend(): pl.pallas_call(attend_kernel, grid_spec=grid_spec, out_shape=jax.ShapeDty...  27.5 us
    all_to_all x1, waiting for transfers between devices, per_device(): recv = lax.all_to_all(send, 'seq', 0, 0, tiled=True)  13.4 us
    all_to_all x1, starting transfers between devices, per_device(): lax.all_to_all(request.reshape(n_seq, 1), 'seq', 0, 0, tiled=True)  7.39 us
    all_to_all x1, waiting for transfers between devices, per_device(): lax.all_to_all(request.reshape(n_seq, 1), 'seq', 0, 0, tiled=True)  5.41 us
    ppermute x1, waiting for transfers between devices, per_device(): pieces.append(lax.ppermute(piece, 'kvh', pairs))  4.82 us
    all_to_all x1, starting transfers between devices, per_device(): recv = lax.all_to_all(send, 'seq', 0, 0, tiled=True)  3.78 us
    unnamed x14, local copies, waits for them, and re-layouts  2.82 us
    ppermute x1, starting transfers between devices, per_device(): pieces.append(lax.ppermute(piece, 'kvh', pairs))  1.56 us
  transfers between devices with their start and end apart: 3, of which 3 were waited for; matrix products, arithmetic and copies ran while one was open for 5% of the time, Pallas kernels for 0%

profile of v2, /device:TPU:0, one launch (start us, length us, event | category | flops | bytes accessed | tf_op | source)
XLA Modules:
  0.0 73.0 jit_solution(11474579547055141339)
XLA Ops:
  0.0 0.0 copy-start.3
  0.0 0.0 copy-start.4
  0.0 0.7 copy-done.3
  0.7 0.0 copy-done.4
  0.7 0.2 select_reduce_fusion.2
  0.9 0.0 copy-start.6
  0.9 0.6 copy-done.6
  1.5 0.1 select_reduce_fusion
  1.6 0.7 copy.11
  2.3 7.4 %all-to-all-start = ((s32[16,1,1]{2,1,0:T(1,128)}), s32[16,1,1]{2,1,0:T(1,128)S(1)}, u32[]{:S(2)}, u32[]{:S(2)}) async-start(s32[16,1,1]{2,1,0:T(1,128)} %copy.11), calls=%async_computation | async-start | bytes 16384 | tf_op jit(solution)/shard_map/all_to_all | solution.py:112
  9.7 0.9 %slice_bitcast_fusion.2 = (bf16[128,256]{1,0:T(8,128)(2,1)S(1)}, bf16[128,256]{1,0:T(8,128)(2,1)S(1)}, bf16[128,256]{1,0:T(8,128)(2,1)S(1)}) fusion(bf16[3,128,256]{2,1,0:T(8,128)(2,1)} %param.10), kind=kLoop, calls=%fused_computation.6 | loop fusion | bytes 393216 | tf_op jit(solution)/shard_map/squeeze | solution.py:115
  10.6 5.4 %all-to-all-done = s32[16,1,1]{2,1,0:T(1,128)S(1)} async-done(((s32[16,1,1]{2,1,0:T(1,128)}), s32[16,1,1]{2,1,0:T(1,128)S(1)}, u32[]{:S(2)}, u32[]{:S(2)}) %all-to-all-start) | async-done | bytes 96 | tf_op jit(solution)/shard_map/all_to_all | solution.py:112
  16.0 0.7 compare_reduce_fusion.1
  16.7 1.2 %select_select_fusion = bf16[16,128,256]{2,1,0:T(8,128)(2,1)} fusion(pred[16]{0:T(512)(128)(4,1)S(1)} %get-tuple-element.6, pred[16]{0:T(512)(128)(4,1)S(1)} %get-tuple-element.5, bf16[128,256]{1,0:T(8,128)(2,1)S(1)} %get-tuple-element.10, bf16[128,256]{1,0:T(8,128)(2,1)S(1)} %get-tuple-element.11, bf16[128,256]{1,0:T(8,128)(2,1)S(1)} %get-tuple-element.9), kind=kLoop, calls=%fused_computation | loop fusion | flops 1048576 | bytes 1245216 | tf_op jit(solution)/shard_map/jit(_where)/select_n | solution.py:115
  17.8 0.0 copy-start.1
  17.8 3.8 %all-to-all-start.1 = ((bf16[16,128,256]{2,1,0:T(8,128)(2,1)}), bf16[16,128,256]{2,1,0:T(8,128)(2,1)S(1)}, u32[]{:S(2)}, u32[]{:S(2)}) async-start(bf16[16,128,256]{2,1,0:T(8,128)(2,1)} %select_select_fusion), calls=%async_computation.1 | async-start | bytes 2097152 | tf_op jit(solution)/shard_map/all_to_all | solution.py:116
  21.7 0.0 copy-done.1
  21.7 0.0 copy-start.2
  21.7 1.6 %collective-permute-start = (bf16[16,32,256]{2,1,0:T(8,128)(2,1)S(1)}, bf16[16,32,256]{2,1,0:T(8,128)(2,1)S(1)}, u32[]{:S(2)}, u32[]{:S(2)}) collective-permute-start(bf16[16,32,256]{2,1,0:T(8,128)(2,1)S(1)} %get-tuple-element.8), channel_id=1, source_target_pairs={{0,16},{16,0},{1,17},{17,1},{2,18},{18,2},{3,19},{19,3},{4,20},{20... | collective-permute-start | bytes 786440 | tf_op jit(solution)/shard_map/ppermute | solution.py:129
  23.3 0.0 copy-done.2
  23.3 0.0 copy-start.5
  23.3 0.1 dynamic-slice_bitcast_fusion.3
  23.4 0.6 copy-done.5
  23.9 0.2 select_reduce_fusion.1
  24.1 0.7 pad_add_fusion.pos_ref
  24.8 0.7 fusion
  25.5 4.8 %collective-permute-done = bf16[16,32,256]{2,1,0:T(8,128)(2,1)S(1)} collective-permute-done((bf16[16,32,256]{2,1,0:T(8,128)(2,1)S(1)}, bf16[16,32,256]{2,1,0:T(8,128)(2,1)S(1)}, u32[]{:S(2)}, u32[]{:S(2)}) %collective-permute-start) | collective-permute-done | bytes 262176 | tf_op jit(solution)/shard_map/ppermute | solution.py:129
  30.3 0.8 %pad_maximum_fusion.fresh_ref = bf16[16,64,256]{2,1,0:T(8,128)(2,1)} fusion(bf16[16,32,256]{2,1,0:T(8,128)(2,1)S(1)} %collective-permute-done, bf16[16,32,256]{2,1,0:T(8,128)(2,1)S(1)} %get-tuple-element.7), kind=kLoop, calls=%fused_computation.1 | loop fusion | flops 1048576 | bytes 1048576 | tf_op jit(solution)/shard_map/concatenate | solution.py:132
  31.1 13.4 %all-to-all-done.1.recv_ref = bf16[16,128,256]{2,1,0:T(8,128)(2,1)S(1)} async-done(((bf16[16,128,256]{2,1,0:T(8,128)(2,1)}), bf16[16,128,256]{2,1,0:T(8,128)(2,1)S(1)}, u32[]{:S(2)}, u32[]{:S(2)}) %all-to-all-start.1) | async-done | bytes 1048608 | tf_op jit(solution)/shard_map/all_to_all | solution.py:116
  44.5 0.0 copy-start
  44.5 1.0 %copy-done = bf16[16,128,256]{2,1,0:T(8,128)(2,1)} copy-done((bf16[16,128,256]{2,1,0:T(8,128)(2,1)}, bf16[16,128,256]{2,1,0:T(8,128)(2,1)S(1)}, u32[]{:S(2)}) %copy-start) | copy-done | bytes 1048600
  45.5 27.5 %shard_map.82 = bf16[384,1024]{1,0:T(8,128)(2,1)} custom-call(s32[16]{0:T(128)} %copy-done.6, f32[1,2048]{1,0:T(1,128)} %bitcast.17, s32[16,64]{1,0:T(8,128)} %pad_add_fusion.pos_ref, bf16[16,128,256]{2,1,0:T(8,128)(2,1)} %copy-done, bf16[16,64,256]{2,1,0:T(8,128)(2,1)} %pad_maximum_fusion.fresh_ref, bf16[384,256]{1,0:T(8,128)(2,1)} %own_ref.1, ...), custom_call_target="tpu_custom_call" | custom-call | flops 3892314112 | bytes 3354624 | tf_op jit(solution)/shard_map/pallas_call | solution.py:90
  (2 shorter events, 0.1 us)
Async XLA Ops:
  0.0 0.7 copy-start.3
  0.0 0.7 copy-start.4
  0.9 0.6 copy-start.6
  2.3 13.7 %all-to-all-start = ((s32[16,1,1]{2,1,0:T(1,128)}), s32[16,1,1]{2,1,0:T(1,128)S(1)}, u32[]{:S(2)}, u32[]{:S(2)}) async-start(s32[16,1,1]{2,1,0:T(1,128)} %copy.11), calls=%async_computation | async-start | bytes 16384 | tf_op jit(solution)/shard_map/all_to_all | solution.py:112
  17.8 3.8 %copy-start.1 = (bf16[1,16,32,512]{3,2,1,0:T(8,128)(2,1)S(1)}, bf16[1,16,32,512]{3,2,1,0:T(8,128)(2,1)}, u32[]{:S(2)}) copy-start(bf16[1,16,32,512]{3,2,1,0:T(8,128)(2,1)} %param.11) | copy-start | bytes 1572868
  17.8 26.7 %all-to-all-start.1 = ((bf16[16,128,256]{2,1,0:T(8,128)(2,1)}), bf16[16,128,256]{2,1,0:T(8,128)(2,1)S(1)}, u32[]{:S(2)}, u32[]{:S(2)}) async-start(bf16[16,128,256]{2,1,0:T(8,128)(2,1)} %select_select_fusion), calls=%async_computation.1 | async-start | bytes 2097152 | tf_op jit(solution)/shard_map/all_to_all | solution.py:116
  21.7 1.6 %copy-start.2 = (s32[1,16,64]{2,1,0:T(8,128)S(1)}, s32[1,16,64]{2,1,0:T(8,128)}, u32[]{:S(2)}) copy-start(s32[1,16,64]{2,1,0:T(8,128)} %param.15) | copy-start | bytes 12292
  21.7 8.5 %collective-permute-start = (bf16[16,32,256]{2,1,0:T(8,128)(2,1)S(1)}, bf16[16,32,256]{2,1,0:T(8,128)(2,1)S(1)}, u32[]{:S(2)}, u32[]{:S(2)}) collective-permute-start(bf16[16,32,256]{2,1,0:T(8,128)(2,1)S(1)} %get-tuple-element.8), channel_id=1, source_target_pairs={{0,16},{16,0},{1,17},{17,1},{2,18},{18,2},{3,19},{19,3},{4,20},{20... | collective-permute-start | bytes 786440 | tf_op jit(solution)/shard_map/ppermute | solution.py:129
  23.3 0.7 copy-start.5
  44.5 1.0 %copy-start = (bf16[16,128,256]{2,1,0:T(8,128)(2,1)}, bf16[16,128,256]{2,1,0:T(8,128)(2,1)S(1)}, u32[]{:S(2)}) copy-start(bf16[16,128,256]{2,1,0:T(8,128)(2,1)S(1)} %all-to-all-done.1.recv_ref) | copy-start | bytes 3145732

commit v3 on v2

--- a/solution.py
+++ b/solution.py
@@ -21,7 +21,7 @@
 ):
     nch, nrec = pos_ref.shape
     rows = q_ref.shape[0]
-    scale = HD ** (-0.5)
+    rate = HD ** (-0.5) * 1.4426950408889634
 
     @pl.when(pl.program_id(0) == 0)
     def _():
@@ -41,20 +41,18 @@
         ot_ref[...] = own_ref[:, :HD].T
 
     q = q_ref[...]
-    s1 = jnp.dot(q, kt_ref[...], preferred_element_type=jnp.float32) * scale + bias_ref[...]
-    s2 = jnp.dot(q, ot_ref[...], preferred_element_type=jnp.float32) * scale
+    s1 = jnp.dot(q, kt_ref[...], preferred_element_type=jnp.float32) + bias_ref[...]
+    s2 = jnp.dot(q, ot_ref[...], preferred_element_type=jnp.float32)
     row = lax.broadcasted_iota(jnp.int32, (rows, rows), 0)
     col = lax.broadcasted_iota(jnp.int32, (rows, rows), 1)
     s2 = jnp.where(col <= row, s2, -jnp.inf)
     top = jnp.maximum(jnp.max(s1, axis=1, keepdims=True), jnp.max(s2, axis=1, keepdims=True))
-    e1 = jnp.exp(s1 - top)
-    e2 = jnp.exp(s2 - top)
-    inv = 1.0 / (jnp.sum(e1, axis=1, keepdims=True) + jnp.sum(e2, axis=1, keepdims=True))
-    w1 = (e1 * inv).astype(jnp.bfloat16)
-    w2 = (e2 * inv).astype(jnp.bfloat16)
-    mixed = jnp.dot(w1, vb_ref[...], preferred_element_type=jnp.float32)
-    mixed = mixed + jnp.dot(w2, own_ref[:, HD:], preferred_element_type=jnp.float32)
-    out_ref[...] = mixed.astype(out_ref.dtype)
+    e1 = jnp.exp2((s1 - top) * rate)
+    e2 = jnp.exp2((s2 - top) * rate)
+    total = jnp.sum(e1, axis=1, keepdims=True) + jnp.sum(e2, axis=1, keepdims=True)
+    mixed = jnp.dot(e1.astype(jnp.bfloat16), vb_ref[...], preferred_element_type=jnp.float32)
+    mixed = mixed + jnp.dot(e2.astype(jnp.bfloat16), own_ref[:, HD:], preferred_element_type=jnp.float32)
+    out_ref[...] = (mixed * (1.0 / total)).astype(out_ref.dtype)
 
 
 def attend(owner, bias, pos, recv, fresh, own_kv, queries):

time: 74.4 us -> 73.3 us (0.985)
  Pallas kernels: 27.5 us -> 26.3 us
    pallas_call x1, Pallas kernels: 27.5 us -> 26.3 us  [attend(): pl.pallas_call(attend_kernel, grid_spec=grid_spec, out_shape=jax.ShapeDty...]
where the time goes in v3:
time: 73.3 us; the launch traced here: 71.8 us
  Pallas kernels  26.3 us (36%)
  waiting for transfers between devices  23.7 us (32%)
  starting transfers between devices  12.7 us (17%)
  local copies, waits for them, and re-layouts  4.54 us (6%)
  other arithmetic  4.51 us (6%)
    pallas_call x1, Pallas kernels, attend(): pl.pallas_call(attend_kernel, grid_spec=grid_spec, out_shape=jax.ShapeDty...  26.3 us
    all_to_all x1, waiting for transfers between devices, per_device(): recv = lax.all_to_all(send, 'seq', 0, 0, tiled=True)  13.4 us
    all_to_all x1, starting transfers between devices, per_device(): lax.all_to_all(request.reshape(n_seq, 1), 'seq', 0, 0, tiled=True)  7.39 us
    all_to_all x1, waiting for transfers between devices, per_device(): lax.all_to_all(request.reshape(n_seq, 1), 'seq', 0, 0, tiled=True)  5.41 us
    ppermute x1, waiting for transfers between devices, per_device(): pieces.append(lax.ppermute(piece, 'kvh', pairs))  4.82 us
    all_to_all x1, starting transfers between devices, per_device(): recv = lax.all_to_all(send, 'seq', 0, 0, tiled=True)  3.78 us
    unnamed x14, local copies, waits for them, and re-layouts  2.82 us
    ppermute x1, starting transfers between devices, per_device(): pieces.append(lax.ppermute(piece, 'kvh', pairs))  1.56 us
  transfers between devices with their start and end apart: 3, of which 3 were waited for; matrix products, arithmetic and copies ran while one was open for 5% of the time, Pallas kernels for 0%

profile of v3, /device:TPU:0, one launch (start us, length us, event | category | flops | bytes accessed | tf_op | source)
XLA Modules:
  0.0 71.8 jit_solution(3958427989361732073)
XLA Ops:
  0.0 0.0 copy-start.3
  0.0 0.0 copy-start.4
  0.0 0.7 copy-done.3
  0.7 0.0 copy-done.4
  0.7 0.2 select_reduce_fusion.2
  0.9 0.0 copy-start.6
  0.9 0.6 copy-done.6
  1.5 0.1 select_reduce_fusion
  1.6 0.7 copy.11
  2.3 7.4 %all-to-all-start = ((s32[16,1,1]{2,1,0:T(1,128)}), s32[16,1,1]{2,1,0:T(1,128)S(1)}, u32[]{:S(2)}, u32[]{:S(2)}) async-start(s32[16,1,1]{2,1,0:T(1,128)} %copy.11), calls=%async_computation | async-start | bytes 16384 | tf_op jit(solution)/shard_map/all_to_all | solution.py:110
  9.7 0.9 %slice_bitcast_fusion.2 = (bf16[128,256]{1,0:T(8,128)(2,1)S(1)}, bf16[128,256]{1,0:T(8,128)(2,1)S(1)}, bf16[128,256]{1,0:T(8,128)(2,1)S(1)}) fusion(bf16[3,128,256]{2,1,0:T(8,128)(2,1)} %param.10), kind=kLoop, calls=%fused_computation.6 | loop fusion | bytes 393216 | tf_op jit(solution)/shard_map/squeeze | solution.py:113
  10.6 5.4 %all-to-all-done = s32[16,1,1]{2,1,0:T(1,128)S(1)} async-done(((s32[16,1,1]{2,1,0:T(1,128)}), s32[16,1,1]{2,1,0:T(1,128)S(1)}, u32[]{:S(2)}, u32[]{:S(2)}) %all-to-all-start) | async-done | bytes 96 | tf_op jit(solution)/shard_map/all_to_all | solution.py:110
  16.0 0.7 compare_reduce_fusion.1
  16.7 1.2 %select_select_fusion = bf16[16,128,256]{2,1,0:T(8,128)(2,1)} fusion(pred[16]{0:T(512)(128)(4,1)S(1)} %get-tuple-element.6, pred[16]{0:T(512)(128)(4,1)S(1)} %get-tuple-element.5, bf16[128,256]{1,0:T(8,128)(2,1)S(1)} %get-tuple-element.10, bf16[128,256]{1,0:T(8,128)(2,1)S(1)} %get-tuple-element.11, bf16[128,256]{1,0:T(8,128)(2,1)S(1)} %get-tuple-element.9), kind=kLoop, calls=%fused_computation | loop fusion | flops 1048576 | bytes 1245216 | tf_op jit(solution)/shard_map/jit(_where)/select_n | solution.py:113
  17.8 0.0 copy-start.1
  17.8 3.8 %all-to-all-start.1 = ((bf16[16,128,256]{2,1,0:T(8,128)(2,1)}), bf16[16,128,256]{2,1,0:T(8,128)(2,1)S(1)}, u32[]{:S(2)}, u32[]{:S(2)}) async-start(bf16[16,128,256]{2,1,0:T(8,128)(2,1)} %select_select_fusion), calls=%async_computation.1 | async-start | bytes 2097152 | tf_op jit(solution)/shard_map/all_to_all | solution.py:114
  21.7 0.0 copy-done.1
  21.7 0.0 copy-start.2
  21.7 1.6 %collective-permute-start = (bf16[16,32,256]{2,1,0:T(8,128)(2,1)S(1)}, bf16[16,32,256]{2,1,0:T(8,128)(2,1)S(1)}, u32[]{:S(2)}, u32[]{:S(2)}) collective-permute-start(bf16[16,32,256]{2,1,0:T(8,128)(2,1)S(1)} %get-tuple-element.8), channel_id=1, source_target_pairs={{0,16},{16,0},{1,17},{17,1},{2,18},{18,2},{3,19},{19,3},{4,20},{20... | collective-permute-start | bytes 786440 | tf_op jit(solution)/shard_map/ppermute | solution.py:127
  23.3 0.0 copy-done.2
  23.3 0.0 copy-start.5
  23.3 0.1 dynamic-slice_bitcast_fusion.3
  23.4 0.6 copy-done.5
  23.9 0.2 select_reduce_fusion.1
  24.1 0.7 pad_add_fusion.pos_ref
  24.8 0.7 fusion
  25.5 4.8 %collective-permute-done = bf16[16,32,256]{2,1,0:T(8,128)(2,1)S(1)} collective-permute-done((bf16[16,32,256]{2,1,0:T(8,128)(2,1)S(1)}, bf16[16,32,256]{2,1,0:T(8,128)(2,1)S(1)}, u32[]{:S(2)}, u32[]{:S(2)}) %collective-permute-start) | collective-permute-done | bytes 262176 | tf_op jit(solution)/shard_map/ppermute | solution.py:127
  30.3 0.8 %pad_maximum_fusion.fresh_ref = bf16[16,64,256]{2,1,0:T(8,128)(2,1)} fusion(bf16[16,32,256]{2,1,0:T(8,128)(2,1)S(1)} %collective-permute-done, bf16[16,32,256]{2,1,0:T(8,128)(2,1)S(1)} %get-tuple-element.7), kind=kLoop, calls=%fused_computation.1 | loop fusion | flops 1048576 | bytes 1048576 | tf_op jit(solution)/shard_map/concatenate | solution.py:130
  31.1 13.4 %all-to-all-done.1.recv_ref = bf16[16,128,256]{2,1,0:T(8,128)(2,1)S(1)} async-done(((bf16[16,128,256]{2,1,0:T(8,128)(2,1)}), bf16[16,128,256]{2,1,0:T(8,128)(2,1)S(1)}, u32[]{:S(2)}, u32[]{:S(2)}) %all-to-all-start.1) | async-done | bytes 1048608 | tf_op jit(solution)/shard_map/all_to_all | solution.py:114
  44.5 0.0 copy-start
  44.5 1.0 %copy-done = bf16[16,128,256]{2,1,0:T(8,128)(2,1)} copy-done((bf16[16,128,256]{2,1,0:T(8,128)(2,1)}, bf16[16,128,256]{2,1,0:T(8,128)(2,1)S(1)}, u32[]{:S(2)}) %copy-start) | copy-done | bytes 1048600
  45.5 26.3 %shard_map.82 = bf16[384,1024]{1,0:T(8,128)(2,1)} custom-call(s32[16]{0:T(128)} %copy-done.6, f32[1,2048]{1,0:T(1,128)} %bitcast.17, s32[16,64]{1,0:T(8,128)} %pad_add_fusion.pos_ref, bf16[16,128,256]{2,1,0:T(8,128)(2,1)} %copy-done, bf16[16,64,256]{2,1,0:T(8,128)(2,1)} %pad_maximum_fusion.fresh_ref, bf16[384,256]{1,0:T(8,128)(2,1)} %own_ref.1, ...), custom_call_target="tpu_custom_call" | custom-call | flops 3892314112 | bytes 3354624 | tf_op jit(solution)/shard_map/pallas_call | solution.py:88
  (2 shorter events, 0.1 us)
Async XLA Ops:
  0.0 0.7 copy-start.3
  0.0 0.7 copy-start.4
  0.9 0.6 copy-start.6
  2.3 13.7 %all-to-all-start = ((s32[16,1,1]{2,1,0:T(1,128)}), s32[16,1,1]{2,1,0:T(1,128)S(1)}, u32[]{:S(2)}, u32[]{:S(2)}) async-start(s32[16,1,1]{2,1,0:T(1,128)} %copy.11), calls=%async_computation | async-start | bytes 16384 | tf_op jit(solution)/shard_map/all_to_all | solution.py:110
  17.8 3.8 %copy-start.1 = (bf16[1,16,32,512]{3,2,1,0:T(8,128)(2,1)S(1)}, bf16[1,16,32,512]{3,2,1,0:T(8,128)(2,1)}, u32[]{:S(2)}) copy-start(bf16[1,16,32,512]{3,2,1,0:T(8,128)(2,1)} %param.11) | copy-start | bytes 1572868
  17.8 26.7 %all-to-all-start.1 = ((bf16[16,128,256]{2,1,0:T(8,128)(2,1)}), bf16[16,128,256]{2,1,0:T(8,128)(2,1)S(1)}, u32[]{:S(2)}, u32[]{:S(2)}) async-start(bf16[16,128,256]{2,1,0:T(8,128)(2,1)} %select_select_fusion), calls=%async_computation.1 | async-start | bytes 2097152 | tf_op jit(solution)/shard_map/all_to_all | solution.py:114
  21.7 1.6 %copy-start.2 = (s32[1,16,64]{2,1,0:T(8,128)S(1)}, s32[1,16,64]{2,1,0:T(8,128)}, u32[]{:S(2)}) copy-start(s32[1,16,64]{2,1,0:T(8,128)} %param.15) | copy-start | bytes 12292
  21.7 8.5 %collective-permute-start = (bf16[16,32,256]{2,1,0:T(8,128)(2,1)S(1)}, bf16[16,32,256]{2,1,0:T(8,128)(2,1)S(1)}, u32[]{:S(2)}, u32[]{:S(2)}) collective-permute-start(bf16[16,32,256]{2,1,0:T(8,128)(2,1)S(1)} %get-tuple-element.8), channel_id=1, source_target_pairs={{0,16},{16,0},{1,17},{17,1},{2,18},{18,2},{3,19},{19,3},{4,20},{20... | collective-permute-start | bytes 786440 | tf_op jit(solution)/shard_map/ppermute | solution.py:127
  23.3 0.7 copy-start.5
  44.5 1.0 %copy-start = (bf16[16,128,256]{2,1,0:T(8,128)(2,1)}, bf16[16,128,256]{2,1,0:T(8,128)(2,1)S(1)}, u32[]{:S(2)}) copy-start(bf16[16,128,256]{2,1,0:T(8,128)(2,1)S(1)} %all-to-all-done.1.recv_ref) | copy-start | bytes 3145732

commit v4 on v3

--- a/solution.py
+++ b/solution.py
@@ -9,6 +9,8 @@
 
 HD = 128
 CL = 128
+TR = 128
+PAIR = 4
 
 
 def lookup(table, indices):
@@ -40,24 +42,30 @@
         lax.fori_loop(0, nch, build, 0)
         ot_ref[...] = own_ref[:, :HD].T
 
-    q = q_ref[...]
-    s1 = jnp.dot(q, kt_ref[...], preferred_element_type=jnp.float32) + bias_ref[...]
-    s2 = jnp.dot(q, ot_ref[...], preferred_element_type=jnp.float32)
-    row = lax.broadcasted_iota(jnp.int32, (rows, rows), 0)
-    col = lax.broadcasted_iota(jnp.int32, (rows, rows), 1)
-    s2 = jnp.where(col <= row, s2, -jnp.inf)
-    top = jnp.maximum(jnp.max(s1, axis=1, keepdims=True), jnp.max(s2, axis=1, keepdims=True))
-    e1 = jnp.exp2((s1 - top) * rate)
-    e2 = jnp.exp2((s2 - top) * rate)
-    total = jnp.sum(e1, axis=1, keepdims=True) + jnp.sum(e2, axis=1, keepdims=True)
-    mixed = jnp.dot(e1.astype(jnp.bfloat16), vb_ref[...], preferred_element_type=jnp.float32)
-    mixed = mixed + jnp.dot(e2.astype(jnp.bfloat16), own_ref[:, HD:], preferred_element_type=jnp.float32)
-    out_ref[...] = (mixed * (1.0 / total)).astype(out_ref.dtype)
+    for g in range(q_ref.shape[1] // HD):
+        for t in range(rows // TR):
+            qt = q_ref[t * TR:(t + 1) * TR, g * HD:(g + 1) * HD]
+            s1 = jnp.dot(qt, kt_ref[...], preferred_element_type=jnp.float32) + bias_ref[...]
+            kk = (t + 1) * TR
+            s2 = jnp.dot(qt, ot_ref[:, :kk], preferred_element_type=jnp.float32)
+            row = lax.broadcasted_iota(jnp.int32, (TR, kk), 0) + t * TR
+            col = lax.broadcasted_iota(jnp.int32, (TR, kk), 1)
+            s2 = jnp.where(col <= row, s2, -jnp.inf)
+            top = jnp.maximum(jnp.max(s1, axis=1, keepdims=True), jnp.max(s2, axis=1, keepdims=True))
+            e1 = jnp.exp2((s1 - top) * rate)
+            e2 = jnp.exp2((s2 - top) * rate)
+            inv = 1.0 / (jnp.sum(e1, axis=1, keepdims=True) + jnp.sum(e2, axis=1, keepdims=True))
+            w1 = (e1 * inv).astype(jnp.bfloat16)
+            w2 = (e2 * inv).astype(jnp.bfloat16)
+            mixed = jnp.dot(w1, vb_ref[...], preferred_element_type=jnp.float32)
+            mixed = mixed + jnp.dot(w2, own_ref[:kk, HD:], preferred_element_type=jnp.float32)
+            out_ref[t * TR:(t + 1) * TR, g * HD:(g + 1) * HD] = mixed.astype(out_ref.dtype)
 
 
 def attend(owner, bias, pos, recv, fresh, own_kv, queries):
     rows, width = queries.shape
     heads = width // HD
+    step = PAIR if heads % PAIR == 0 else 1
     nch, nrec = pos.shape
     span = nch * CL
     keys = span + rows
@@ -69,16 +77,16 @@
 
     grid_spec = pltpu.PrefetchScalarGridSpec(
         num_scalar_prefetch=1,
-        grid=(heads,),
+        grid=(heads // step,),
         in_specs=[
             full(bias.shape),
             full(pos.shape),
             full(recv.shape),
             full(fresh.shape),
             full(own_kv.shape),
-            pl.BlockSpec((rows, HD), lambda g, o: (0, g)),
+            pl.BlockSpec((rows, step * HD), lambda g, o: (0, g)),
         ],
-        out_specs=pl.BlockSpec((rows, HD), lambda g, o: (0, g)),
+        out_specs=pl.BlockSpec((rows, step * HD), lambda g, o: (0, g)),
         scratch_shapes=[
             pltpu.VMEM((HD, span), jnp.bfloat16),
             pltpu.VMEM((span, HD), jnp.bfloat16),

time: 73.3 us -> 71.7 us (0.978)
  the two profiles are of different devices: /device:TPU:0 before, /device:TPU:9 now
where the time goes in v4:
time: 71.7 us; the launch traced here: 71.3 us
  Pallas kernels  24.7 us (34%)
  waiting for transfers between devices  24.2 us (34%)
  starting transfers between devices  13.3 us (19%)
  local copies, waits for them, and re-layouts  4.54 us (6%)
  other arithmetic  4.51 us (6%)
    pallas_call x1, Pallas kernels, attend(): pl.pallas_call(attend_kernel, grid_spec=grid_spec, out_shape=jax.ShapeDty...  24.7 us
    all_to_all x1, waiting for transfers between devices, per_device(): recv = lax.all_to_all(send, 'seq', 0, 0, tiled=True)  16.4 us
    all_to_all x1, starting transfers between devices, per_device(): lax.all_to_all(request.reshape(n_seq, 1), 'seq', 0, 0, tiled=True)  6.61 us
    all_to_all x1, starting transfers between devices, per_device(): recv = lax.all_to_all(send, 'seq', 0, 0, tiled=True)  5.41 us
    ppermute x1, waiting for transfers between devices, per_device(): pieces.append(lax.ppermute(piece, 'kvh', pairs))  4.15 us
    all_to_all x1, waiting for transfers between devices, per_device(): lax.all_to_all(request.reshape(n_seq, 1), 'seq', 0, 0, tiled=True)  3.7 us
    unnamed x14, local copies, waits for them, and re-layouts  2.82 us
  transfers between devices with their start and end apart: 3, of which 3 were waited for; matrix products, arithmetic and copies ran while one was open for 5% of the time, Pallas kernels for 0%

profile of v4, /device:TPU:9, one launch (start us, length us, event | category | flops | bytes accessed | tf_op | source)
XLA Modules:
  0.0 71.3 jit_solution(2655900101984167141)
XLA Ops:
  0.0 0.0 copy-start.3
  0.0 0.0 copy-start.4
  0.0 0.7 copy-done.3
  0.7 0.0 copy-done.4
  0.7 0.2 select_reduce_fusion.2
  0.9 0.0 copy-start.6
  0.9 0.6 copy-done.6
  1.5 0.1 select_reduce_fusion
  1.6 0.7 copy.11
  2.3 6.6 %all-to-all-start = ((s32[16,1,1]{2,1,0:T(1,128)}), s32[16,1,1]{2,1,0:T(1,128)S(1)}, u32[]{:S(2)}, u32[]{:S(2)}) async-start(s32[16,1,1]{2,1,0:T(1,128)} %copy.11), calls=%async_computation | async-start | bytes 16384 | tf_op jit(solution)/shard_map/all_to_all | solution.py:118
  8.9 0.9 %slice_bitcast_fusion.2 = (bf16[128,256]{1,0:T(8,128)(2,1)S(1)}, bf16[128,256]{1,0:T(8,128)(2,1)S(1)}, bf16[128,256]{1,0:T(8,128)(2,1)S(1)}) fusion(bf16[3,128,256]{2,1,0:T(8,128)(2,1)} %param.10), kind=kLoop, calls=%fused_computation.6 | loop fusion | bytes 393216 | tf_op jit(solution)/shard_map/squeeze | solution.py:121
  9.8 3.7 %all-to-all-done = s32[16,1,1]{2,1,0:T(1,128)S(1)} async-done(((s32[16,1,1]{2,1,0:T(1,128)}), s32[16,1,1]{2,1,0:T(1,128)S(1)}, u32[]{:S(2)}, u32[]{:S(2)}) %all-to-all-start) | async-done | bytes 96 | tf_op jit(solution)/shard_map/all_to_all | solution.py:118
  13.5 0.7 compare_reduce_fusion.1
  14.2 1.2 %select_select_fusion = bf16[16,128,256]{2,1,0:T(8,128)(2,1)} fusion(pred[16]{0:T(512)(128)(4,1)S(1)} %get-tuple-element.6, pred[16]{0:T(512)(128)(4,1)S(1)} %get-tuple-element.5, bf16[128,256]{1,0:T(8,128)(2,1)S(1)} %get-tuple-element.10, bf16[128,256]{1,0:T(8,128)(2,1)S(1)} %get-tuple-element.11, bf16[128,256]{1,0:T(8,128)(2,1)S(1)} %get-tuple-element.9), kind=kLoop, calls=%fused_computation | loop fusion | flops 1048576 | bytes 1245216 | tf_op jit(solution)/shard_map/jit(_where)/select_n | solution.py:121
  15.3 0.0 copy-start.1
  15.4 5.4 %all-to-all-start.1 = ((bf16[16,128,256]{2,1,0:T(8,128)(2,1)}), bf16[16,128,256]{2,1,0:T(8,128)(2,1)S(1)}, u32[]{:S(2)}, u32[]{:S(2)}) async-start(bf16[16,128,256]{2,1,0:T(8,128)(2,1)} %select_select_fusion), calls=%async_computation.1 | async-start | bytes 2097152 | tf_op jit(solution)/shard_map/all_to_all | solution.py:122
  20.8 0.0 copy-done.1
  20.8 0.0 copy-start.2
  20.8 1.3 %collective-permute-start = (bf16[16,32,256]{2,1,0:T(8,128)(2,1)S(1)}, bf16[16,32,256]{2,1,0:T(8,128)(2,1)S(1)}, u32[]{:S(2)}, u32[]{:S(2)}) collective-permute-start(bf16[16,32,256]{2,1,0:T(8,128)(2,1)S(1)} %get-tuple-element.8), channel_id=1, source_target_pairs={{0,16},{16,0},{1,17},{17,1},{2,18},{18,2},{3,19},{19,3},{4,20},{20... | collective-permute-start | bytes 786440 | tf_op jit(solution)/shard_map/ppermute | solution.py:135
  22.1 0.0 copy-done.2
  22.1 0.0 copy-start.5
  22.1 0.1 dynamic-slice_bitcast_fusion.3
  22.2 0.6 copy-done.5
  22.8 0.2 select_reduce_fusion.1
  22.9 0.7 pad_add_fusion.pos_ref
  23.6 0.7 fusion
  24.3 4.1 %collective-permute-done = bf16[16,32,256]{2,1,0:T(8,128)(2,1)S(1)} collective-permute-done((bf16[16,32,256]{2,1,0:T(8,128)(2,1)S(1)}, bf16[16,32,256]{2,1,0:T(8,128)(2,1)S(1)}, u32[]{:S(2)}, u32[]{:S(2)}) %collective-permute-start) | collective-permute-done | bytes 262176 | tf_op jit(solution)/shard_map/ppermute | solution.py:135
  28.4 0.8 %pad_maximum_fusion.fresh_ref = bf16[16,64,256]{2,1,0:T(8,128)(2,1)} fusion(bf16[16,32,256]{2,1,0:T(8,128)(2,1)S(1)} %collective-permute-done, bf16[16,32,256]{2,1,0:T(8,128)(2,1)S(1)} %get-tuple-element.7), kind=kLoop, calls=%fused_computation.1 | loop fusion | flops 1048576 | bytes 1048576 | tf_op jit(solution)/shard_map/concatenate | solution.py:138
  29.3 16.4 %all-to-all-done.1.recv_ref = bf16[16,128,256]{2,1,0:T(8,128)(2,1)S(1)} async-done(((bf16[16,128,256]{2,1,0:T(8,128)(2,1)}), bf16[16,128,256]{2,1,0:T(8,128)(2,1)S(1)}, u32[]{:S(2)}, u32[]{:S(2)}) %all-to-all-start.1) | async-done | bytes 1048608 | tf_op jit(solution)/shard_map/all_to_all | solution.py:122
  45.6 0.0 copy-start
  45.6 1.0 %copy-done = bf16[16,128,256]{2,1,0:T(8,128)(2,1)} copy-done((bf16[16,128,256]{2,1,0:T(8,128)(2,1)}, bf16[16,128,256]{2,1,0:T(8,128)(2,1)S(1)}, u32[]{:S(2)}) %copy-start) | copy-done | bytes 1048600
  46.6 24.7 %shard_map.82 = bf16[384,1024]{1,0:T(8,128)(2,1)} custom-call(s32[16]{0:T(128)} %copy-done.6, f32[1,2048]{1,0:T(1,128)} %bitcast.17, s32[16,64]{1,0:T(8,128)} %pad_add_fusion.pos_ref, bf16[16,128,256]{2,1,0:T(8,128)(2,1)} %copy-done, bf16[16,64,256]{2,1,0:T(8,128)(2,1)} %pad_maximum_fusion.fresh_ref, bf16[384,256]{1,0:T(8,128)(2,1)} %own_ref.1, ...), custom_call_target="tpu_custom_call" | custom-call | flops 3892314112 | bytes 3354624 | tf_op jit(solution)/shard_map/pallas_call | solution.py:96
  (2 shorter events, 0.1 us)
Async XLA Ops:
  0.0 0.7 copy-start.3
  0.0 0.7 copy-start.4
  0.9 0.6 copy-start.6
  2.3 11.2 %all-to-all-start = ((s32[16,1,1]{2,1,0:T(1,128)}), s32[16,1,1]{2,1,0:T(1,128)S(1)}, u32[]{:S(2)}, u32[]{:S(2)}) async-start(s32[16,1,1]{2,1,0:T(1,128)} %copy.11), calls=%async_computation | async-start | bytes 16384 | tf_op jit(solution)/shard_map/all_to_all | solution.py:118
  15.3 5.4 %copy-start.1 = (bf16[1,16,32,512]{3,2,1,0:T(8,128)(2,1)S(1)}, bf16[1,16,32,512]{3,2,1,0:T(8,128)(2,1)}, u32[]{:S(2)}) copy-start(bf16[1,16,32,512]{3,2,1,0:T(8,128)(2,1)} %param.11) | copy-start | bytes 1572868
  15.4 30.3 %all-to-all-start.1 = ((bf16[16,128,256]{2,1,0:T(8,128)(2,1)}), bf16[16,128,256]{2,1,0:T(8,128)(2,1)S(1)}, u32[]{:S(2)}, u32[]{:S(2)}) async-start(bf16[16,128,256]{2,1,0:T(8,128)(2,1)} %select_select_fusion), calls=%async_computation.1 | async-start | bytes 2097152 | tf_op jit(solution)/shard_map/all_to_all | solution.py:122
  20.8 1.3 %copy-start.2 = (s32[1,16,64]{2,1,0:T(8,128)S(1)}, s32[1,16,64]{2,1,0:T(8,128)}, u32[]{:S(2)}) copy-start(s32[1,16,64]{2,1,0:T(8,128)} %param.15) | copy-start | bytes 12292
  20.8 7.6 %collective-permute-start = (bf16[16,32,256]{2,1,0:T(8,128)(2,1)S(1)}, bf16[16,32,256]{2,1,0:T(8,128)(2,1)S(1)}, u32[]{:S(2)}, u32[]{:S(2)}) collective-permute-start(bf16[16,32,256]{2,1,0:T(8,128)(2,1)S(1)} %get-tuple-element.8), channel_id=1, source_target_pairs={{0,16},{16,0},{1,17},{17,1},{2,18},{18,2},{3,19},{19,3},{4,20},{20... | collective-permute-start | bytes 786440 | tf_op jit(solution)/shard_map/ppermute | solution.py:135
  22.1 0.7 copy-start.5
  45.6 1.0 %copy-start = (bf16[16,128,256]{2,1,0:T(8,128)(2,1)}, bf16[16,128,256]{2,1,0:T(8,128)(2,1)S(1)}, u32[]{:S(2)}) copy-start(bf16[16,128,256]{2,1,0:T(8,128)(2,1)S(1)} %all-to-all-done.1.recv_ref) | copy-start | bytes 3145732

commit v5 on v4

--- a/solution.py
+++ b/solution.py
@@ -18,22 +18,15 @@
     return jnp.sum(jnp.where(hits, table, 0), axis=-1)
 
 
-def attend_kernel(
-    owner_ref, bias_ref, pos_ref, recv_ref, fresh_ref, own_ref, q_ref, out_ref, kt_ref, vb_ref, ot_ref
-):
-    nch, nrec = pos_ref.shape
+def attend_kernel(owner_ref, bias_ref, recv_ref, fresh_ref, own_ref, q_ref, out_ref, kt_ref, vb_ref, ot_ref):
+    nch = fresh_ref.shape[0]
     rows = q_ref.shape[0]
     rate = HD ** (-0.5) * 1.4426950408889634
 
     @pl.when(pl.program_id(0) == 0)
     def _():
         def build(j, carry):
-            lib = recv_ref[owner_ref[j]]
-            where_at = pos_ref[pl.ds(j, 1), :]
-            pick = lax.broadcasted_iota(jnp.int32, (CL, nrec), 0) == where_at
-            up = jnp.dot(pick.astype(jnp.bfloat16), fresh_ref[j], preferred_element_type=jnp.float32)
-            hit = jnp.max(pick.astype(jnp.float32), axis=1, keepdims=True) > 0
-            block = jnp.where(hit, up.astype(jnp.bfloat16), lib)
+            block = jnp.concatenate([recv_ref[owner_ref[j]], fresh_ref[j]], axis=0)
             at = pl.ds(pl.multiple_of(j * CL, CL), CL)
             kt_ref[:, at] = block[:, :HD].T
             vb_ref[at, :] = block[:, HD:]
@@ -62,15 +55,15 @@
             out_ref[t * TR:(t + 1) * TR, g * HD:(g + 1) * HD] = mixed.astype(out_ref.dtype)
 
 
-def attend(owner, bias, pos, recv, fresh, own_kv, queries):
+def attend(owner, bias, recv, fresh, own_kv, queries):
     rows, width = queries.shape
     heads = width // HD
     step = PAIR if heads % PAIR == 0 else 1
-    nch, nrec = pos.shape
+    nch = fresh.shape[0]
     span = nch * CL
     keys = span + rows
-    flops = 4 * heads * rows * keys * HD + 2 * nch * CL * nrec * 2 * HD
-    bytes_accessed = 2 * (recv.size + fresh.size + own_kv.size + 2 * queries.size) + 4 * (bias.size + pos.size)
+    flops = 4 * heads * rows * keys * HD
+    bytes_accessed = 2 * (recv.size + fresh.size + own_kv.size + 2 * queries.size) + 4 * bias.size
 
     def full(shape):
         return pl.BlockSpec(shape, lambda g, o: (0,) * len(shape))
@@ -80,7 +73,6 @@
         grid=(heads // step,),
         in_specs=[
             full(bias.shape),
-            full(pos.shape),
             full(recv.shape),
             full(fresh.shape),
             full(own_kv.shape),
@@ -101,7 +93,7 @@
         cost_estimate=pl.CostEstimate(
             flops=flops, bytes_accessed=bytes_accessed, transcendentals=heads * rows * keys
         ),
-    )(owner, bias, pos, recv, fresh, own_kv, queries)
+    )(owner, bias, recv, fresh, own_kv, queries)
 
 
 def per_device(
@@ -113,19 +105,27 @@
     local = wanted % per_owner
     limits = lookup(stretch_len, wanted)
 
+    pos_local = recompute_pos[0]
+    pair = jnp.arange(pos_local.shape[1], dtype=jnp.int32)
+    odd_taken = pos_local - 2 * pair[None, :]
+    payload = jnp.concatenate([local[:, None], odd_taken], 1)
     devices = jnp.arange(n_seq, dtype=jnp.int32)
-    request = jnp.sum(jnp.where(owner[None, :] == devices[:, None], local[None, :], 0), axis=1)
-    asked = lax.all_to_all(request.reshape(n_seq, 1), "seq", 0, 0, tiled=True).reshape(n_seq)
-    send = jnp.broadcast_to(library[0], (n_seq,) + library.shape[1:])
-    for k in range(1, per_owner):
-        send = jnp.where((asked == k)[:, None, None], library[k], send)
+    hits = owner[None, :, None] == devices[:, None, None]
+    request = jnp.sum(jnp.where(hits, payload[None], 0), axis=1)
+    asked = lax.all_to_all(request, "seq", 0, 0, tiled=True)
+    which = asked[:, :1, None]
+    odd_given = asked[:, 1:, None]
+    halves = library.reshape(per_owner, -1, 2, library.shape[2])
+    send = None
+    for k in range(per_owner):
+        kept = jnp.where(odd_given == 0, halves[k, :, 1][None], halves[k, :, 0][None])
+        send = kept if send is None else jnp.where(which == k, kept, send)
     recv = lax.all_to_all(send, "seq", 0, 0, tiled=True)
 
     me = lax.axis_index("kvh")
     width = own_kv.shape[1]
     tokens = fresh_kv.shape[2]
     fresh_local = fresh_kv[0]
-    pos_local = recompute_pos[0]
     pieces = [lax.dynamic_slice_in_dim(fresh_local, me * width, width, 2)]
     places = [lax.dynamic_slice_in_dim(pos_local, me * tokens, tokens, 1)]
     for shift in range(1, n_kvh):
@@ -138,10 +138,11 @@
     fresh = jnp.concatenate(pieces, 1)
     pos = jnp.concatenate(places, 1)
 
-    column = jnp.arange(CL, dtype=jnp.int32)
-    bias = jnp.where(column[None, :] < limits[:, None], 0.0, -jnp.inf).astype(jnp.float32)
+    kept_at = 2 * pair[None, :] + 1 - odd_taken
+    at = jnp.concatenate([kept_at, pos], 1)
+    bias = jnp.where(at < limits[:, None], 0.0, -jnp.inf).astype(jnp.float32)
     bias = bias.reshape(1, -1)
-    return attend(owner, bias, pos, recv, fresh, own_kv, queries)
+    return attend(owner, bias, recv, fresh, own_kv, queries)
 
 
 def solution(mesh):

time: 71.7 us -> 59.1 us (0.82)
  the two profiles are of different devices: /device:TPU:9 before, /device:TPU:0 now
where the time goes in v5:
time: 59.1 us; the launch traced here: 58.7 us
  Pallas kernels  22.4 us (38%)
  waiting for transfers between devices  15.4 us (26%)
  starting transfers between devices  12.6 us (21%)
  local copies, waits for them, and re-layouts  4.22 us (7%)
  other arithmetic  3.94 us (7%)
    pallas_call x1, Pallas kernels, attend(): pl.pallas_call(attend_kernel, grid_spec=grid_spec, out_shape=jax.ShapeDty...  22.4 us
    all_to_all x1, starting transfers between devices, per_device(): asked = lax.all_to_all(request, 'seq', 0, 0, tiled=True)  7.39 us
    ppermute x1, waiting for transfers between devices, per_device(): pieces.append(lax.ppermute(piece, 'kvh', pairs))  5.4 us
    all_to_all x1, waiting for transfers between devices, per_device(): asked = lax.all_to_all(request, 'seq', 0, 0, tiled=True)  4.98 us
    all_to_all x1, waiting for transfers between devices, per_device(): recv = lax.all_to_all(send, 'seq', 0, 0, tiled=True)  4.97 us
    all_to_all x1, starting transfers between devices, per_device(): recv = lax.all_to_all(send, 'seq', 0, 0, tiled=True)  3.71 us
    unnamed x14, local copies, waits for them, and re-layouts  2.71 us
    ppermute x1, starting transfers between devices, per_device(): pieces.append(lax.ppermute(piece, 'kvh', pairs))  1.56 us
  transfers between devices with their start and end apart: 3, of which 3 were waited for; matrix products, arithmetic and copies ran while one was open for 5% of the time, Pallas kernels for 0%

profile of v5, /device:TPU:0, one launch (start us, length us, event | category | flops | bytes accessed | tf_op | source)
XLA Modules:
  0.0 58.7 jit_solution(6891456139839996879)
XLA Ops:
  0.0 0.0 copy-start.4
  0.0 0.0 copy-start.5
  0.0 0.7 %copy-done.4 = s32[48]{0:T(128)S(1)} copy-done((s32[48]{0:T(128)S(1)}, s32[48]{0:T(128)}, u32[]{:S(2)}) %copy-start.4) | copy-done | bytes 216
  0.7 0.0 copy-done.5
  0.7 0.2 select_reduce_fusion.2
  0.9 0.0 copy-start.3
  0.9 0.0 copy-start.2
  0.9 0.5 copy-done.3
  1.5 0.1 copy.31
  1.5 0.1 copy-done.2
  1.6 0.1 pad_add_fusion
  1.7 0.7 %select_reduce_fusion = s32[16,65]{1,0:T(8,128)} fusion(s32[16,65]{1,0:T(8,128)S(1)} %pad_add_fusion, pred[16,16]{1,0:T(8,128)(4,1)S(1)} %iota_compare_fusion), kind=kLoop, calls=%fused_computation.4 | loop fusion | flops 32240 | bytes 8576 | tf_op jit(solution)/shard_map/reduce_sum | solution.py:114
  2.4 7.4 %all-to-all-start = ((s32[16,1,65]{2,1,0:T(1,128)}), s32[16,1,65]{2,1,0:T(1,128)S(1)}, u32[]{:S(2)}, u32[]{:S(2)}) async-start(s32[16,1,65]{2,1,0:T(1,128)} %bitcast.7), calls=%async_computation | async-start | bytes 16384 | tf_op jit(solution)/shard_map/all_to_all | solution.py:115
  9.8 1.0 %reshape.131 = bf16[3,64,2,256]{3,2,1,0:T(2,128)(2,1)S(1)} reshape(bf16[3,128,256]{2,1,0:T(8,128)(2,1)} %param.10) | data formatting | bytes 393216 | tf_op jit(solution)/shard_map/reshape | solution.py:118
  10.8 0.3 fusion.1
  11.1 5.0 %all-to-all-done = s32[16,1,65]{2,1,0:T(1,128)S(1)} async-done(((s32[16,1,65]{2,1,0:T(1,128)}), s32[16,1,65]{2,1,0:T(1,128)S(1)}, u32[]{:S(2)}, u32[]{:S(2)}) %all-to-all-start) | async-done | bytes 4192 | tf_op jit(solution)/shard_map/all_to_all | solution.py:115
  16.1 0.1 compare_reduce_fusion.1
  16.2 0.1 slice_compare_fusion
  16.3 1.0 %select_select_fusion = bf16[16,64,256]{2,1,0:T(8,128)(2,1)} fusion(pred[16]{0:T(512)(128)(4,1)S(1)} %get-tuple-element.6, pred[16]{0:T(512)(128)(4,1)S(1)} %get-tuple-element.5, pred[16,64]{1,0:T(8,128)(4,1)S(1)} %slice_compare_fusion, bf16[64,256]{1,0:T(8,128)(2,1)S(1)} %get-tuple-element.21, bf16[64,256]{1,0:T(8,128)(2,1)S(1)} %get-tuple-element.22, ...), kind=kLoop, calls=%fused_computation.1 | loop fusion | flops 1310720 | bytes 721952 | tf_op jit(solution)/shard_map/jit(_where)/select_n | solution.py:122
  17.4 0.0 copy-start
  17.4 3.7 %all-to-all-start.1 = ((bf16[16,64,256]{2,1,0:T(8,128)(2,1)}), bf16[16,64,256]{2,1,0:T(8,128)(2,1)S(1)}, u32[]{:S(2)}, u32[]{:S(2)}) async-start(bf16[16,64,256]{2,1,0:T(8,128)(2,1)} %select_select_fusion), calls=%async_computation.1 | async-start | bytes 1048576 | tf_op jit(solution)/shard_map/all_to_all | solution.py:123
  21.1 0.0 copy-done
  21.1 1.6 %collective-permute-start = (bf16[16,32,256]{2,1,0:T(8,128)(2,1)S(1)}, bf16[16,32,256]{2,1,0:T(8,128)(2,1)S(1)}, u32[]{:S(2)}, u32[]{:S(2)}) collective-permute-start(bf16[16,32,256]{2,1,0:T(8,128)(2,1)S(1)} %get-tuple-element.10), channel_id=1, source_target_pairs={{0,16},{16,0},{1,17},{17,1},{2,18},{18,2},{3,19},{19,3},{4,20},{20... | collective-permute-start | bytes 786440 | tf_op jit(solution)/shard_map/ppermute | solution.py:135
  22.7 0.0 copy-start.6
  22.7 0.7 %copy-done.6 = s32[48]{0:T(128)S(1)} copy-done((s32[48]{0:T(128)S(1)}, s32[48]{0:T(128)}, u32[]{:S(2)}) %copy-start.6) | copy-done | bytes 216
  23.4 0.2 select_reduce_fusion.1
  23.5 0.1 dynamic-slice_bitcast_fusion.3
  23.6 0.7 %fusion = f32[16,128]{1,0:T(8,128)} fusion(s32[16,32]{1,0:T(8,128)S(1)} %get-tuple-element.18, s32[16,32]{1,0:T(8,128)S(1)} %get-tuple-element.17, s32[16,64]{1,0:T(8,128)S(1)} %get-tuple-element.7, s32[16]{0:T(128)S(1)} %select_reduce_fusion.1), kind=kLoop, calls=%fused_computation.22 | loop fusion | flops 8192 | bytes 16448 | tf_op jit(solution)/shard_map/jit(_where)/select_n | solution.py:143
  24.3 5.4 %collective-permute-done = bf16[16,32,256]{2,1,0:T(8,128)(2,1)S(1)} collective-permute-done((bf16[16,32,256]{2,1,0:T(8,128)(2,1)S(1)}, bf16[16,32,256]{2,1,0:T(8,128)(2,1)S(1)}, u32[]{:S(2)}, u32[]{:S(2)}) %collective-permute-start) | collective-permute-done | bytes 262176 | tf_op jit(solution)/shard_map/ppermute | solution.py:135
  29.7 0.8 %pad_maximum_fusion.fresh_ref = bf16[16,64,256]{2,1,0:T(8,128)(2,1)} fusion(bf16[16,32,256]{2,1,0:T(8,128)(2,1)S(1)} %collective-permute-done, bf16[16,32,256]{2,1,0:T(8,128)(2,1)S(1)} %get-tuple-element.9), kind=kLoop, calls=%fused_computation | loop fusion | flops 1048576 | bytes 1048576 | tf_op jit(solution)/shard_map/concatenate | solution.py:138
  30.5 5.0 %all-to-all-done.1.recv_ref = bf16[16,64,256]{2,1,0:T(8,128)(2,1)S(1)} async-done(((bf16[16,64,256]{2,1,0:T(8,128)(2,1)}), bf16[16,64,256]{2,1,0:T(8,128)(2,1)S(1)}, u32[]{:S(2)}, u32[]{:S(2)}) %all-to-all-start.1) | async-done | bytes 524320 | tf_op jit(solution)/shard_map/all_to_all | solution.py:123
  35.5 0.0 copy-start.1
  35.5 0.8 %copy-done.1 = bf16[16,64,256]{2,1,0:T(8,128)(2,1)} copy-done((bf16[16,64,256]{2,1,0:T(8,128)(2,1)}, bf16[16,64,256]{2,1,0:T(8,128)(2,1)S(1)}, u32[]{:S(2)}) %copy-start.1) | copy-done | bytes 524312
  36.3 22.4 %shard_map.82 = bf16[384,1024]{1,0:T(8,128)(2,1)} custom-call(s32[16]{0:T(128)} %copy-done.3, f32[1,2048]{1,0:T(1,128)} %bitcast.33, bf16[16,64,256]{2,1,0:T(8,128)(2,1)} %copy-done.1, bf16[16,64,256]{2,1,0:T(8,128)(2,1)} %pad_maximum_fusion.fresh_ref, bf16[384,256]{1,0:T(8,128)(2,1)} %own_ref.1, bf16[384,1024]{1,0:T(8,128)(2,1)} %q_ref.1), custom_call_target="tpu_custom_call" | custom-call | flops 3825205248 | bytes 2826240 | tf_op jit(solution)/shard_map/pallas_call | solution.py:88
  (9 shorter events, 0.1 us)
Async XLA Ops:
  0.0 0.7 %copy-start.4 = (s32[48]{0:T(128)S(1)}, s32[48]{0:T(128)}, u32[]{:S(2)}) copy-start(s32[48]{0:T(128)} %param.13) | copy-start | bytes 580
  0.0 0.7 %copy-start.5 = (s32[1,16]{1,0:T(1,128)S(1)}, s32[1,16]{1,0:T(1,128)}, u32[]{:S(2)}) copy-start(s32[1,16]{1,0:T(1,128)} %param.12) | copy-start | bytes 196
  0.9 0.6 copy-start.3
  0.9 0.7 %copy-start.2 = (s32[1,16,64]{2,1,0:T(8,128)S(1)}, s32[1,16,64]{2,1,0:T(8,128)}, u32[]{:S(2)}) copy-start(s32[1,16,64]{2,1,0:T(8,128)} %param.15) | copy-start | bytes 12292
  2.4 13.7 %all-to-all-start = ((s32[16,1,65]{2,1,0:T(1,128)}), s32[16,1,65]{2,1,0:T(1,128)S(1)}, u32[]{:S(2)}, u32[]{:S(2)}) async-start(s32[16,1,65]{2,1,0:T(1,128)} %bitcast.7), calls=%async_computation | async-start | bytes 16384 | tf_op jit(solution)/shard_map/all_to_all | solution.py:115
  17.4 3.7 %copy-start = (bf16[1,16,32,512]{3,2,1,0:T(8,128)(2,1)S(1)}, bf16[1,16,32,512]{3,2,1,0:T(8,128)(2,1)}, u32[]{:S(2)}) copy-start(bf16[1,16,32,512]{3,2,1,0:T(8,128)(2,1)} %param.11) | copy-start | bytes 1572868
  17.4 18.1 %all-to-all-start.1 = ((bf16[16,64,256]{2,1,0:T(8,128)(2,1)}), bf16[16,64,256]{2,1,0:T(8,128)(2,1)S(1)}, u32[]{:S(2)}, u32[]{:S(2)}) async-start(bf16[16,64,256]{2,1,0:T(8,128)(2,1)} %select_select_fusion), calls=%async_computation.1 | async-start | bytes 1048576 | tf_op jit(solution)/shard_map/all_to_all | solution.py:123
  21.1 8.5 %collective-permute-start = (bf16[16,32,256]{2,1,0:T(8,128)(2,1)S(1)}, bf16[16,32,256]{2,1,0:T(8,128)(2,1)S(1)}, u32[]{:S(2)}, u32[]{:S(2)}) collective-permute-start(bf16[16,32,256]{2,1,0:T(8,128)(2,1)S(1)} %get-tuple-element.10), channel_id=1, source_target_pairs={{0,16},{16,0},{1,17},{17,1},{2,18},{18,2},{3,19},{19,3},{4,20},{20... | collective-permute-start | bytes 786440 | tf_op jit(solution)/shard_map/ppermute | solution.py:135
  22.7 0.7 %copy-start.6 = (s32[48]{0:T(128)S(1)}, s32[48]{0:T(128)}, u32[]{:S(2)}) copy-start(s32[48]{0:T(128)} %param.14) | copy-start | bytes 580
  35.5 0.8 %copy-start.1 = (bf16[16,64,256]{2,1,0:T(8,128)(2,1)}, bf16[16,64,256]{2,1,0:T(8,128)(2,1)S(1)}, u32[]{:S(2)}) copy-start(bf16[16,64,256]{2,1,0:T(8,128)(2,1)S(1)} %all-to-all-done.1.recv_ref) | copy-start | bytes 1572868

commit v6 on v5

--- a/solution.py
+++ b/solution.py
@@ -35,24 +35,34 @@
         lax.fori_loop(0, nch, build, 0)
         ot_ref[...] = own_ref[:, :HD].T
 
-    for g in range(q_ref.shape[1] // HD):
-        for t in range(rows // TR):
-            qt = q_ref[t * TR:(t + 1) * TR, g * HD:(g + 1) * HD]
-            s1 = jnp.dot(qt, kt_ref[...], preferred_element_type=jnp.float32) + bias_ref[...]
-            kk = (t + 1) * TR
-            s2 = jnp.dot(qt, ot_ref[:, :kk], preferred_element_type=jnp.float32)
-            row = lax.broadcasted_iota(jnp.int32, (TR, kk), 0) + t * TR
-            col = lax.broadcasted_iota(jnp.int32, (TR, kk), 1)
-            s2 = jnp.where(col <= row, s2, -jnp.inf)
-            top = jnp.maximum(jnp.max(s1, axis=1, keepdims=True), jnp.max(s2, axis=1, keepdims=True))
-            e1 = jnp.exp2((s1 - top) * rate)
-            e2 = jnp.exp2((s2 - top) * rate)
-            inv = 1.0 / (jnp.sum(e1, axis=1, keepdims=True) + jnp.sum(e2, axis=1, keepdims=True))
-            w1 = (e1 * inv).astype(jnp.bfloat16)
-            w2 = (e2 * inv).astype(jnp.bfloat16)
-            mixed = jnp.dot(w1, vb_ref[...], preferred_element_type=jnp.float32)
-            mixed = mixed + jnp.dot(w2, own_ref[:kk, HD:], preferred_element_type=jnp.float32)
-            out_ref[t * TR:(t + 1) * TR, g * HD:(g + 1) * HD] = mixed.astype(out_ref.dtype)
+    def scores(g, t):
+        qt = q_ref[t * TR:(t + 1) * TR, g * HD:(g + 1) * HD]
+        s1 = jnp.dot(qt, kt_ref[...], preferred_element_type=jnp.float32) + bias_ref[...]
+        kk = (t + 1) * TR
+        s2 = jnp.dot(qt, ot_ref[:, :kk], preferred_element_type=jnp.float32)
+        row = lax.broadcasted_iota(jnp.int32, (TR, kk), 0) + t * TR
+        col = lax.broadcasted_iota(jnp.int32, (TR, kk), 1)
+        return s1, jnp.where(col <= row, s2, -jnp.inf)
+
+    def finish(g, t, s1, s2):
+        kk = (t + 1) * TR
+        top = jnp.maximum(jnp.max(s1, axis=1, keepdims=True), jnp.max(s2, axis=1, keepdims=True))
+        e1 = jnp.exp2((s1 - top) * rate)
+        e2 = jnp.exp2((s2 - top) * rate)
+        inv = 1.0 / (jnp.sum(e1, axis=1, keepdims=True) + jnp.sum(e2, axis=1, keepdims=True))
+        w1 = (e1 * inv).astype(jnp.bfloat16)
+        w2 = (e2 * inv).astype(jnp.bfloat16)
+        mixed = jnp.dot(w1, vb_ref[...], preferred_element_type=jnp.float32)
+        mixed = mixed + jnp.dot(w2, own_ref[:kk, HD:], preferred_element_type=jnp.float32)
+        out_ref[t * TR:(t + 1) * TR, g * HD:(g + 1) * HD] = mixed.astype(out_ref.dtype)
+
+    tiles = [(g, t) for g in range(q_ref.shape[1] // HD) for t in range(rows // TR)]
+    ahead = scores(*tiles[0])
+    for k, tile in enumerate(tiles):
+        now = ahead
+        if k + 1 < len(tiles):
+            ahead = scores(*tiles[k + 1])
+        finish(*tile, *now)
 
 
 def attend(owner, bias, recv, fresh, own_kv, queries):

time: 59.1 us -> 53.3 us (0.902)
  Pallas kernels: 22.4 us -> 16.6 us
    pallas_call x1, Pallas kernels: 22.4 us -> 16.6 us  [attend(): pl.pallas_call(attend_kernel, grid_spec=grid_spec, out_shape=jax.ShapeDty...]
  transfers between devices with their start and end apart: 3 -> 3, of which waited for: 3 -> 3; matrix products, arithmetic and copies ran while one was open for 5% -> 6% of each run, Pallas kernels for 0% -> 0%
where the time goes in v6:
time: 53.3 us; the launch traced here: 52.9 us
  Pallas kernels  16.6 us (31%)
  waiting for transfers between devices  15.4 us (29%)
  starting transfers between devices  12.6 us (24%)
  local copies, waits for them, and re-layouts  4.22 us (8%)
  other arithmetic  3.94 us (7%)
    pallas_call x1, Pallas kernels, attend(): pl.pallas_call(attend_kernel, grid_spec=grid_spec, out_shape=jax.ShapeDty...  16.6 us
    all_to_all x1, starting transfers between devices, per_device(): asked = lax.all_to_all(request, 'seq', 0, 0, tiled=True)  7.39 us
    ppermute x1, waiting for transfers between devices, per_device(): pieces.append(lax.ppermute(piece, 'kvh', pairs))  5.4 us
    all_to_all x1, waiting for transfers between devices, per_device(): asked = lax.all_to_all(request, 'seq', 0, 0, tiled=True)  4.98 us
    all_to_all x1, waiting for transfers between devices, per_device(): recv = lax.all_to_all(send, 'seq', 0, 0, tiled=True)  4.97 us
    all_to_all x1, starting transfers between devices, per_device(): recv = lax.all_to_all(send, 'seq', 0, 0, tiled=True)  3.71 us
    unnamed x14, local copies, waits for them, and re-layouts  2.71 us
    ppermute x1, starting transfers between devices, per_device(): pieces.append(lax.ppermute(piece, 'kvh', pairs))  1.56 us
  transfers between devices with their start and end apart: 3, of which 3 were waited for; matrix products, arithmetic and copies ran while one was open for 6% of the time, Pallas kernels for 0%

profile of v6, /device:TPU:0, one launch (start us, length us, event | category | flops | bytes accessed | tf_op | source)
XLA Modules:
  0.0 52.9 jit_solution(5453254888912479587)
XLA Ops:
  0.0 0.0 copy-start.4
  0.0 0.0 copy-start.5
  0.0 0.7 %copy-done.4 = s32[48]{0:T(128)S(1)} copy-done((s32[48]{0:T(128)S(1)}, s32[48]{0:T(128)}, u32[]{:S(2)}) %copy-start.4) | copy-done | bytes 216
  0.7 0.0 copy-done.5
  0.7 0.2 select_reduce_fusion.2
  0.9 0.0 copy-start.3
  0.9 0.0 copy-start.2
  0.9 0.5 copy-done.3
  1.5 0.1 copy.31
  1.5 0.1 copy-done.2
  1.6 0.1 pad_add_fusion
  1.7 0.7 %select_reduce_fusion = s32[16,65]{1,0:T(8,128)} fusion(s32[16,65]{1,0:T(8,128)S(1)} %pad_add_fusion, pred[16,16]{1,0:T(8,128)(4,1)S(1)} %iota_compare_fusion), kind=kLoop, calls=%fused_computation.4 | loop fusion | flops 32240 | bytes 8576 | tf_op jit(solution)/shard_map/reduce_sum | solution.py:124
  2.4 7.4 %all-to-all-start = ((s32[16,1,65]{2,1,0:T(1,128)}), s32[16,1,65]{2,1,0:T(1,128)S(1)}, u32[]{:S(2)}, u32[]{:S(2)}) async-start(s32[16,1,65]{2,1,0:T(1,128)} %bitcast.7), calls=%async_computation | async-start | bytes 16384 | tf_op jit(solution)/shard_map/all_to_all | solution.py:125
  9.8 1.0 %reshape.131 = bf16[3,64,2,256]{3,2,1,0:T(2,128)(2,1)S(1)} reshape(bf16[3,128,256]{2,1,0:T(8,128)(2,1)} %param.10) | data formatting | bytes 393216 | tf_op jit(solution)/shard_map/reshape | solution.py:128
  10.8 0.3 fusion.1
  11.1 5.0 %all-to-all-done = s32[16,1,65]{2,1,0:T(1,128)S(1)} async-done(((s32[16,1,65]{2,1,0:T(1,128)}), s32[16,1,65]{2,1,0:T(1,128)S(1)}, u32[]{:S(2)}, u32[]{:S(2)}) %all-to-all-start) | async-done | bytes 4192 | tf_op jit(solution)/shard_map/all_to_all | solution.py:125
  16.1 0.1 compare_reduce_fusion.1
  16.2 0.1 slice_compare_fusion
  16.3 1.0 %select_select_fusion = bf16[16,64,256]{2,1,0:T(8,128)(2,1)} fusion(pred[16]{0:T(512)(128)(4,1)S(1)} %get-tuple-element.6, pred[16]{0:T(512)(128)(4,1)S(1)} %get-tuple-element.5, pred[16,64]{1,0:T(8,128)(4,1)S(1)} %slice_compare_fusion, bf16[64,256]{1,0:T(8,128)(2,1)S(1)} %get-tuple-element.21, bf16[64,256]{1,0:T(8,128)(2,1)S(1)} %get-tuple-element.22, ...), kind=kLoop, calls=%fused_computation.1 | loop fusion | flops 1310720 | bytes 721952 | tf_op jit(solution)/shard_map/jit(_where)/select_n | solution.py:132
  17.4 0.0 copy-start
  17.4 3.7 %all-to-all-start.1 = ((bf16[16,64,256]{2,1,0:T(8,128)(2,1)}), bf16[16,64,256]{2,1,0:T(8,128)(2,1)S(1)}, u32[]{:S(2)}, u32[]{:S(2)}) async-start(bf16[16,64,256]{2,1,0:T(8,128)(2,1)} %select_select_fusion), calls=%async_computation.1 | async-start | bytes 1048576 | tf_op jit(solution)/shard_map/all_to_all | solution.py:133
  21.1 0.0 copy-done
  21.1 1.6 %collective-permute-start = (bf16[16,32,256]{2,1,0:T(8,128)(2,1)S(1)}, bf16[16,32,256]{2,1,0:T(8,128)(2,1)S(1)}, u32[]{:S(2)}, u32[]{:S(2)}) collective-permute-start(bf16[16,32,256]{2,1,0:T(8,128)(2,1)S(1)} %get-tuple-element.10), channel_id=1, source_target_pairs={{0,16},{16,0},{1,17},{17,1},{2,18},{18,2},{3,19},{19,3},{4,20},{20... | collective-permute-start | bytes 786440 | tf_op jit(solution)/shard_map/ppermute | solution.py:145
  22.7 0.0 copy-start.6
  22.7 0.7 %copy-done.6 = s32[48]{0:T(128)S(1)} copy-done((s32[48]{0:T(128)S(1)}, s32[48]{0:T(128)}, u32[]{:S(2)}) %copy-start.6) | copy-done | bytes 216
  23.4 0.2 select_reduce_fusion.1
  23.5 0.1 dynamic-slice_bitcast_fusion.3
  23.6 0.7 %fusion = f32[16,128]{1,0:T(8,128)} fusion(s32[16,32]{1,0:T(8,128)S(1)} %get-tuple-element.18, s32[16,32]{1,0:T(8,128)S(1)} %get-tuple-element.17, s32[16,64]{1,0:T(8,128)S(1)} %get-tuple-element.7, s32[16]{0:T(128)S(1)} %select_reduce_fusion.1), kind=kLoop, calls=%fused_computation.22 | loop fusion | flops 8192 | bytes 16448 | tf_op jit(solution)/shard_map/jit(_where)/select_n | solution.py:153
  24.3 5.4 %collective-permute-done = bf16[16,32,256]{2,1,0:T(8,128)(2,1)S(1)} collective-permute-done((bf16[16,32,256]{2,1,0:T(8,128)(2,1)S(1)}, bf16[16,32,256]{2,1,0:T(8,128)(2,1)S(1)}, u32[]{:S(2)}, u32[]{:S(2)}) %collective-permute-start) | collective-permute-done | bytes 262176 | tf_op jit(solution)/shard_map/ppermute | solution.py:145
  29.7 0.8 %pad_maximum_fusion.fresh_ref = bf16[16,64,256]{2,1,0:T(8,128)(2,1)} fusion(bf16[16,32,256]{2,1,0:T(8,128)(2,1)S(1)} %collective-permute-done, bf16[16,32,256]{2,1,0:T(8,128)(2,1)S(1)} %get-tuple-element.9), kind=kLoop, calls=%fused_computation | loop fusion | flops 1048576 | bytes 1048576 | tf_op jit(solution)/shard_map/concatenate | solution.py:148
  30.5 5.0 %all-to-all-done.1.recv_ref = bf16[16,64,256]{2,1,0:T(8,128)(2,1)S(1)} async-done(((bf16[16,64,256]{2,1,0:T(8,128)(2,1)}), bf16[16,64,256]{2,1,0:T(8,128)(2,1)S(1)}, u32[]{:S(2)}, u32[]{:S(2)}) %all-to-all-start.1) | async-done | bytes 524320 | tf_op jit(solution)/shard_map/all_to_all | solution.py:133
  35.5 0.0 copy-start.1
  35.5 0.8 %copy-done.1 = bf16[16,64,256]{2,1,0:T(8,128)(2,1)} copy-done((bf16[16,64,256]{2,1,0:T(8,128)(2,1)}, bf16[16,64,256]{2,1,0:T(8,128)(2,1)S(1)}, u32[]{:S(2)}) %copy-start.1) | copy-done | bytes 524312
  36.3 16.6 %shard_map.82 = bf16[384,1024]{1,0:T(8,128)(2,1)} custom-call(s32[16]{0:T(128)} %copy-done.3, f32[1,2048]{1,0:T(1,128)} %bitcast.33, bf16[16,64,256]{2,1,0:T(8,128)(2,1)} %copy-done.1, bf16[16,64,256]{2,1,0:T(8,128)(2,1)} %pad_maximum_fusion.fresh_ref, bf16[384,256]{1,0:T(8,128)(2,1)} %own_ref.1, bf16[384,1024]{1,0:T(8,128)(2,1)} %q_ref.1), custom_call_target="tpu_custom_call" | custom-call | flops 3825205248 | bytes 2826240 | tf_op jit(solution)/shard_map/pallas_call | solution.py:98
  (9 shorter events, 0.1 us)
Async XLA Ops:
  0.0 0.7 %copy-start.4 = (s32[48]{0:T(128)S(1)}, s32[48]{0:T(128)}, u32[]{:S(2)}) copy-start(s32[48]{0:T(128)} %param.13) | copy-start | bytes 580
  0.0 0.7 %copy-start.5 = (s32[1,16]{1,0:T(1,128)S(1)}, s32[1,16]{1,0:T(1,128)}, u32[]{:S(2)}) copy-start(s32[1,16]{1,0:T(1,128)} %param.12) | copy-start | bytes 196
  0.9 0.6 %copy-start.3 = (s32[16]{0:T(128)}, s32[16]{0:T(128)S(1)}, u32[]{:S(2)}) copy-start(s32[16]{0:T(128)S(1)} %and_select_fusion.1.owner_ref) | copy-start | bytes 196
  0.9 0.7 %copy-start.2 = (s32[1,16,64]{2,1,0:T(8,128)S(1)}, s32[1,16,64]{2,1,0:T(8,128)}, u32[]{:S(2)}) copy-start(s32[1,16,64]{2,1,0:T(8,128)} %param.15) | copy-start | bytes 12292
  2.4 13.7 %all-to-all-start = ((s32[16,1,65]{2,1,0:T(1,128)}), s32[16,1,65]{2,1,0:T(1,128)S(1)}, u32[]{:S(2)}, u32[]{:S(2)}) async-start(s32[16,1,65]{2,1,0:T(1,128)} %bitcast.7), calls=%async_computation | async-start | bytes 16384 | tf_op jit(solution)/shard_map/all_to_all | solution.py:125
  17.4 3.7 %copy-start = (bf16[1,16,32,512]{3,2,1,0:T(8,128)(2,1)S(1)}, bf16[1,16,32,512]{3,2,1,0:T(8,128)(2,1)}, u32[]{:S(2)}) copy-start(bf16[1,16,32,512]{3,2,1,0:T(8,128)(2,1)} %param.11) | copy-start | bytes 1572868
  17.4 18.1 %all-to-all-start.1 = ((bf16[16,64,256]{2,1,0:T(8,128)(2,1)}), bf16[16,64,256]{2,1,0:T(8,128)(2,1)S(1)}, u32[]{:S(2)}, u32[]{:S(2)}) async-start(bf16[16,64,256]{2,1,0:T(8,128)(2,1)} %select_select_fusion), calls=%async_computation.1 | async-start | bytes 1048576 | tf_op jit(solution)/shard_map/all_to_all | solution.py:133
  21.1 8.5 %collective-permute-start = (bf16[16,32,256]{2,1,0:T(8,128)(2,1)S(1)}, bf16[16,32,256]{2,1,0:T(8,128)(2,1)S(1)}, u32[]{:S(2)}, u32[]{:S(2)}) collective-permute-start(bf16[16,32,256]{2,1,0:T(8,128)(2,1)S(1)} %get-tuple-element.10), channel_id=1, source_target_pairs={{0,16},{16,0},{1,17},{17,1},{2,18},{18,2},{3,19},{19,3},{4,20},{20... | collective-permute-start | bytes 786440 | tf_op jit(solution)/shard_map/ppermute | solution.py:145
  22.7 0.7 %copy-start.6 = (s32[48]{0:T(128)S(1)}, s32[48]{0:T(128)}, u32[]{:S(2)}) copy-start(s32[48]{0:T(128)} %param.14) | copy-start | bytes 580
  35.5 0.8 %copy-start.1 = (bf16[16,64,256]{2,1,0:T(8,128)(2,1)}, bf16[16,64,256]{2,1,0:T(8,128)(2,1)S(1)}, u32[]{:S(2)}) copy-start(bf16[16,64,256]{2,1,0:T(8,128)(2,1)S(1)} %all-to-all-done.1.recv_ref) | copy-start | bytes 1572868

commit v7 on v6

--- a/solution.py
+++ b/solution.py
@@ -11,6 +11,7 @@
 CL = 128
 TR = 128
 PAIR = 4
+LEAD = 2
 
 
 def lookup(table, indices):
@@ -18,28 +19,18 @@
     return jnp.sum(jnp.where(hits, table, 0), axis=-1)
 
 
-def attend_kernel(owner_ref, bias_ref, recv_ref, fresh_ref, own_ref, q_ref, out_ref, kt_ref, vb_ref, ot_ref):
-    nch = fresh_ref.shape[0]
+def attend_kernel(bias_ref, kept_ref, fresh_ref, own_ref, q_ref, out_ref):
     rows = q_ref.shape[0]
     rate = HD ** (-0.5) * 1.4426950408889634
-
-    @pl.when(pl.program_id(0) == 0)
-    def _():
-        def build(j, carry):
-            block = jnp.concatenate([recv_ref[owner_ref[j]], fresh_ref[j]], axis=0)
-            at = pl.ds(pl.multiple_of(j * CL, CL), CL)
-            kt_ref[:, at] = block[:, :HD].T
-            vb_ref[at, :] = block[:, HD:]
-            return carry
-
-        lax.fori_loop(0, nch, build, 0)
-        ot_ref[...] = own_ref[:, :HD].T
+    nt = (((1,), (1,)), ((), ()))
 
     def scores(g, t):
         qt = q_ref[t * TR:(t + 1) * TR, g * HD:(g + 1) * HD]
-        s1 = jnp.dot(qt, kt_ref[...], preferred_element_type=jnp.float32) + bias_ref[...]
+        sk = lax.dot_general(qt, kept_ref[:, :HD], nt, preferred_element_type=jnp.float32)
+        sf = lax.dot_general(qt, fresh_ref[:, :HD], nt, preferred_element_type=jnp.float32)
+        s1 = jnp.concatenate([sk, sf], 1) + bias_ref[...]
         kk = (t + 1) * TR
-        s2 = jnp.dot(qt, ot_ref[:, :kk], preferred_element_type=jnp.float32)
+        s2 = lax.dot_general(qt, own_ref[:kk, :HD], nt, preferred_element_type=jnp.float32)
         row = lax.broadcasted_iota(jnp.int32, (TR, kk), 0) + t * TR
         col = lax.broadcasted_iota(jnp.int32, (TR, kk), 1)
         return s1, jnp.where(col <= row, s2, -jnp.inf)
@@ -52,58 +43,48 @@
         inv = 1.0 / (jnp.sum(e1, axis=1, keepdims=True) + jnp.sum(e2, axis=1, keepdims=True))
         w1 = (e1 * inv).astype(jnp.bfloat16)
         w2 = (e2 * inv).astype(jnp.bfloat16)
-        mixed = jnp.dot(w1, vb_ref[...], preferred_element_type=jnp.float32)
+        split = kept_ref.shape[0]
+        mixed = jnp.dot(w1[:, :split], kept_ref[:, HD:], preferred_element_type=jnp.float32)
+        mixed = mixed + jnp.dot(w1[:, split:], fresh_ref[:, HD:], preferred_element_type=jnp.float32)
         mixed = mixed + jnp.dot(w2, own_ref[:kk, HD:], preferred_element_type=jnp.float32)
         out_ref[t * TR:(t + 1) * TR, g * HD:(g + 1) * HD] = mixed.astype(out_ref.dtype)
 
     tiles = [(g, t) for g in range(q_ref.shape[1] // HD) for t in range(rows // TR)]
-    ahead = scores(*tiles[0])
+    ready = [scores(*tile) for tile in tiles[:LEAD]]
     for k, tile in enumerate(tiles):
-        now = ahead
-        if k + 1 < len(tiles):
-            ahead = scores(*tiles[k + 1])
-        finish(*tile, *now)
+        if k + LEAD < len(tiles):
+            ready.append(scores(*tiles[k + LEAD]))
+        finish(*tile, *ready[k])
 
 
-def attend(owner, bias, recv, fresh, own_kv, queries):
+def attend(bias, kept, fresh, own_kv, queries):
     rows, width = queries.shape
     heads = width // HD
     step = PAIR if heads % PAIR == 0 else 1
-    nch = fresh.shape[0]
-    span = nch * CL
-    keys = span + rows
+    keys = kept.shape[0] + fresh.shape[0] + rows
     flops = 4 * heads * rows * keys * HD
-    bytes_accessed = 2 * (recv.size + fresh.size + own_kv.size + 2 * queries.size) + 4 * bias.size
+    bytes_accessed = 2 * (kept.size + fresh.size + own_kv.size + 2 * queries.size) + 4 * bias.size
 
     def full(shape):
-        return pl.BlockSpec(shape, lambda g, o: (0,) * len(shape))
+        return pl.BlockSpec(shape, lambda g: (0,) * len(shape))
 
-    grid_spec = pltpu.PrefetchScalarGridSpec(
-        num_scalar_prefetch=1,
+    return pl.pallas_call(
+        attend_kernel,
         grid=(heads // step,),
         in_specs=[
             full(bias.shape),
-            full(recv.shape),
+            full(kept.shape),
             full(fresh.shape),
             full(own_kv.shape),
-            pl.BlockSpec((rows, step * HD), lambda g, o: (0, g)),
+            pl.BlockSpec((rows, step * HD), lambda g: (0, g)),
         ],
-        out_specs=pl.BlockSpec((rows, step * HD), lambda g, o: (0, g)),
-        scratch_shapes=[
-            pltpu.VMEM((HD, span), jnp.bfloat16),
-            pltpu.VMEM((span, HD), jnp.bfloat16),
-            pltpu.VMEM((HD, rows), jnp.bfloat16),
-        ],
-    )
-    return pl.pallas_call(
-        attend_kernel,
-        grid_spec=grid_spec,
+        out_specs=pl.BlockSpec((rows, step * HD), lambda g: (0, g)),
         out_shape=jax.ShapeDtypeStruct(queries.shape, queries.dtype),
         compiler_params=pltpu.CompilerParams(dimension_semantics=("arbitrary",)),
         cost_estimate=pl.CostEstimate(
             flops=flops, bytes_accessed=bytes_accessed, transcendentals=heads * rows * keys
         ),
-    )(owner, bias, recv, fresh, own_kv, queries)
+    )(bias, kept, fresh, own_kv, queries)
 
 
 def per_device(
@@ -149,10 +130,14 @@
     pos = jnp.concatenate(places, 1)
 
     kept_at = 2 * pair[None, :] + 1 - odd_taken
-    at = jnp.concatenate([kept_at, pos], 1)
-    bias = jnp.where(at < limits[:, None], 0.0, -jnp.inf).astype(jnp.float32)
-    bias = bias.reshape(1, -1)
-    return attend(owner, bias, recv, fresh, own_kv, queries)
+    kept_bias = jnp.where(kept_at < limits[:, None], 0.0, -jnp.inf).astype(jnp.float32)
+    slot_of = owner[None, :] == devices[:, None]
+    kept_bias = jnp.where(slot_of[:, :, None], kept_bias[None], 0.0).sum(1)
+    kept_bias = jnp.where(jnp.any(slot_of, 1)[:, None], kept_bias, -jnp.inf)
+    fresh_bias = jnp.where(pos < limits[:, None], 0.0, -jnp.inf).astype(jnp.float32)
+    bias = jnp.concatenate([kept_bias.reshape(1, -1), fresh_bias.reshape(1, -1)], 1)
+    kept = recv.reshape(-1, recv.shape[2])
+    return attend(bias, kept, fresh.reshape(-1, fresh.shape[2]), own_kv, queries)
 
 
 def solution(mesh):

time: 53.3 us -> 50.1 us (0.940)
  Pallas kernels: 16.6 us -> 13.7 us
    all_to_all x1, waiting for transfers between devices: 4.97 us -> 12.5 us  [per_device(): recv = lax.all_to_all(send, 'seq', 0, 0, tiled=True)]
    ppermute x1, waiting for transfers between devices: 5.4 us -> 0.01 us  [per_device(): pieces.append(lax.ppermute(piece, 'kvh', pairs))]
    pallas_call x1, Pallas kernels: 16.6 us -> 13.7 us  [attend(): pl.pallas_call(attend_kernel, grid=(heads // step,), in_specs=[full(bias....]
    all_to_all x1, waiting for transfers between devices: 4.98 us -> 2.91 us  [per_device(): asked = lax.all_to_all(request, 'seq', 0, 0, tiled=True)]
    dynamic_slice x1, local copies, waits for them, and re-layouts: 0.04 us -> 1.11 us  [per_device(): pieces = [lax.dynamic_slice_in_dim(fresh_local, me * width, width, 2)]]
    reshape x1, local copies, waits for them, and re-layouts: 1.01 us -> 0.08 us  [per_device(): halves = library.reshape(per_owner, -1, 2, library.shape[2])]
    unnamed x14 -> x15, local copies, waits for them, and re-layouts: 2.71 us -> 1.98 us
    concatenate x0 -> x1, other arithmetic: none -> 0.61 us  [per_device(): jnp.concatenate([kept_bias.reshape(1, -1), fresh_bias.reshape(1, -1)], 1)]
  transfers between devices with their start and end apart: 3 -> 3, of which waited for: 3 -> 2; matrix products, arithmetic and copies ran while one was open for 6% -> 10% of each run, Pallas kernels for 0% -> 0%
where the time goes in v7:
time: 50.1 us; the launch traced here: 49.8 us
  waiting for transfers between devices  15.4 us (31%)
  Pallas kernels  13.7 us (27%)
  starting transfers between devices  12.5 us (25%)
  other arithmetic  4.33 us (9%)
  local copies, waits for them, and re-layouts  3.76 us (8%)
    pallas_call x1, Pallas kernels, attend(): pl.pallas_call(attend_kernel, grid=(heads // step,), in_specs=[full(bias....  13.7 us
    all_to_all x1, waiting for transfers between devices, per_device(): recv = lax.all_to_all(send, 'seq', 0, 0, tiled=True)  12.5 us
    all_to_all x1, starting transfers between devices, per_device(): asked = lax.all_to_all(request, 'seq', 0, 0, tiled=True)  7.39 us
    all_to_all x1, starting transfers between devices, per_device(): recv = lax.all_to_all(send, 'seq', 0, 0, tiled=True)  3.57 us
    all_to_all x1, waiting for transfers between devices, per_device(): asked = lax.all_to_all(request, 'seq', 0, 0, tiled=True)  2.91 us
    unnamed x15, local copies, waits for them, and re-layouts  1.98 us
    ppermute x1, starting transfers between devices, per_device(): pieces.append(lax.ppermute(piece, 'kvh', pairs))  1.59 us
    dynamic_slice x1, local copies, waits for them, and re-layouts, per_device(): pieces = [lax.dynamic_slice_in_dim(fresh_local, me * width, width, 2)]  1.11 us
  transfers between devices with their start and end apart: 3, of which 2 were waited for; matrix products, arithmetic and copies ran while one was open for 10% of the time, Pallas kernels for 0%

profile of v7, /device:TPU:0, one launch (start us, length us, event | category | flops | bytes accessed | tf_op | source)
XLA Modules:
  0.0 49.8 jit_solution(4246491966223571015)
XLA Ops:
  0.0 0.0 copy-start.3
  0.0 0.0 copy-start.4
  0.0 0.7 %copy-done.3 = s32[48]{0:T(128)S(1)} copy-done((s32[48]{0:T(128)S(1)}, s32[48]{0:T(128)}, u32[]{:S(2)}) %copy-start.3) | copy-done | bytes 216
  0.7 0.0 copy-done.4
  0.7 0.2 select_reduce_fusion.3
  0.9 0.0 copy-start.2
  0.9 0.1 fusion.1
  1.0 0.1 copy.17
  1.1 0.5 copy-done.2
  1.6 0.1 pad_add_fusion
  1.7 0.7 %select_reduce_fusion = s32[16,65]{1,0:T(8,128)} fusion(s32[16,65]{1,0:T(8,128)S(1)} %pad_add_fusion, pred[16,16]{1,0:T(8,128)(4,1)S(1)} %get-tuple-element.18), kind=kLoop, calls=%fused_computation.4 | loop fusion | flops 32240 | bytes 8576 | tf_op jit(solution)/shard_map/reduce_sum | solution.py:105
  2.4 7.4 %all-to-all-start = ((s32[16,1,65]{2,1,0:T(1,128)}), s32[16,1,65]{2,1,0:T(1,128)S(1)}, u32[]{:S(2)}, u32[]{:S(2)}) async-start(s32[16,1,65]{2,1,0:T(1,128)} %bitcast.7), calls=%async_computation | async-start | bytes 16384 | tf_op jit(solution)/shard_map/all_to_all | solution.py:106
  9.8 0.0 copy-start.1
  9.8 1.1 %dynamic-slice_bitcast_fusion.1 = (bf16[16,32,256]{2,1,0:T(8,128)(2,1)S(1)}, bf16[16,32,256]{2,1,0:T(8,128)(2,1)S(1)}) fusion(bf16[1,16,32,512]{3,2,1,0:T(8,128)(2,1)} %param.11, s32[]{:T(128)S(6)} %select_n.121, s32[]{:T(128)S(6)} %select_n.122), kind=kLoop, calls=%fused_computation.3 | loop fusion | bytes 1048584 | tf_op jit(solution)/shard_map/dynamic_slice | solution.py:120
  10.9 0.0 copy-start.5
  10.9 1.6 %collective-permute-start = (bf16[16,32,256]{2,1,0:T(8,128)(2,1)S(1)}, bf16[16,32,256]{2,1,0:T(8,128)(2,1)S(1)}, u32[]{:S(2)}, u32[]{:S(2)}) collective-permute-start(bf16[16,32,256]{2,1,0:T(8,128)(2,1)S(1)} %get-tuple-element.8), channel_id=1, source_target_pairs={{0,16},{16,0},{1,17},{17,1},{2,18},{18,2},{3,19},{19,3},{4,20},{20... | collective-permute-start | bytes 786440 | tf_op jit(solution)/shard_map/ppermute | solution.py:126
  12.5 0.0 copy-done.5
  12.5 0.2 select_reduce_fusion.2
  12.7 0.0 copy-done.1
  12.7 0.1 reshape.206
  12.8 0.3 fusion.2
  13.1 0.1 select_bitcast_fusion
  13.2 2.9 %all-to-all-done = s32[16,1,65]{2,1,0:T(1,128)S(1)} async-done(((s32[16,1,65]{2,1,0:T(1,128)}), s32[16,1,65]{2,1,0:T(1,128)S(1)}, u32[]{:S(2)}, u32[]{:S(2)}) %all-to-all-start) | async-done | bytes 4192 | tf_op jit(solution)/shard_map/all_to_all | solution.py:106
  16.1 0.1 compare_reduce_fusion.1
  16.2 0.1 slice_compare_fusion
  16.3 1.0 %select_select_fusion = bf16[16,64,256]{2,1,0:T(8,128)(2,1)} fusion(pred[16]{0:T(512)(128)(4,1)S(1)} %get-tuple-element.6, pred[16]{0:T(512)(128)(4,1)S(1)} %get-tuple-element.5, pred[16,64]{1,0:T(8,128)(4,1)S(1)} %slice_compare_fusion, bf16[64,256]{1,0:T(8,128)(2,1)S(1)} %get-tuple-element.21, bf16[64,256]{1,0:T(8,128)(2,1)S(1)} %get-tuple-element.22, ...), kind=kLoop, calls=%fused_computation.1 | loop fusion | flops 1310720 | bytes 721952 | tf_op jit(solution)/shard_map/jit(_where)/select_n | solution.py:113
  17.3 3.6 %all-to-all-start.1 = ((bf16[16,64,256]{2,1,0:T(8,128)(2,1)}), bf16[16,64,256]{2,1,0:T(8,128)(2,1)S(1)}, u32[]{:S(2)}, u32[]{:S(2)}) async-start(bf16[16,64,256]{2,1,0:T(8,128)(2,1)} %select_select_fusion), calls=%async_computation.1 | async-start | bytes 1048576 | tf_op jit(solution)/shard_map/all_to_all | solution.py:114
  20.9 0.1 dynamic-slice_bitcast_fusion.3
  21.0 0.1 select_reduce_fusion.1
  21.1 0.1 broadcast_select_fusion
  21.2 0.1 fusion
  21.3 0.1 select_n.109
  21.4 0.1 select_n.113
  21.4 0.6 %pad_maximum_fusion.1.bias_ref = f32[1,2048]{1,0:T(1,128)} fusion(f32[1,1024]{1,0:T(1,128)S(1)} %select_n.113, f32[1,1024]{1,0:T(1,128)S(1)} %select_n.109), kind=kLoop, calls=%fused_computation.14 | loop fusion | flops 2048 | bytes 16384 | tf_op jit(solution)/shard_map/concatenate | solution.py:138
  22.0 0.0 collective-permute-done
  22.0 0.8 %pad_maximum_fusion = bf16[16,64,256]{2,1,0:T(8,128)(2,1)} fusion(bf16[16,32,256]{2,1,0:T(8,128)(2,1)S(1)} %collective-permute-done, bf16[16,32,256]{2,1,0:T(8,128)(2,1)S(1)} %get-tuple-element.7), kind=kLoop, calls=%fused_computation | loop fusion | flops 1048576 | bytes 1048576 | tf_op jit(solution)/shard_map/concatenate | solution.py:129
  22.9 12.5 %all-to-all-done.1 = bf16[16,64,256]{2,1,0:T(8,128)(2,1)S(1)} async-done(((bf16[16,64,256]{2,1,0:T(8,128)(2,1)}), bf16[16,64,256]{2,1,0:T(8,128)(2,1)S(1)}, u32[]{:S(2)}, u32[]{:S(2)}) %all-to-all-start.1) | async-done | bytes 524320 | tf_op jit(solution)/shard_map/all_to_all | solution.py:114
  35.3 0.0 copy-start
  35.4 0.8 %copy-done = bf16[16,64,256]{2,1,0:T(8,128)(2,1)} copy-done((bf16[16,64,256]{2,1,0:T(8,128)(2,1)}, bf16[16,64,256]{2,1,0:T(8,128)(2,1)S(1)}, u32[]{:S(2)}) %copy-start) | copy-done | bytes 524312
  36.1 13.7 %shard_map.82 = bf16[384,1024]{1,0:T(8,128)(2,1)} custom-call(f32[1,2048]{1,0:T(1,128)} %pad_maximum_fusion.1.bias_ref, bf16[1024,256]{1,0:T(8,128)(2,1)} %bitcast.33, bf16[1024,256]{1,0:T(8,128)(2,1)} %bitcast.34, bf16[384,256]{1,0:T(8,128)(2,1)} %own_ref.1, bf16[384,1024]{1,0:T(8,128)(2,1)} %q_ref.1), custom_call_target="tpu_custom_call" | custom-call | flops 3825205248 | bytes 2826240 | tf_op jit(solution)/shard_map/pallas_call | solution.py:71
  (7 shorter events, 0.1 us)
Async XLA Ops:
  0.0 0.7 %copy-start.3 = (s32[48]{0:T(128)S(1)}, s32[48]{0:T(128)}, u32[]{:S(2)}) copy-start(s32[48]{0:T(128)} %param.13) | copy-start | bytes 580
  0.0 0.7 %copy-start.4 = (s32[1,16]{1,0:T(1,128)S(1)}, s32[1,16]{1,0:T(1,128)}, u32[]{:S(2)}) copy-start(s32[1,16]{1,0:T(1,128)} %param.12) | copy-start | bytes 196
  0.9 0.7 %copy-start.2 = (s32[1,16,64]{2,1,0:T(8,128)S(1)}, s32[1,16,64]{2,1,0:T(8,128)}, u32[]{:S(2)}) copy-start(s32[1,16,64]{2,1,0:T(8,128)} %param.15) | copy-start | bytes 12292
  2.4 13.7 %all-to-all-start = ((s32[16,1,65]{2,1,0:T(1,128)}), s32[16,1,65]{2,1,0:T(1,128)S(1)}, u32[]{:S(2)}, u32[]{:S(2)}) async-start(s32[16,1,65]{2,1,0:T(1,128)} %bitcast.7), calls=%async_computation | async-start | bytes 16384 | tf_op jit(solution)/shard_map/all_to_all | solution.py:106
  9.8 2.9 %copy-start.1 = (bf16[3,128,256]{2,1,0:T(8,128)(2,1)S(1)}, bf16[3,128,256]{2,1,0:T(8,128)(2,1)}, u32[]{:S(2)}) copy-start(bf16[3,128,256]{2,1,0:T(8,128)(2,1)} %param.10) | copy-start | bytes 589828
  10.9 1.6 %copy-start.5 = (s32[48]{0:T(128)S(1)}, s32[48]{0:T(128)}, u32[]{:S(2)}) copy-start(s32[48]{0:T(128)} %param.14) | copy-start | bytes 580
  10.9 11.1 %collective-permute-start = (bf16[16,32,256]{2,1,0:T(8,128)(2,1)S(1)}, bf16[16,32,256]{2,1,0:T(8,128)(2,1)S(1)}, u32[]{:S(2)}, u32[]{:S(2)}) collective-permute-start(bf16[16,32,256]{2,1,0:T(8,128)(2,1)S(1)} %get-tuple-element.8), channel_id=1, source_target_pairs={{0,16},{16,0},{1,17},{17,1},{2,18},{18,2},{3,19},{19,3},{4,20},{20... | collective-permute-start | bytes 786440 | tf_op jit(solution)/shard_map/ppermute | solution.py:126
  17.3 18.0 %all-to-all-start.1 = ((bf16[16,64,256]{2,1,0:T(8,128)(2,1)}), bf16[16,64,256]{2,1,0:T(8,128)(2,1)S(1)}, u32[]{:S(2)}, u32[]{:S(2)}) async-start(bf16[16,64,256]{2,1,0:T(8,128)(2,1)} %select_select_fusion), calls=%async_computation.1 | async-start | bytes 1048576 | tf_op jit(solution)/shard_map/all_to_all | solution.py:114
  35.3 0.8 %copy-start = (bf16[16,64,256]{2,1,0:T(8,128)(2,1)}, bf16[16,64,256]{2,1,0:T(8,128)(2,1)S(1)}, u32[]{:S(2)}) copy-start(bf16[16,64,256]{2,1,0:T(8,128)(2,1)S(1)} %all-to-all-done.1) | copy-start | bytes 1572868

commit v8 on v7

--- a/solution.py
+++ b/solution.py
@@ -19,21 +19,31 @@
     return jnp.sum(jnp.where(hits, table, 0), axis=-1)
 
 
-def attend_kernel(bias_ref, kept_ref, fresh_ref, own_ref, q_ref, out_ref):
+def early_kernel(bias_ref, fresh_ref, own_ref, q_ref, sa_ref):
+    rows = q_ref.shape[0]
+    nt = (((1,), (1,)), ((), ()))
+    split = fresh_ref.shape[0]
+    for g in range(q_ref.shape[1] // HD):
+        for t in range(rows // TR):
+            qt = q_ref[t * TR:(t + 1) * TR, g * HD:(g + 1) * HD]
+            sf = lax.dot_general(qt, fresh_ref[:, :HD], nt, preferred_element_type=jnp.float32)
+            sa_ref[g, t * TR:(t + 1) * TR, :split] = sf + bias_ref[...]
+            so = lax.dot_general(qt, own_ref[:, :HD], nt, preferred_element_type=jnp.float32)
+            row = lax.broadcasted_iota(jnp.int32, so.shape, 0) + t * TR
+            col = lax.broadcasted_iota(jnp.int32, so.shape, 1)
+            sa_ref[g, t * TR:(t + 1) * TR, split:] = jnp.where(col <= row, so, -jnp.inf)
+
+
+def attend_kernel(bias_ref, kept_ref, fresh_ref, own_ref, q_ref, sa_ref, out_ref):
     rows = q_ref.shape[0]
     rate = HD ** (-0.5) * 1.4426950408889634
     nt = (((1,), (1,)), ((), ()))
+    split = fresh_ref.shape[0]
 
     def scores(g, t):
         qt = q_ref[t * TR:(t + 1) * TR, g * HD:(g + 1) * HD]
         sk = lax.dot_general(qt, kept_ref[:, :HD], nt, preferred_element_type=jnp.float32)
-        sf = lax.dot_general(qt, fresh_ref[:, :HD], nt, preferred_element_type=jnp.float32)
-        s1 = jnp.concatenate([sk, sf], 1) + bias_ref[...]
-        kk = (t + 1) * TR
-        s2 = lax.dot_general(qt, own_ref[:kk, :HD], nt, preferred_element_type=jnp.float32)
-        row = lax.broadcasted_iota(jnp.int32, (TR, kk), 0) + t * TR
-        col = lax.broadcasted_iota(jnp.int32, (TR, kk), 1)
-        return s1, jnp.where(col <= row, s2, -jnp.inf)
+        return sk + bias_ref[...], sa_ref[g, t * TR:(t + 1) * TR, :]
 
     def finish(g, t, s1, s2):
         kk = (t + 1) * TR
@@ -43,10 +53,9 @@
         inv = 1.0 / (jnp.sum(e1, axis=1, keepdims=True) + jnp.sum(e2, axis=1, keepdims=True))
         w1 = (e1 * inv).astype(jnp.bfloat16)
         w2 = (e2 * inv).astype(jnp.bfloat16)
-        split = kept_ref.shape[0]
-        mixed = jnp.dot(w1[:, :split], kept_ref[:, HD:], preferred_element_type=jnp.float32)
-        mixed = mixed + jnp.dot(w1[:, split:], fresh_ref[:, HD:], preferred_element_type=jnp.float32)
-        mixed = mixed + jnp.dot(w2, own_ref[:kk, HD:], preferred_element_type=jnp.float32)
+        mixed = jnp.dot(w1, kept_ref[:, HD:], preferred_element_type=jnp.float32)
+        mixed = mixed + jnp.dot(w2[:, :split], fresh_ref[:, HD:], preferred_element_type=jnp.float32)
+        mixed = mixed + jnp.dot(w2[:, split:split + kk], own_ref[:kk, HD:], preferred_element_type=jnp.float32)
         out_ref[t * TR:(t + 1) * TR, g * HD:(g + 1) * HD] = mixed.astype(out_ref.dtype)
 
     tiles = [(g, t) for g in range(q_ref.shape[1] // HD) for t in range(rows // TR)]
@@ -57,26 +66,54 @@
         finish(*tile, *ready[k])
 
 
-def attend(bias, kept, fresh, own_kv, queries):
+def full(shape):
+    return pl.BlockSpec(shape, lambda g: (0,) * len(shape))
+
+
+def early(fresh_bias, fresh, own_kv, queries):
+    rows, width = queries.shape
+    heads = width // HD
+    step = PAIR if heads % PAIR == 0 else 1
+    keys = fresh.shape[0] + rows
+    block = (step, rows, keys)
+    return pl.pallas_call(
+        early_kernel,
+        grid=(heads // step,),
+        in_specs=[
+            full(fresh_bias.shape),
+            full(fresh.shape),
+            full(own_kv.shape),
+            pl.BlockSpec((rows, step * HD), lambda g: (0, g)),
+        ],
+        out_specs=pl.BlockSpec(block, lambda g: (g, 0, 0)),
+        out_shape=jax.ShapeDtypeStruct((heads, rows, keys), jnp.float32),
+        compiler_params=pltpu.CompilerParams(dimension_semantics=("arbitrary",)),
+        cost_estimate=pl.CostEstimate(
+            flops=2 * heads * rows * keys * HD,
+            bytes_accessed=2 * (fresh.size + own_kv.size + queries.size) + 4 * heads * rows * keys,
+            transcendentals=0,
+        ),
+    )(fresh_bias, fresh, own_kv, queries)
+
+
+def attend(kept_bias, kept, fresh, own_kv, queries, partial):
     rows, width = queries.shape
     heads = width // HD
     step = PAIR if heads % PAIR == 0 else 1
     keys = kept.shape[0] + fresh.shape[0] + rows
-    flops = 4 * heads * rows * keys * HD
-    bytes_accessed = 2 * (kept.size + fresh.size + own_kv.size + 2 * queries.size) + 4 * bias.size
-
-    def full(shape):
-        return pl.BlockSpec(shape, lambda g: (0,) * len(shape))
+    flops = 2 * heads * rows * (keys + kept.shape[0]) * HD
+    bytes_accessed = 2 * (kept.size + fresh.size + own_kv.size + 2 * queries.size) + 4 * partial.size
 
     return pl.pallas_call(
         attend_kernel,
         grid=(heads // step,),
         in_specs=[
-            full(bias.shape),
+            full(kept_bias.shape),
             full(kept.shape),
             full(fresh.shape),
             full(own_kv.shape),
             pl.BlockSpec((rows, step * HD), lambda g: (0, g)),
+            pl.BlockSpec((step,) + partial.shape[1:], lambda g: (g, 0, 0)),
         ],
         out_specs=pl.BlockSpec((rows, step * HD), lambda g: (0, g)),
         out_shape=jax.ShapeDtypeStruct(queries.shape, queries.dtype),
@@ -84,7 +121,7 @@
         cost_estimate=pl.CostEstimate(
             flops=flops, bytes_accessed=bytes_accessed, transcendentals=heads * rows * keys
         ),
-    )(bias, kept, fresh, own_kv, queries)
+    )(kept_bias, kept, fresh, own_kv, queries, partial)
 
 
 def per_device(
@@ -135,9 +172,10 @@
     kept_bias = jnp.where(slot_of[:, :, None], kept_bias[None], 0.0).sum(1)
     kept_bias = jnp.where(jnp.any(slot_of, 1)[:, None], kept_bias, -jnp.inf)
     fresh_bias = jnp.where(pos < limits[:, None], 0.0, -jnp.inf).astype(jnp.float32)
-    bias = jnp.concatenate([kept_bias.reshape(1, -1), fresh_bias.reshape(1, -1)], 1)
+    fresh = fresh.reshape(-1, fresh.shape[2])
+    partial = early(fresh_bias.reshape(1, -1), fresh, own_kv, queries)
     kept = recv.reshape(-1, recv.shape[2])
-    return attend(bias, kept, fresh.reshape(-1, fresh.shape[2]), own_kv, queries)
+    return attend(kept_bias.reshape(1, -1), kept, fresh, own_kv, queries, partial)
 
 
 def solution(mesh):

time: 50.1 us -> 53.1 us (1.060)
  waiting for transfers between devices: 15.4 us -> 3.33 us
  Pallas kernels: 13.7 us -> 23.8 us
  other arithmetic: 4.33 us -> 6.45 us
  local copies, waits for them, and re-layouts: 3.76 us -> 5.48 us
  starting transfers between devices: 12.5 us -> 13.5 us
    all_to_all x1, waiting for transfers between devices: 12.5 us -> 1.85 us  [per_device(): recv = lax.all_to_all(send, 'seq', 0, 0, tiled=True)]
    pallas_call x1 -> x2, Pallas kernels: 13.7 us -> 23.8 us  [the longest x1 15.3 us: attend(): pl.pallas_call(attend_kernel, grid=(heads // step,), in_specs=[full(kept_...]
    all_to_all x1, waiting for transfers between devices: 2.91 us -> 1.47 us  [per_device(): asked = lax.all_to_all(request, 'seq', 0, 0, tiled=True)]
    reduce_sum x2, other arithmetic: 0.36 us -> 1.69 us  [lookup(): return jnp.sum(jnp.where(hits, table, 0), axis=-1)]
    unnamed x15 -> x5, local copies, waits for them, and re-layouts: 1.98 us -> 0.85 us
    reshape x1, local copies, waits for them, and re-layouts: 0.08 us -> 1 us  [per_device(): halves = library.reshape(per_owner, -1, 2, library.shape[2])]
    all_to_all x1, starting transfers between devices: 3.57 us -> 4.49 us  [per_device(): recv = lax.all_to_all(send, 'seq', 0, 0, tiled=True)]
    dynamic_slice x1, local copies, waits for them, and re-layouts: 0.08 us -> 0.85 us  [per_device(): places = [lax.dynamic_slice_in_dim(pos_local, me * tokens, tokens, 1)]]
  transfers between devices with their start and end apart: 3 -> 3, of which waited for: 2 -> 2; matrix products, arithmetic and copies ran while one was open for 10% -> 16% of each run, Pallas kernels for 0% -> 16%
where the time goes in v8:
time: 53.1 us; the launch traced here: 52.6 us
  Pallas kernels  23.8 us (45%)
  starting transfers between devices  13.5 us (25%)
  other arithmetic  6.45 us (12%)
  local copies, waits for them, and re-layouts  5.48 us (10%)
  waiting for transfers between devices  3.33 us (6%)
    pallas_call x1, Pallas kernels, attend(): pl.pallas_call(attend_kernel, grid=(heads // step,), in_specs=[full(kept_...  15.3 us
    pallas_call x1, Pallas kernels, early(): pl.pallas_call(early_kernel, grid=(heads // step,), in_specs=[full(fresh_...  8.53 us
    all_to_all x1, starting transfers between devices, per_device(): asked = lax.all_to_all(request, 'seq', 0, 0, tiled=True)  7.39 us
    all_to_all x1, starting transfers between devices, per_device(): recv = lax.all_to_all(send, 'seq', 0, 0, tiled=True)  4.49 us
    all_to_all x1, waiting for transfers between devices, per_device(): recv = lax.all_to_all(send, 'seq', 0, 0, tiled=True)  1.85 us
    reduce_sum x2, other arithmetic, lookup(): return jnp.sum(jnp.where(hits, table, 0), axis=-1)  1.69 us
    ppermute x1, starting transfers between devices, per_device(): pieces.append(lax.ppermute(piece, 'kvh', pairs))  1.59 us
    all_to_all x1, waiting for transfers between devices, per_device(): asked = lax.all_to_all(request, 'seq', 0, 0, tiled=True)  1.47 us
  transfers between devices with their start and end apart: 3, of which 2 were waited for; matrix products, arithmetic and copies ran while one was open for 16% of the time, Pallas kernels for 16%

profile of v8, /device:TPU:0, one launch (start us, length us, event | category | flops | bytes accessed | tf_op | source)
XLA Modules:
  0.0 52.6 jit_solution(4275563554418566194)
XLA Ops:
  0.0 0.9 %select_reduce_fusion.3 = s32[16]{0:T(128)S(1)} fusion(s32[48]{0:T(128)} %param.13, s32[16]{0:T(128)} %bitcast.38), kind=kLoop, calls=%fused_computation.23 | loop fusion | flops 2288 | bytes 320 | tf_op jit(solution)/shard_map/reduce_sum | solution.py:19
  0.9 0.1 fusion.1
  1.0 0.1 copy.17
  1.1 0.7 %bitcast_subtract_fusion = s32[16,64]{1,0:T(8,128)S(1)} fusion(s32[1,16,64]{2,1,0:T(8,128)} %param.15, s32[64]{0:T(128)S(1)} %get-tuple-element.19), kind=kLoop, calls=%fused_computation.15 | loop fusion | flops 1024 | bytes 8448 | tf_op jit(solution)/shard_map/sub | solution.py:138
  1.8 0.1 pad_add_fusion
  1.9 0.7 %select_reduce_fusion = s32[16,65]{1,0:T(8,128)} fusion(s32[16,65]{1,0:T(8,128)S(1)} %pad_add_fusion, pred[16,16]{1,0:T(8,128)(4,1)S(1)} %get-tuple-element.18), kind=kLoop, calls=%fused_computation.4 | loop fusion | flops 32240 | bytes 8576 | tf_op jit(solution)/shard_map/reduce_sum | solution.py:142
  2.6 7.4 %all-to-all-start = ((s32[16,1,65]{2,1,0:T(1,128)}), s32[16,1,65]{2,1,0:T(1,128)S(1)}, u32[]{:S(2)}, u32[]{:S(2)}) async-start(s32[16,1,65]{2,1,0:T(1,128)} %bitcast.5), calls=%async_computation | async-start | bytes 16384 | tf_op jit(solution)/shard_map/all_to_all | solution.py:143
  10.0 1.1 %dynamic-slice_bitcast_fusion.1 = (bf16[16,32,256]{2,1,0:T(8,128)(2,1)S(1)}, bf16[16,32,256]{2,1,0:T(8,128)(2,1)S(1)}) fusion(bf16[1,16,32,512]{3,2,1,0:T(8,128)(2,1)} %param.11, s32[]{:T(128)S(6)} %select_n.117, s32[]{:T(128)S(6)} %select_n.118), kind=kLoop, calls=%fused_computation.3 | loop fusion | bytes 1048584 | tf_op jit(solution)/shard_map/dynamic_slice | solution.py:157
  11.1 1.6 %collective-permute-start = (bf16[16,32,256]{2,1,0:T(8,128)(2,1)S(1)}, bf16[16,32,256]{2,1,0:T(8,128)(2,1)S(1)}, u32[]{:S(2)}, u32[]{:S(2)}) collective-permute-start(bf16[16,32,256]{2,1,0:T(8,128)(2,1)S(1)} %get-tuple-element.8), channel_id=1, source_target_pairs={{0,16},{16,0},{1,17},{17,1},{2,18},{18,2},{3,19},{19,3},{4,20},{20... | collective-permute-start | bytes 786440 | tf_op jit(solution)/shard_map/ppermute | solution.py:163
  12.7 1.0 %reshape.206 = bf16[3,64,2,256]{3,2,1,0:T(2,128)(2,1)S(1)} reshape(bf16[3,128,256]{2,1,0:T(8,128)(2,1)} %param.10) | data formatting | bytes 393216 | tf_op jit(solution)/shard_map/reshape | solution.py:146
  13.7 0.3 fusion.2
  14.0 0.8 %select_reduce_fusion.2 = s32[16]{0:T(128)S(1)} fusion(s32[48]{0:T(128)} %param.14, s32[16]{0:T(128)S(1)} %select_reduce_fusion.3), kind=kLoop, calls=%fused_computation.19 | loop fusion | flops 2288 | bytes 320 | tf_op jit(solution)/shard_map/reduce_sum | solution.py:19
  14.8 1.5 %all-to-all-done = s32[16,1,65]{2,1,0:T(1,128)S(1)} async-done(((s32[16,1,65]{2,1,0:T(1,128)}), s32[16,1,65]{2,1,0:T(1,128)S(1)}, u32[]{:S(2)}, u32[]{:S(2)}) %all-to-all-start) | async-done | bytes 4192 | tf_op jit(solution)/shard_map/all_to_all | solution.py:143
  16.3 0.1 compare_reduce_fusion.1
  16.4 0.1 slice_compare_fusion
  16.5 1.0 %select_select_fusion = bf16[16,64,256]{2,1,0:T(8,128)(2,1)} fusion(pred[16]{0:T(512)(128)(4,1)S(1)} %get-tuple-element.6, pred[16]{0:T(512)(128)(4,1)S(1)} %get-tuple-element.5, pred[16,64]{1,0:T(8,128)(4,1)S(1)} %slice_compare_fusion, bf16[64,256]{1,0:T(8,128)(2,1)S(1)} %get-tuple-element.21, bf16[64,256]{1,0:T(8,128)(2,1)S(1)} %get-tuple-element.22, ...), kind=kLoop, calls=%fused_computation.1 | loop fusion | flops 1310720 | bytes 721952 | tf_op jit(solution)/shard_map/jit(_where)/select_n | solution.py:150
  17.6 4.5 %all-to-all-start.1 = ((bf16[16,64,256]{2,1,0:T(8,128)(2,1)}), bf16[16,64,256]{2,1,0:T(8,128)(2,1)S(1)}, u32[]{:S(2)}, u32[]{:S(2)}) async-start(bf16[16,64,256]{2,1,0:T(8,128)(2,1)} %select_select_fusion), calls=%async_computation.1 | async-start | bytes 1048576 | tf_op jit(solution)/shard_map/all_to_all | solution.py:151
  22.1 0.8 %select_bitcast_fusion = f32[16,64]{1,0:T(8,128)S(1)} fusion(s32[1,16,64]{2,1,0:T(8,128)} %param.15, s32[16]{0:T(128)S(1)} %select_reduce_fusion.2, s32[64]{0:T(128)S(1)} %get-tuple-element.19, s32[64]{0:T(128)S(1)} %get-tuple-element.20), kind=kLoop, calls=%fused_computation.18 | loop fusion | flops 4096 | bytes 8768 | tf_op jit(solution)/shard_map/jit(_where)/broadcast_in_dim | solution.py:172
  22.8 0.1 select_reduce_fusion.1
  23.0 0.1 broadcast_select_fusion
  23.0 0.8 %dynamic-slice_bitcast_fusion.3 = (s32[16,32]{1,0:T(8,128)S(1)}, s32[16,32]{1,0:T(8,128)S(1)}) fusion(s32[1,16,64]{2,1,0:T(8,128)} %param.15, s32[]{:T(128)S(6)} %select_n.119, s32[]{:T(128)S(6)} %select_n.120), kind=kLoop, calls=%fused_computation.17 | loop fusion | bytes 8200 | tf_op jit(solution)/shard_map/dynamic_slice | solution.py:158
  23.9 0.7 %select_n.109.bias_ref = f32[1,1024]{1,0:T(1,128)} reshape(f32[16,64]{1,0:T(8,128)S(1)} %broadcast_select_fusion) | data formatting | bytes 8192 | tf_op jit(solution)/shard_map/jit(_where)/select_n | solution.py:173
  24.5 0.1 fusion
  24.6 0.7 %select_n.122.bias_ref = f32[1,1024]{1,0:T(1,128)} reshape(f32[16,64]{1,0:T(8,128)S(1)} %fusion) | data formatting | bytes 8192 | tf_op jit(solution)/shard_map/jit(_where)/select_n | solution.py:174
  25.3 0.0 collective-permute-done
  25.3 0.8 %pad_maximum_fusion = bf16[16,64,256]{2,1,0:T(8,128)(2,1)} fusion(bf16[16,32,256]{2,1,0:T(8,128)(2,1)S(1)} %collective-permute-done, bf16[16,32,256]{2,1,0:T(8,128)(2,1)S(1)} %get-tuple-element.7), kind=kLoop, calls=%fused_computation | loop fusion | flops 1048576 | bytes 1048576 | tf_op jit(solution)/shard_map/concatenate | solution.py:166
  26.1 8.5 %shard_map.82.sa_ref = f32[8,384,1408]{2,1,0:T(8,128)} custom-call(f32[1,1024]{1,0:T(1,128)} %select_n.122.bias_ref, bf16[1024,256]{1,0:T(8,128)(2,1)} %bitcast.33, bf16[384,256]{1,0:T(8,128)(2,1)} %own_ref.3, bf16[384,1024]{1,0:T(8,128)(2,1)} %q_ref.3), custom_call_target="tpu_custom_call" | custom-call | flops 1107296256 | bytes 18808832 | tf_op jit(solution)/shard_map/pallas_call | solution.py:79
  34.7 1.9 %all-to-all-done.1 = bf16[16,64,256]{2,1,0:T(8,128)(2,1)S(1)} async-done(((bf16[16,64,256]{2,1,0:T(8,128)(2,1)}), bf16[16,64,256]{2,1,0:T(8,128)(2,1)S(1)}, u32[]{:S(2)}, u32[]{:S(2)}) %all-to-all-start.1) | async-done | bytes 524320 | tf_op jit(solution)/shard_map/all_to_all | solution.py:151
  36.5 0.0 copy-start
  36.5 0.8 %copy-done = bf16[16,64,256]{2,1,0:T(8,128)(2,1)} copy-done((bf16[16,64,256]{2,1,0:T(8,128)(2,1)}, bf16[16,64,256]{2,1,0:T(8,128)(2,1)S(1)}, u32[]{:S(2)}) %copy-start) | copy-done | bytes 524312
  37.3 15.3 %shard_map.83 = bf16[384,1024]{1,0:T(8,128)(2,1)} custom-call(f32[1,1024]{1,0:T(1,128)} %select_n.109.bias_ref, bf16[1024,256]{1,0:T(8,128)(2,1)} %bitcast.35, bf16[1024,256]{1,0:T(8,128)(2,1)} %bitcast.34, bf16[384,256]{1,0:T(8,128)(2,1)} %own_ref.3, bf16[384,1024]{1,0:T(8,128)(2,1)} %q_ref.3, f32[8,384,1408]{2,1,0:T(8,128)} %shard_map.82.sa_ref), custom_call_target="tpu_custom_call" | custom-call | flops 2717908992 | bytes 20119552 | tf_op jit(solution)/shard_map/pallas_call | solution.py:107
  (6 shorter events, 0.1 us)
Async XLA Ops:
  2.6 13.7 %all-to-all-start = ((s32[16,1,65]{2,1,0:T(1,128)}), s32[16,1,65]{2,1,0:T(1,128)S(1)}, u32[]{:S(2)}, u32[]{:S(2)}) async-start(s32[16,1,65]{2,1,0:T(1,128)} %bitcast.5), calls=%async_computation | async-start | bytes 16384 | tf_op jit(solution)/shard_map/all_to_all | solution.py:143
  11.1 14.2 %collective-permute-start = (bf16[16,32,256]{2,1,0:T(8,128)(2,1)S(1)}, bf16[16,32,256]{2,1,0:T(8,128)(2,1)S(1)}, u32[]{:S(2)}, u32[]{:S(2)}) collective-permute-start(bf16[16,32,256]{2,1,0:T(8,128)(2,1)S(1)} %get-tuple-element.8), channel_id=1, source_target_pairs={{0,16},{16,0},{1,17},{17,1},{2,18},{18,2},{3,19},{19,3},{4,20},{20... | collective-permute-start | bytes 786440 | tf_op jit(solution)/shard_map/ppermute | solution.py:163
  17.6 19.0 %all-to-all-start.1 = ((bf16[16,64,256]{2,1,0:T(8,128)(2,1)}), bf16[16,64,256]{2,1,0:T(8,128)(2,1)S(1)}, u32[]{:S(2)}, u32[]{:S(2)}) async-start(bf16[16,64,256]{2,1,0:T(8,128)(2,1)} %select_select_fusion), calls=%async_computation.1 | async-start | bytes 1048576 | tf_op jit(solution)/shard_map/all_to_all | solution.py:151
  36.5 0.8 %copy-start = (bf16[16,64,256]{2,1,0:T(8,128)(2,1)}, bf16[16,64,256]{2,1,0:T(8,128)(2,1)S(1)}, u32[]{:S(2)}) copy-start(bf16[16,64,256]{2,1,0:T(8,128)(2,1)S(1)} %all-to-all-done.1) | copy-start | bytes 1572868

commit v9 on v7

--- a/solution.py
+++ b/solution.py
@@ -91,15 +91,16 @@
     n_seq, n_kvh, queries, own_kv, library, fresh_kv, retrieved, stretch_slot, stretch_len, recompute_pos
 ):
     per_owner = library.shape[0]
-    wanted = lookup(stretch_slot, retrieved[0])
+    wanted = jnp.take(stretch_slot, retrieved[0], mode="clip")
     owner = wanted // per_owner
-    local = wanted % per_owner
-    limits = lookup(stretch_len, wanted)
+    limits = jnp.take(stretch_len, wanted, mode="clip")
 
     pos_local = recompute_pos[0]
     pair = jnp.arange(pos_local.shape[1], dtype=jnp.int32)
     odd_taken = pos_local - 2 * pair[None, :]
-    payload = jnp.concatenate([local[:, None], odd_taken], 1)
+    column = jnp.arange(pos_local.shape[1] + 1, dtype=jnp.int32)
+    shifted = jnp.pad(pos_local, ((0, 0), (1, 0))) - 2 * column[None, :] + 2
+    payload = jnp.where(column[None, :] == 0, (wanted - owner * per_owner)[:, None], shifted)
     devices = jnp.arange(n_seq, dtype=jnp.int32)
     hits = owner[None, :, None] == devices[:, None, None]
     request = jnp.sum(jnp.where(hits, payload[None], 0), axis=1)

time: 50.1 us -> 50.7 us (1.012)
    gather x0 -> x2, local copies, waits for them, and re-layouts: none -> 1.31 us  [the longest x1 0.66 us: per_device(): wanted = jnp.take(stretch_slot, retrieved[0], mode='clip')]
    dynamic_slice x1, local copies, waits for them, and re-layouts: 1.11 us -> 0.04 us  [per_device(): pieces = [lax.dynamic_slice_in_dim(fresh_local, me * width, width, 2)]]
    gather x0 -> x2, other arithmetic: none -> 0.73 us  [the longest x1 0.72 us: per_device(): wanted = jnp.take(stretch_slot, retrieved[0], mode='clip')]
  transfers between devices with their start and end apart: 3 -> 3, of which waited for: 2 -> 2; matrix products, arithmetic and copies ran while one was open for 10% -> 9% of each run, Pallas kernels for 0% -> 0%
where the time goes in v9:
time: 50.7 us; the launch traced here: 50.3 us
  waiting for transfers between devices  15.6 us (31%)
  Pallas kernels  13.7 us (27%)
  starting transfers between devices  12.5 us (25%)
  other arithmetic  4.68 us (9%)
  local copies, waits for them, and re-layouts  3.72 us (7%)
    pallas_call x1, Pallas kernels, attend(): pl.pallas_call(attend_kernel, grid=(heads // step,), in_specs=[full(bias....  13.7 us
    all_to_all x1, waiting for transfers between devices, per_device(): recv = lax.all_to_all(send, 'seq', 0, 0, tiled=True)  12.5 us
    all_to_all x1, starting transfers between devices, per_device(): asked = lax.all_to_all(request, 'seq', 0, 0, tiled=True)  7.39 us
    all_to_all x1, starting transfers between devices, per_device(): recv = lax.all_to_all(send, 'seq', 0, 0, tiled=True)  3.57 us
    all_to_all x1, waiting for transfers between devices, per_device(): asked = lax.all_to_all(request, 'seq', 0, 0, tiled=True)  3.1 us
    unnamed x15, local copies, waits for them, and re-layouts  1.77 us
    ppermute x1, starting transfers between devices, per_device(): pieces.append(lax.ppermute(piece, 'kvh', pairs))  1.58 us
    select_n x1, other arithmetic, per_device(): send = kept if send is None else jnp.where(which == k, kept, send)  1.05 us
  transfers between devices with their start and end apart: 3, of which 2 were waited for; matrix products, arithmetic and copies ran while one was open for 9% of the time, Pallas kernels for 0%

profile of v9, /device:TPU:0, one launch (start us, length us, event | category | flops | bytes accessed | tf_op | source)
XLA Modules:
  0.0 50.3 jit_solution(1695394344091111155)
XLA Ops:
  0.0 0.0 copy-start
  0.0 0.0 copy-start.2
  0.0 0.7 %pad_clamp_fusion.1 = s32[1024]{0:T(1024)S(1)} fusion(s32[16]{0:T(128)} %bitcast.35), kind=kLoop, calls=%fused_computation.27 | loop fusion | flops 1024 | bytes 4160 | tf_op jit(solution)/shard_map/jit(_take)/gather | solution.py:94
  0.7 0.0 copy-done
  0.7 0.7 %gather_fusion = s32[16]{0:T(128)S(1)} fusion(s32[48]{0:T(128)S(1)} %copy-done, s32[1024]{0:T(1024)S(1)} %pad_clamp_fusion.1), kind=kCustom, calls=%fused_computation | custom fusion | bytes 192 | tf_op jit(solution)/shard_map/jit(_take)/gather | solution.py:94
  1.4 0.0 copy-start.5
  1.4 0.1 fusion.1
  1.5 0.6 %copy-done.5 = s32[1,16,64]{2,1,0:T(8,128)S(1)} copy-done((s32[1,16,64]{2,1,0:T(8,128)S(1)}, s32[1,16,64]{2,1,0:T(8,128)}, u32[]{:S(2)}) %copy-start.5) | copy-done | bytes 4120
  2.1 0.1 add_select_fusion
  2.2 0.7 %select_reduce_fusion = s32[16,65]{1,0:T(8,128)} fusion(s32[16,65]{1,0:T(8,128)S(1)} %add_select_fusion, pred[16,16]{1,0:T(8,128)(4,1)S(1)} %get-tuple-element.20), kind=kLoop, calls=%fused_computation.6 | loop fusion | flops 32240 | bytes 8576 | tf_op jit(solution)/shard_map/reduce_sum | solution.py:106
  2.9 7.4 %all-to-all-start = ((s32[16,1,65]{2,1,0:T(1,128)}), s32[16,1,65]{2,1,0:T(1,128)S(1)}, u32[]{:S(2)}, u32[]{:S(2)}) async-start(s32[16,1,65]{2,1,0:T(1,128)} %bitcast.6), calls=%async_computation | async-start | bytes 16384 | tf_op jit(solution)/shard_map/all_to_all | solution.py:107
  10.3 0.0 copy-done.2
  10.3 0.0 copy-start.4
  10.4 1.6 %collective-permute-start = (bf16[16,32,256]{2,1,0:T(8,128)(2,1)S(1)}, bf16[16,32,256]{2,1,0:T(8,128)(2,1)S(1)}, u32[]{:S(2)}, u32[]{:S(2)}) collective-permute-start(bf16[16,32,256]{2,1,0:T(8,128)(2,1)S(1)} %get-tuple-element.10), channel_id=1, source_target_pairs={{0,16},{16,0},{1,17},{17,1},{2,18},{18,2},{3,19},{19,3},{4,20},{20... | collective-permute-start | bytes 786440 | tf_op jit(solution)/shard_map/ppermute | solution.py:127
  12.0 0.0 copy-done.4
  12.0 0.1 reshape.203
  12.1 0.0 copy-start.1
  12.1 0.3 fusion.2
  12.4 0.4 copy-done.1
  12.7 0.7 %gather_fusion.1 = s32[16]{0:T(128)S(1)} fusion(s32[48]{0:T(128)S(1)} %copy-done.1, s32[1024]{0:T(1024)S(1)} %pad_clamp_fusion), kind=kCustom, calls=%fused_computation.1 | custom fusion | bytes 192 | tf_op jit(solution)/shard_map/jit(_take)/gather | solution.py:96
  13.5 0.1 select_bitcast_fusion
  13.5 3.1 %all-to-all-done = s32[16,1,65]{2,1,0:T(1,128)S(1)} async-done(((s32[16,1,65]{2,1,0:T(1,128)}), s32[16,1,65]{2,1,0:T(1,128)S(1)}, u32[]{:S(2)}, u32[]{:S(2)}) %all-to-all-start) | async-done | bytes 4192 | tf_op jit(solution)/shard_map/all_to_all | solution.py:107
  16.6 0.1 compare_reduce_fusion.1
  16.7 0.1 slice_compare_fusion
  16.8 1.0 %select_select_fusion = bf16[16,64,256]{2,1,0:T(8,128)(2,1)} fusion(pred[16]{0:T(512)(128)(4,1)S(1)} %get-tuple-element.6, pred[16]{0:T(512)(128)(4,1)S(1)} %get-tuple-element.5, pred[16,64]{1,0:T(8,128)(4,1)S(1)} %slice_compare_fusion, bf16[64,256]{1,0:T(8,128)(2,1)S(1)} %get-tuple-element.23, bf16[64,256]{1,0:T(8,128)(2,1)S(1)} %get-tuple-element.24, ...), kind=kLoop, calls=%fused_computation.3 | loop fusion | flops 1310720 | bytes 721952 | tf_op jit(solution)/shard_map/jit(_where)/select_n | solution.py:114
  17.9 3.6 %all-to-all-start.1 = ((bf16[16,64,256]{2,1,0:T(8,128)(2,1)}), bf16[16,64,256]{2,1,0:T(8,128)(2,1)S(1)}, u32[]{:S(2)}, u32[]{:S(2)}) async-start(bf16[16,64,256]{2,1,0:T(8,128)(2,1)} %select_select_fusion), calls=%async_computation.1 | async-start | bytes 1048576 | tf_op jit(solution)/shard_map/all_to_all | solution.py:115
  21.5 0.1 dynamic-slice_bitcast_fusion.3
  21.5 0.1 select_reduce_fusion.1
  21.7 0.1 broadcast_select_fusion
  21.7 0.1 fusion
  21.8 0.1 select_n.94
  21.9 0.1 select_n.98
  22.0 0.6 %pad_maximum_fusion.1.bias_ref = f32[1,2048]{1,0:T(1,128)} fusion(f32[1,1024]{1,0:T(1,128)S(1)} %select_n.98, f32[1,1024]{1,0:T(1,128)S(1)} %select_n.94), kind=kLoop, calls=%fused_computation.16 | loop fusion | flops 2048 | bytes 16384 | tf_op jit(solution)/shard_map/concatenate | solution.py:139
  22.6 0.0 collective-permute-done
  22.6 0.8 %pad_maximum_fusion = bf16[16,64,256]{2,1,0:T(8,128)(2,1)} fusion(bf16[16,32,256]{2,1,0:T(8,128)(2,1)S(1)} %collective-permute-done, bf16[16,32,256]{2,1,0:T(8,128)(2,1)S(1)} %get-tuple-element.9), kind=kLoop, calls=%fused_computation.2 | loop fusion | flops 1048576 | bytes 1048576 | tf_op jit(solution)/shard_map/concatenate | solution.py:130
  23.4 12.5 %all-to-all-done.1 = bf16[16,64,256]{2,1,0:T(8,128)(2,1)S(1)} async-done(((bf16[16,64,256]{2,1,0:T(8,128)(2,1)}), bf16[16,64,256]{2,1,0:T(8,128)(2,1)S(1)}, u32[]{:S(2)}, u32[]{:S(2)}) %all-to-all-start.1) | async-done | bytes 524320 | tf_op jit(solution)/shard_map/all_to_all | solution.py:115
  35.9 0.0 copy-start.3
  35.9 0.8 %copy-done.3 = bf16[16,64,256]{2,1,0:T(8,128)(2,1)} copy-done((bf16[16,64,256]{2,1,0:T(8,128)(2,1)}, bf16[16,64,256]{2,1,0:T(8,128)(2,1)S(1)}, u32[]{:S(2)}) %copy-start.3) | copy-done | bytes 524312
  36.7 13.7 %shard_map.82 = bf16[384,1024]{1,0:T(8,128)(2,1)} custom-call(f32[1,2048]{1,0:T(1,128)} %pad_maximum_fusion.1.bias_ref, bf16[1024,256]{1,0:T(8,128)(2,1)} %bitcast.30, bf16[1024,256]{1,0:T(8,128)(2,1)} %bitcast.31, bf16[384,256]{1,0:T(8,128)(2,1)} %own_ref.1, bf16[384,1024]{1,0:T(8,128)(2,1)} %q_ref.1), custom_call_target="tpu_custom_call" | custom-call | flops 3825205248 | bytes 2826240 | tf_op jit(solution)/shard_map/pallas_call | solution.py:71
  (9 shorter events, 0.1 us)
Async XLA Ops:
  0.0 0.7 %copy-start = (s32[48]{0:T(128)S(1)}, s32[48]{0:T(128)}, u32[]{:S(2)}) copy-start(s32[48]{0:T(128)} %param.13) | copy-start | bytes 580
  0.0 10.3 %copy-start.2 = (bf16[1,16,32,512]{3,2,1,0:T(8,128)(2,1)S(1)}, bf16[1,16,32,512]{3,2,1,0:T(8,128)(2,1)}, u32[]{:S(2)}) copy-start(bf16[1,16,32,512]{3,2,1,0:T(8,128)(2,1)} %param.11) | copy-start | bytes 1572868
  1.4 0.7 %copy-start.5 = (s32[1,16,64]{2,1,0:T(8,128)S(1)}, s32[1,16,64]{2,1,0:T(8,128)}, u32[]{:S(2)}) copy-start(s32[1,16,64]{2,1,0:T(8,128)} %param.15) | copy-start | bytes 12292
  2.9 13.7 %all-to-all-start = ((s32[16,1,65]{2,1,0:T(1,128)}), s32[16,1,65]{2,1,0:T(1,128)S(1)}, u32[]{:S(2)}, u32[]{:S(2)}) async-start(s32[16,1,65]{2,1,0:T(1,128)} %bitcast.6), calls=%async_computation | async-start | bytes 16384 | tf_op jit(solution)/shard_map/all_to_all | solution.py:107
  10.3 1.7 %copy-start.4 = (bf16[3,128,256]{2,1,0:T(8,128)(2,1)S(1)}, bf16[3,128,256]{2,1,0:T(8,128)(2,1)}, u32[]{:S(2)}) copy-start(bf16[3,128,256]{2,1,0:T(8,128)(2,1)} %param.10) | copy-start | bytes 589828
  10.4 12.2 %collective-permute-start = (bf16[16,32,256]{2,1,0:T(8,128)(2,1)S(1)}, bf16[16,32,256]{2,1,0:T(8,128)(2,1)S(1)}, u32[]{:S(2)}, u32[]{:S(2)}) collective-permute-start(bf16[16,32,256]{2,1,0:T(8,128)(2,1)S(1)} %get-tuple-element.10), channel_id=1, source_target_pairs={{0,16},{16,0},{1,17},{17,1},{2,18},{18,2},{3,19},{19,3},{4,20},{20... | collective-permute-start | bytes 786440 | tf_op jit(solution)/shard_map/ppermute | solution.py:127
  12.1 0.7 %copy-start.1 = (s32[48]{0:T(128)S(1)}, s32[48]{0:T(128)}, u32[]{:S(2)}) copy-start(s32[48]{0:T(128)} %param.14) | copy-start | bytes 580
  17.9 18.0 %all-to-all-start.1 = ((bf16[16,64,256]{2,1,0:T(8,128)(2,1)}), bf16[16,64,256]{2,1,0:T(8,128)(2,1)S(1)}, u32[]{:S(2)}, u32[]{:S(2)}) async-start(bf16[16,64,256]{2,1,0:T(8,128)(2,1)} %select_select_fusion), calls=%async_computation.1 | async-start | bytes 1048576 | tf_op jit(solution)/shard_map/all_to_all | solution.py:115
  35.9 0.8 %copy-start.3 = (bf16[16,64,256]{2,1,0:T(8,128)(2,1)}, bf16[16,64,256]{2,1,0:T(8,128)(2,1)S(1)}, u32[]{:S(2)}) copy-start(bf16[16,64,256]{2,1,0:T(8,128)(2,1)S(1)} %all-to-all-done.1) | copy-start | bytes 1572868

commit v10 on v7

--- a/solution.py
+++ b/solution.py
@@ -87,6 +87,18 @@
     )(bias, kept, fresh, own_kv, queries)
 
 
+def two_stage(table, n):
+    inner = max(d for d in range(1, n + 1) if n % d == 0 and d * d <= n)
+    outer = n // inner
+    rest = table.shape[1:]
+    near = [[a * inner + b for b in range(inner)] for a in range(outer)]
+    far = [[a * inner + b for a in range(outer)] for b in range(inner)]
+    table = table.reshape((outer, inner) + rest)
+    table = lax.all_to_all(table, "seq", 1, 1, axis_index_groups=near, tiled=True)
+    table = lax.all_to_all(table, "seq", 0, 0, axis_index_groups=far, tiled=True)
+    return table.reshape((n,) + rest)
+
+
 def per_device(
     n_seq, n_kvh, queries, own_kv, library, fresh_kv, retrieved, stretch_slot, stretch_len, recompute_pos
 ):
@@ -103,7 +115,7 @@
     devices = jnp.arange(n_seq, dtype=jnp.int32)
     hits = owner[None, :, None] == devices[:, None, None]
     request = jnp.sum(jnp.where(hits, payload[None], 0), axis=1)
-    asked = lax.all_to_all(request, "seq", 0, 0, tiled=True)
+    asked = two_stage(request, n_seq)
     which = asked[:, :1, None]
     odd_given = asked[:, 1:, None]
     halves = library.reshape(per_owner, -1, 2, library.shape[2])

time: 50.1 us -> 56.2 us (1.12)
  waiting for transfers between devices: 15.4 us -> 18 us
  starting transfers between devices: 12.5 us -> 14.7 us
  local copies, waits for them, and re-layouts: 3.76 us -> 5.57 us
  other arithmetic: 4.33 us -> 3.71 us
    all_to_all x1 -> x2, waiting for transfers between devices: 2.91 us -> 5.52 us  [the longest x1 5.52 us: two_stage(): lax.all_to_all(table, 'seq', 0, 0, axis_index_groups=far, tiled=True)]
    all_to_all x1 -> x2, starting transfers between devices: 7.39 us -> 9.11 us  [the longest x1 4.87 us: two_stage(): lax.all_to_all(table, 'seq', 0, 0, axis_index_groups=far, tiled=True)]
    unnamed x15, local copies, waits for them, and re-layouts: 1.98 us -> 2.6 us
    all_to_all x0 -> x1, local copies, waits for them, and re-layouts: none -> 0.6 us  [two_stage(): lax.all_to_all(table, 'seq', 1, 1, axis_index_groups=near, tiled=True)]
    reshape x0 -> x1, local copies, waits for them, and re-layouts: none -> 0.6 us  [two_stage(): table = table.reshape((outer, inner) + rest)]
    reduce_sum x1, other arithmetic: 0.72 us -> 0.12 us  [per_device(): request = jnp.sum(jnp.where(hits, payload[None], 0), axis=1)]
  transfers between devices with their start and end apart: 3 -> 4, of which waited for: 2 -> 2; matrix products, arithmetic and copies ran while one was open for 10% -> 10% of each run, Pallas kernels for 0% -> 0%
where the time goes in v10:
time: 56.2 us; the launch traced here: 55.8 us
  waiting for transfers between devices  18 us (32%)
  starting transfers between devices  14.7 us (26%)
  Pallas kernels  13.7 us (24%)
  local copies, waits for them, and re-layouts  5.57 us (10%)
  other arithmetic  3.71 us (7%)
    pallas_call x1, Pallas kernels, attend(): pl.pallas_call(attend_kernel, grid=(heads // step,), in_specs=[full(bias....  13.7 us
    all_to_all x1, waiting for transfers between devices, per_device(): recv = lax.all_to_all(send, 'seq', 0, 0, tiled=True)  12.5 us
    all_to_all x1, waiting for transfers between devices, two_stage(): lax.all_to_all(table, 'seq', 0, 0, axis_index_groups=far, tiled=True)  5.52 us
    all_to_all x1, starting transfers between devices, two_stage(): lax.all_to_all(table, 'seq', 0, 0, axis_index_groups=far, tiled=True)  4.87 us
    all_to_all x1, starting transfers between devices, two_stage(): lax.all_to_all(table, 'seq', 1, 1, axis_index_groups=near, tiled=True)  4.24 us
    all_to_all x1, starting transfers between devices, per_device(): recv = lax.all_to_all(send, 'seq', 0, 0, tiled=True)  3.57 us
    unnamed x15, local copies, waits for them, and re-layouts  2.6 us
    ppermute x1, starting transfers between devices, per_device(): pieces.append(lax.ppermute(piece, 'kvh', pairs))  2.05 us
  transfers between devices with their start and end apart: 4, of which 2 were waited for; matrix products, arithmetic and copies ran while one was open for 10% of the time, Pallas kernels for 0%

profile of v10, /device:TPU:0, one launch (start us, length us, event | category | flops | bytes accessed | tf_op | source)
XLA Modules:
  0.0 55.8 jit_solution(8195104615365534198)
XLA Ops:
  0.0 0.0 copy-start.3
  0.0 0.0 copy-start.4
  0.0 0.7 %copy-done.3 = s32[48]{0:T(128)S(1)} copy-done((s32[48]{0:T(128)S(1)}, s32[48]{0:T(128)}, u32[]{:S(2)}) %copy-start.3) | copy-done | bytes 216
  0.7 0.0 copy-done.4
  0.7 0.2 select_reduce_fusion.3
  0.9 0.0 copy-start.2
  0.9 0.1 fusion.1
  1.0 0.1 copy.19
  1.1 0.5 copy-done.2
  1.6 0.1 pad_add_fusion
  1.7 0.1 select_reduce_fusion
  1.8 0.6 %copy.20 = s32[4,4,65]{2,0,1:T(4,128)} copy(s32[4,4,65]{2,1,0:T(4,128)S(1)} %bitcast.35) | data formatting | bytes 8320 | tf_op jit(solution)/shard_map/reshape | solution.py:96
  2.4 4.2 %all-to-all-start = ((s32[4,4,65]{2,0,1:T(4,128)}), s32[4,4,65]{2,0,1:T(4,128)S(1)}, u32[]{:S(2)}, u32[]{:S(2)}) async-start(s32[4,4,65]{2,0,1:T(4,128)} %copy.20), calls=%async_computation | async-start | bytes 16384 | tf_op jit(solution)/shard_map/all_to_all | solution.py:97
  6.6 0.0 copy-start.1
  6.6 1.1 %dynamic-slice_bitcast_fusion.1 = (bf16[16,32,256]{2,1,0:T(8,128)(2,1)S(1)}, bf16[16,32,256]{2,1,0:T(8,128)(2,1)S(1)}) fusion(bf16[1,16,32,512]{3,2,1,0:T(8,128)(2,1)} %param.11, s32[]{:T(128)S(6)} %select_n.121, s32[]{:T(128)S(6)} %select_n.122), kind=kLoop, calls=%fused_computation.3 | loop fusion | bytes 1048584 | tf_op jit(solution)/shard_map/dynamic_slice | solution.py:132
  7.7 2.1 %collective-permute-start = (bf16[16,32,256]{2,1,0:T(8,128)(2,1)S(1)}, bf16[16,32,256]{2,1,0:T(8,128)(2,1)S(1)}, u32[]{:S(2)}, u32[]{:S(2)}) collective-permute-start(bf16[16,32,256]{2,1,0:T(8,128)(2,1)S(1)} %get-tuple-element.8), channel_id=1, source_target_pairs={{0,16},{16,0},{1,17},{17,1},{2,18},{18,2},{3,19},{19,3},{4,20},{20... | collective-permute-start | bytes 786440 | tf_op jit(solution)/shard_map/ppermute | solution.py:138
  9.8 0.0 copy-done.1
  9.8 0.1 reshape.212
  9.9 0.3 fusion.2
  10.2 0.0 copy-start.5
  10.2 0.6 %copy-done.5 = s32[48]{0:T(128)S(1)} copy-done((s32[48]{0:T(128)S(1)}, s32[48]{0:T(128)}, u32[]{:S(2)}) %copy-start.5) | copy-done | bytes 216
  10.9 0.2 select_reduce_fusion.2
  11.0 0.0 all-to-all-done
  11.0 0.6 %copy.21 = s32[4,4,65]{2,1,0:T(4,128)} copy(s32[4,4,65]{2,0,1:T(4,128)S(1)} %all-to-all-done) | data formatting | bytes 8320 | tf_op jit(solution)/shard_map/all_to_all | solution.py:97
  11.6 4.9 %all-to-all-start.1 = ((s32[4,4,65]{2,1,0:T(4,128)}), s32[4,4,65]{2,1,0:T(4,128)S(1)}, u32[]{:S(2)}, u32[]{:S(2)}) async-start(s32[4,4,65]{2,1,0:T(4,128)} %copy.21), calls=%async_computation.1 | async-start | bytes 16384 | tf_op jit(solution)/shard_map/all_to_all | solution.py:98
  16.5 0.1 select_bitcast_fusion
  16.6 5.5 %all-to-all-done.1 = s32[4,4,65]{2,1,0:T(4,128)S(1)} async-done(((s32[4,4,65]{2,1,0:T(4,128)}), s32[4,4,65]{2,1,0:T(4,128)S(1)}, u32[]{:S(2)}, u32[]{:S(2)}) %all-to-all-start.1) | async-done | bytes 4192 | tf_op jit(solution)/shard_map/all_to_all | solution.py:98
  22.1 0.1 compare_reduce_fusion.1
  22.2 0.1 slice_compare_fusion
  22.3 1.0 %select_select_fusion = bf16[16,64,256]{2,1,0:T(8,128)(2,1)} fusion(pred[16]{0:T(512)(128)(4,1)S(1)} %get-tuple-element.6, pred[16]{0:T(512)(128)(4,1)S(1)} %get-tuple-element.5, pred[16,64]{1,0:T(8,128)(4,1)S(1)} %slice_compare_fusion, bf16[64,256]{1,0:T(8,128)(2,1)S(1)} %get-tuple-element.21, bf16[64,256]{1,0:T(8,128)(2,1)S(1)} %get-tuple-element.22, ...), kind=kLoop, calls=%fused_computation.1 | loop fusion | flops 1310720 | bytes 721952 | tf_op jit(solution)/shard_map/jit(_where)/select_n | solution.py:125
  23.3 3.6 %all-to-all-start.2 = ((bf16[16,64,256]{2,1,0:T(8,128)(2,1)}), bf16[16,64,256]{2,1,0:T(8,128)(2,1)S(1)}, u32[]{:S(2)}, u32[]{:S(2)}) async-start(bf16[16,64,256]{2,1,0:T(8,128)(2,1)} %select_select_fusion), calls=%async_computation.2 | async-start | bytes 1048576 | tf_op jit(solution)/shard_map/all_to_all | solution.py:126
  26.9 0.1 dynamic-slice_bitcast_fusion.3
  27.0 0.1 select_reduce_fusion.1
  27.1 0.1 broadcast_select_fusion
  27.2 0.1 fusion
  27.3 0.1 select_n.109
  27.3 0.1 select_n.113
  27.4 0.6 %pad_maximum_fusion.1.bias_ref = f32[1,2048]{1,0:T(1,128)} fusion(f32[1,1024]{1,0:T(1,128)S(1)} %select_n.113, f32[1,1024]{1,0:T(1,128)S(1)} %select_n.109), kind=kLoop, calls=%fused_computation.14 | loop fusion | flops 2048 | bytes 16384 | tf_op jit(solution)/shard_map/concatenate | solution.py:150
  28.0 0.0 collective-permute-done
  28.0 0.8 %pad_maximum_fusion = bf16[16,64,256]{2,1,0:T(8,128)(2,1)} fusion(bf16[16,32,256]{2,1,0:T(8,128)(2,1)S(1)} %collective-permute-done, bf16[16,32,256]{2,1,0:T(8,128)(2,1)S(1)} %get-tuple-element.7), kind=kLoop, calls=%fused_computation | loop fusion | flops 1048576 | bytes 1048576 | tf_op jit(solution)/shard_map/concatenate | solution.py:141
  28.9 12.5 %all-to-all-done.2 = bf16[16,64,256]{2,1,0:T(8,128)(2,1)S(1)} async-done(((bf16[16,64,256]{2,1,0:T(8,128)(2,1)}), bf16[16,64,256]{2,1,0:T(8,128)(2,1)S(1)}, u32[]{:S(2)}, u32[]{:S(2)}) %all-to-all-start.2) | async-done | bytes 524320 | tf_op jit(solution)/shard_map/all_to_all | solution.py:126
  41.3 0.0 copy-start
  41.3 0.8 %copy-done = bf16[16,64,256]{2,1,0:T(8,128)(2,1)} copy-done((bf16[16,64,256]{2,1,0:T(8,128)(2,1)}, bf16[16,64,256]{2,1,0:T(8,128)(2,1)S(1)}, u32[]{:S(2)}) %copy-start) | copy-done | bytes 524312
  42.1 13.7 %shard_map.82 = bf16[384,1024]{1,0:T(8,128)(2,1)} custom-call(f32[1,2048]{1,0:T(1,128)} %pad_maximum_fusion.1.bias_ref, bf16[1024,256]{1,0:T(8,128)(2,1)} %bitcast.31, bf16[1024,256]{1,0:T(8,128)(2,1)} %bitcast.32, bf16[384,256]{1,0:T(8,128)(2,1)} %own_ref.1, bf16[384,1024]{1,0:T(8,128)(2,1)} %q_ref.1), custom_call_target="tpu_custom_call" | custom-call | flops 3825205248 | bytes 2826240 | tf_op jit(solution)/shard_map/pallas_call | solution.py:71
  (7 shorter events, 0.1 us)
Async XLA Ops:
  0.0 0.7 %copy-start.3 = (s32[48]{0:T(128)S(1)}, s32[48]{0:T(128)}, u32[]{:S(2)}) copy-start(s32[48]{0:T(128)} %param.13) | copy-start | bytes 580
  0.0 0.7 %copy-start.4 = (s32[1,16]{1,0:T(1,128)S(1)}, s32[1,16]{1,0:T(1,128)}, u32[]{:S(2)}) copy-start(s32[1,16]{1,0:T(1,128)} %param.12) | copy-start | bytes 196
  0.9 0.7 %copy-start.2 = (s32[1,16,64]{2,1,0:T(8,128)S(1)}, s32[1,16,64]{2,1,0:T(8,128)}, u32[]{:S(2)}) copy-start(s32[1,16,64]{2,1,0:T(8,128)} %param.15) | copy-start | bytes 12292
  2.4 8.6 %all-to-all-start = ((s32[4,4,65]{2,0,1:T(4,128)}), s32[4,4,65]{2,0,1:T(4,128)S(1)}, u32[]{:S(2)}, u32[]{:S(2)}) async-start(s32[4,4,65]{2,0,1:T(4,128)} %copy.20), calls=%async_computation | async-start | bytes 16384 | tf_op jit(solution)/shard_map/all_to_all | solution.py:97
  6.6 3.2 %copy-start.1 = (bf16[3,128,256]{2,1,0:T(8,128)(2,1)S(1)}, bf16[3,128,256]{2,1,0:T(8,128)(2,1)}, u32[]{:S(2)}) copy-start(bf16[3,128,256]{2,1,0:T(8,128)(2,1)} %param.10) | copy-start | bytes 589828
  7.7 20.3 %collective-permute-start = (bf16[16,32,256]{2,1,0:T(8,128)(2,1)S(1)}, bf16[16,32,256]{2,1,0:T(8,128)(2,1)S(1)}, u32[]{:S(2)}, u32[]{:S(2)}) collective-permute-start(bf16[16,32,256]{2,1,0:T(8,128)(2,1)S(1)} %get-tuple-element.8), channel_id=1, source_target_pairs={{0,16},{16,0},{1,17},{17,1},{2,18},{18,2},{3,19},{19,3},{4,20},{20... | collective-permute-start | bytes 786440 | tf_op jit(solution)/shard_map/ppermute | solution.py:138
  10.2 0.7 %copy-start.5 = (s32[48]{0:T(128)S(1)}, s32[48]{0:T(128)}, u32[]{:S(2)}) copy-start(s32[48]{0:T(128)} %param.14) | copy-start | bytes 580
  11.6 10.5 %all-to-all-start.1 = ((s32[4,4,65]{2,1,0:T(4,128)}), s32[4,4,65]{2,1,0:T(4,128)S(1)}, u32[]{:S(2)}, u32[]{:S(2)}) async-start(s32[4,4,65]{2,1,0:T(4,128)} %copy.21), calls=%async_computation.1 | async-start | bytes 16384 | tf_op jit(solution)/shard_map/all_to_all | solution.py:98
  23.3 18.0 %all-to-all-start.2 = ((bf16[16,64,256]{2,1,0:T(8,128)(2,1)}), bf16[16,64,256]{2,1,0:T(8,128)(2,1)S(1)}, u32[]{:S(2)}, u32[]{:S(2)}) async-start(bf16[16,64,256]{2,1,0:T(8,128)(2,1)} %select_select_fusion), calls=%async_computation.2 | async-start | bytes 1048576 | tf_op jit(solution)/shard_map/all_to_all | solution.py:126
  41.3 0.8 %copy-start = (bf16[16,64,256]{2,1,0:T(8,128)(2,1)}, bf16[16,64,256]{2,1,0:T(8,128)(2,1)S(1)}, u32[]{:S(2)}) copy-start(bf16[16,64,256]{2,1,0:T(8,128)(2,1)S(1)} %all-to-all-done.2) | copy-start | bytes 1572868

commit v11 on v7

--- a/solution.py
+++ b/solution.py
@@ -10,7 +10,7 @@
 HD = 128
 CL = 128
 TR = 128
-PAIR = 4
+PAIR = 8
 LEAD = 2
 
 

time: 50.1 us -> 50.1 us (level)
  no operation moved by 1% of the time
where the time goes in v11:
time: 50.1 us; the launch traced here: 49.8 us
  waiting for transfers between devices  15.4 us (31%)
  Pallas kernels  13.6 us (27%)
  starting transfers between devices  12.5 us (25%)
  other arithmetic  4.33 us (9%)
  local copies, waits for them, and re-layouts  3.76 us (8%)
    pallas_call x1, Pallas kernels, attend(): pl.pallas_call(attend_kernel, grid=(heads // step,), in_specs=[full(bias....  13.6 us
    all_to_all x1, waiting for transfers between devices, per_device(): recv = lax.all_to_all(send, 'seq', 0, 0, tiled=True)  12.5 us
    all_to_all x1, starting transfers between devices, per_device(): asked = lax.all_to_all(request, 'seq', 0, 0, tiled=True)  7.39 us
    all_to_all x1, starting transfers between devices, per_device(): recv = lax.all_to_all(send, 'seq', 0, 0, tiled=True)  3.57 us
    all_to_all x1, waiting for transfers between devices, per_device(): asked = lax.all_to_all(request, 'seq', 0, 0, tiled=True)  2.91 us
    unnamed x15, local copies, waits for them, and re-layouts  1.98 us
    ppermute x1, starting transfers between devices, per_device(): pieces.append(lax.ppermute(piece, 'kvh', pairs))  1.59 us
    dynamic_slice x1, local copies, waits for them, and re-layouts, per_device(): pieces = [lax.dynamic_slice_in_dim(fresh_local, me * width, width, 2)]  1.11 us
  transfers between devices with their start and end apart: 3, of which 2 were waited for; matrix products, arithmetic and copies ran while one was open for 10% of the time, Pallas kernels for 0%

profile of v11, /device:TPU:0, one launch (start us, length us, event | category | flops | bytes accessed | tf_op | source)
XLA Modules:
  0.0 49.8 jit_solution(3482813605496175104)
XLA Ops:
  0.0 0.0 copy-start.3
  0.0 0.0 copy-start.4
  0.0 0.7 %copy-done.3 = s32[48]{0:T(128)S(1)} copy-done((s32[48]{0:T(128)S(1)}, s32[48]{0:T(128)}, u32[]{:S(2)}) %copy-start.3) | copy-done | bytes 216
  0.7 0.0 copy-done.4
  0.7 0.2 select_reduce_fusion.3
  0.9 0.0 copy-start.2
  0.9 0.1 fusion.1
  1.0 0.1 copy.17
  1.1 0.5 copy-done.2
  1.6 0.1 pad_add_fusion
  1.7 0.7 %select_reduce_fusion = s32[16,65]{1,0:T(8,128)} fusion(s32[16,65]{1,0:T(8,128)S(1)} %pad_add_fusion, pred[16,16]{1,0:T(8,128)(4,1)S(1)} %get-tuple-element.18), kind=kLoop, calls=%fused_computation.4 | loop fusion | flops 32240 | bytes 8576 | tf_op jit(solution)/shard_map/reduce_sum | solution.py:105
  2.4 7.4 %all-to-all-start = ((s32[16,1,65]{2,1,0:T(1,128)}), s32[16,1,65]{2,1,0:T(1,128)S(1)}, u32[]{:S(2)}, u32[]{:S(2)}) async-start(s32[16,1,65]{2,1,0:T(1,128)} %bitcast.7), calls=%async_computation | async-start | bytes 16384 | tf_op jit(solution)/shard_map/all_to_all | solution.py:106
  9.8 0.0 copy-start.1
  9.8 1.1 %dynamic-slice_bitcast_fusion.1 = (bf16[16,32,256]{2,1,0:T(8,128)(2,1)S(1)}, bf16[16,32,256]{2,1,0:T(8,128)(2,1)S(1)}) fusion(bf16[1,16,32,512]{3,2,1,0:T(8,128)(2,1)} %param.11, s32[]{:T(128)S(6)} %select_n.121, s32[]{:T(128)S(6)} %select_n.122), kind=kLoop, calls=%fused_computation.3 | loop fusion | bytes 1048584 | tf_op jit(solution)/shard_map/dynamic_slice | solution.py:120
  10.9 0.0 copy-start.5
  10.9 1.6 %collective-permute-start = (bf16[16,32,256]{2,1,0:T(8,128)(2,1)S(1)}, bf16[16,32,256]{2,1,0:T(8,128)(2,1)S(1)}, u32[]{:S(2)}, u32[]{:S(2)}) collective-permute-start(bf16[16,32,256]{2,1,0:T(8,128)(2,1)S(1)} %get-tuple-element.8), channel_id=1, source_target_pairs={{0,16},{16,0},{1,17},{17,1},{2,18},{18,2},{3,19},{19,3},{4,20},{20... | collective-permute-start | bytes 786440 | tf_op jit(solution)/shard_map/ppermute | solution.py:126
  12.5 0.0 copy-done.5
  12.5 0.2 select_reduce_fusion.2
  12.7 0.0 copy-done.1
  12.7 0.1 reshape.206
  12.8 0.3 fusion.2
  13.1 0.1 select_bitcast_fusion
  13.2 2.9 %all-to-all-done = s32[16,1,65]{2,1,0:T(1,128)S(1)} async-done(((s32[16,1,65]{2,1,0:T(1,128)}), s32[16,1,65]{2,1,0:T(1,128)S(1)}, u32[]{:S(2)}, u32[]{:S(2)}) %all-to-all-start) | async-done | bytes 4192 | tf_op jit(solution)/shard_map/all_to_all | solution.py:106
  16.1 0.1 compare_reduce_fusion.1
  16.2 0.1 slice_compare_fusion
  16.3 1.0 %select_select_fusion = bf16[16,64,256]{2,1,0:T(8,128)(2,1)} fusion(pred[16]{0:T(512)(128)(4,1)S(1)} %get-tuple-element.6, pred[16]{0:T(512)(128)(4,1)S(1)} %get-tuple-element.5, pred[16,64]{1,0:T(8,128)(4,1)S(1)} %slice_compare_fusion, bf16[64,256]{1,0:T(8,128)(2,1)S(1)} %get-tuple-element.21, bf16[64,256]{1,0:T(8,128)(2,1)S(1)} %get-tuple-element.22, ...), kind=kLoop, calls=%fused_computation.1 | loop fusion | flops 1310720 | bytes 721952 | tf_op jit(solution)/shard_map/jit(_where)/select_n | solution.py:113
  17.3 3.6 %all-to-all-start.1 = ((bf16[16,64,256]{2,1,0:T(8,128)(2,1)}), bf16[16,64,256]{2,1,0:T(8,128)(2,1)S(1)}, u32[]{:S(2)}, u32[]{:S(2)}) async-start(bf16[16,64,256]{2,1,0:T(8,128)(2,1)} %select_select_fusion), calls=%async_computation.1 | async-start | bytes 1048576 | tf_op jit(solution)/shard_map/all_to_all | solution.py:114
  20.9 0.1 dynamic-slice_bitcast_fusion.3
  21.0 0.1 select_reduce_fusion.1
  21.1 0.1 broadcast_select_fusion
  21.2 0.1 fusion
  21.3 0.1 select_n.109
  21.4 0.1 select_n.113
  21.4 0.6 %pad_maximum_fusion.1.bias_ref = f32[1,2048]{1,0:T(1,128)} fusion(f32[1,1024]{1,0:T(1,128)S(1)} %select_n.113, f32[1,1024]{1,0:T(1,128)S(1)} %select_n.109), kind=kLoop, calls=%fused_computation.14 | loop fusion | flops 2048 | bytes 16384 | tf_op jit(solution)/shard_map/concatenate | solution.py:138
  22.0 0.0 collective-permute-done
  22.0 0.8 %pad_maximum_fusion = bf16[16,64,256]{2,1,0:T(8,128)(2,1)} fusion(bf16[16,32,256]{2,1,0:T(8,128)(2,1)S(1)} %collective-permute-done, bf16[16,32,256]{2,1,0:T(8,128)(2,1)S(1)} %get-tuple-element.7), kind=kLoop, calls=%fused_computation | loop fusion | flops 1048576 | bytes 1048576 | tf_op jit(solution)/shard_map/concatenate | solution.py:129
  22.9 12.5 %all-to-all-done.1 = bf16[16,64,256]{2,1,0:T(8,128)(2,1)S(1)} async-done(((bf16[16,64,256]{2,1,0:T(8,128)(2,1)}), bf16[16,64,256]{2,1,0:T(8,128)(2,1)S(1)}, u32[]{:S(2)}, u32[]{:S(2)}) %all-to-all-start.1) | async-done | bytes 524320 | tf_op jit(solution)/shard_map/all_to_all | solution.py:114
  35.3 0.0 copy-start
  35.4 0.8 %copy-done = bf16[16,64,256]{2,1,0:T(8,128)(2,1)} copy-done((bf16[16,64,256]{2,1,0:T(8,128)(2,1)}, bf16[16,64,256]{2,1,0:T(8,128)(2,1)S(1)}, u32[]{:S(2)}) %copy-start) | copy-done | bytes 524312
  36.1 13.6 %shard_map.82 = bf16[384,1024]{1,0:T(8,128)(2,1)} custom-call(f32[1,2048]{1,0:T(1,128)} %pad_maximum_fusion.1.bias_ref, bf16[1024,256]{1,0:T(8,128)(2,1)} %bitcast.33, bf16[1024,256]{1,0:T(8,128)(2,1)} %bitcast.34, bf16[384,256]{1,0:T(8,128)(2,1)} %own_ref.1, bf16[384,1024]{1,0:T(8,128)(2,1)} %q_ref.1), custom_call_target="tpu_custom_call" | custom-call | flops 3825205248 | bytes 2826240 | tf_op jit(solution)/shard_map/pallas_call | solution.py:71
  (7 shorter events, 0.1 us)
Async XLA Ops:
  0.0 0.7 %copy-start.3 = (s32[48]{0:T(128)S(1)}, s32[48]{0:T(128)}, u32[]{:S(2)}) copy-start(s32[48]{0:T(128)} %param.13) | copy-start | bytes 580
  0.0 0.7 %copy-start.4 = (s32[1,16]{1,0:T(1,128)S(1)}, s32[1,16]{1,0:T(1,128)}, u32[]{:S(2)}) copy-start(s32[1,16]{1,0:T(1,128)} %param.12) | copy-start | bytes 196
  0.9 0.7 %copy-start.2 = (s32[1,16,64]{2,1,0:T(8,128)S(1)}, s32[1,16,64]{2,1,0:T(8,128)}, u32[]{:S(2)}) copy-start(s32[1,16,64]{2,1,0:T(8,128)} %param.15) | copy-start | bytes 12292
  2.4 13.7 %all-to-all-start = ((s32[16,1,65]{2,1,0:T(1,128)}), s32[16,1,65]{2,1,0:T(1,128)S(1)}, u32[]{:S(2)}, u32[]{:S(2)}) async-start(s32[16,1,65]{2,1,0:T(1,128)} %bitcast.7), calls=%async_computation | async-start | bytes 16384 | tf_op jit(solution)/shard_map/all_to_all | solution.py:106
  9.8 2.9 %copy-start.1 = (bf16[3,128,256]{2,1,0:T(8,128)(2,1)S(1)}, bf16[3,128,256]{2,1,0:T(8,128)(2,1)}, u32[]{:S(2)}) copy-start(bf16[3,128,256]{2,1,0:T(8,128)(2,1)} %param.10) | copy-start | bytes 589828
  10.9 1.6 %copy-start.5 = (s32[48]{0:T(128)S(1)}, s32[48]{0:T(128)}, u32[]{:S(2)}) copy-start(s32[48]{0:T(128)} %param.14) | copy-start | bytes 580
  10.9 11.1 %collective-permute-start = (bf16[16,32,256]{2,1,0:T(8,128)(2,1)S(1)}, bf16[16,32,256]{2,1,0:T(8,128)(2,1)S(1)}, u32[]{:S(2)}, u32[]{:S(2)}) collective-permute-start(bf16[16,32,256]{2,1,0:T(8,128)(2,1)S(1)} %get-tuple-element.8), channel_id=1, source_target_pairs={{0,16},{16,0},{1,17},{17,1},{2,18},{18,2},{3,19},{19,3},{4,20},{20... | collective-permute-start | bytes 786440 | tf_op jit(solution)/shard_map/ppermute | solution.py:126
  17.3 18.0 %all-to-all-start.1 = ((bf16[16,64,256]{2,1,0:T(8,128)(2,1)}), bf16[16,64,256]{2,1,0:T(8,128)(2,1)S(1)}, u32[]{:S(2)}, u32[]{:S(2)}) async-start(bf16[16,64,256]{2,1,0:T(8,128)(2,1)} %select_select_fusion), calls=%async_computation.1 | async-start | bytes 1048576 | tf_op jit(solution)/shard_map/all_to_all | solution.py:114
  35.3 0.8 %copy-start = (bf16[16,64,256]{2,1,0:T(8,128)(2,1)}, bf16[16,64,256]{2,1,0:T(8,128)(2,1)S(1)}, u32[]{:S(2)}) copy-start(bf16[16,64,256]{2,1,0:T(8,128)(2,1)S(1)} %all-to-all-done.1) | copy-start | bytes 1572868

commit v12 on v7

--- a/solution.py
+++ b/solution.py
@@ -103,7 +103,10 @@
     devices = jnp.arange(n_seq, dtype=jnp.int32)
     hits = owner[None, :, None] == devices[:, None, None]
     request = jnp.sum(jnp.where(hits, payload[None], 0), axis=1)
+    width_asked = request.shape[1]
+    request = jnp.pad(request, ((0, 0), (0, 1024 - width_asked))).reshape(n_seq, 8, 128)
     asked = lax.all_to_all(request, "seq", 0, 0, tiled=True)
+    asked = asked.reshape(n_seq, 1024)[:, :width_asked]
     which = asked[:, :1, None]
     odd_given = asked[:, 1:, None]
     halves = library.reshape(per_owner, -1, 2, library.shape[2])

time: 50.1 us -> 50.8 us (1.014)
  local copies, waits for them, and re-layouts: 3.76 us -> 5.15 us
  other arithmetic: 4.33 us -> 3.6 us
    unnamed x15 -> x19, local copies, waits for them, and re-layouts: 1.98 us -> 3.37 us
    reduce_sum x1, other arithmetic: 0.72 us -> 0.12 us  [per_device(): request = jnp.sum(jnp.where(hits, payload[None], 0), axis=1)]
where the time goes in v12:
time: 50.8 us; the launch traced here: 50.4 us
  waiting for transfers between devices  15.3 us (30%)
  Pallas kernels  13.7 us (27%)
  starting transfers between devices  12.5 us (25%)
  local copies, waits for them, and re-layouts  5.15 us (10%)
  other arithmetic  3.6 us (7%)
    pallas_call x1, Pallas kernels, attend(): pl.pallas_call(attend_kernel, grid=(heads // step,), in_specs=[full(bias....  13.7 us
    all_to_all x1, waiting for transfers between devices, per_device(): recv = lax.all_to_all(send, 'seq', 0, 0, tiled=True)  12.5 us
    all_to_all x1, starting transfers between devices, per_device(): asked = lax.all_to_all(request, 'seq', 0, 0, tiled=True)  7.39 us
    all_to_all x1, starting transfers between devices, per_device(): recv = lax.all_to_all(send, 'seq', 0, 0, tiled=True)  3.57 us
    unnamed x19, local copies, waits for them, and re-layouts  3.37 us
    all_to_all x1, waiting for transfers between devices, per_device(): asked = lax.all_to_all(request, 'seq', 0, 0, tiled=True)  2.83 us
    ppermute x1, starting transfers between devices, per_device(): pieces.append(lax.ppermute(piece, 'kvh', pairs))  1.59 us
    dynamic_slice x1, local copies, waits for them, and re-layouts, per_device(): pieces = [lax.dynamic_slice_in_dim(fresh_local, me * width, width, 2)]  1.11 us
  transfers between devices with their start and end apart: 3, of which 2 were waited for; matrix products, arithmetic and copies ran while one was open for 10% of the time, Pallas kernels for 0%

profile of v12, /device:TPU:0, one launch (start us, length us, event | category | flops | bytes accessed | tf_op | source)
XLA Modules:
  0.0 50.4 jit_solution(13817399895306913199)
XLA Ops:
  0.0 0.0 copy-start.3
  0.0 0.0 copy-start.4
  0.0 0.7 %copy-done.3 = s32[48]{0:T(128)S(1)} copy-done((s32[48]{0:T(128)S(1)}, s32[48]{0:T(128)}, u32[]{:S(2)}) %copy-start.3) | copy-done | bytes 216
  0.7 0.0 copy-done.4
  0.7 0.2 select_reduce_fusion.3
  0.9 0.0 copy-start.2
  0.9 0.1 fusion.1
  1.0 0.1 copy.17
  1.1 0.5 copy-done.2
  1.6 0.1 pad_add_fusion
  1.7 0.1 select_reduce_fusion
  1.8 0.6 %copy.26 = s32[2,8,8,128]{3,2,1,0:T(8,128)} copy(s32[2,8,8,128]{3,1,2,0:T(8,128)S(1)} %pad_bitcast_fusion) | data formatting | bytes 131072
  2.4 7.4 %all-to-all-start = ((s32[16,8,128]{2,1,0:T(8,128)}), s32[16,8,128]{2,1,0:T(8,128)S(1)}, u32[]{:S(2)}, u32[]{:S(2)}) async-start(s32[16,8,128]{2,1,0:T(8,128)} %bitcast.19), calls=%async_computation | async-start | bytes 131072 | tf_op jit(solution)/shard_map/all_to_all | solution.py:108
  9.9 0.0 copy-start.1
  9.9 1.1 %dynamic-slice_bitcast_fusion.1 = (bf16[16,32,256]{2,1,0:T(8,128)(2,1)S(1)}, bf16[16,32,256]{2,1,0:T(8,128)(2,1)S(1)}) fusion(bf16[1,16,32,512]{3,2,1,0:T(8,128)(2,1)} %param.11, s32[]{:T(128)S(6)} %select_n.121, s32[]{:T(128)S(6)} %select_n.122), kind=kLoop, calls=%fused_computation.3 | loop fusion | bytes 1048584 | tf_op jit(solution)/shard_map/dynamic_slice | solution.py:123
  11.0 1.6 %collective-permute-start = (bf16[16,32,256]{2,1,0:T(8,128)(2,1)S(1)}, bf16[16,32,256]{2,1,0:T(8,128)(2,1)S(1)}, u32[]{:S(2)}, u32[]{:S(2)}) collective-permute-start(bf16[16,32,256]{2,1,0:T(8,128)(2,1)S(1)} %get-tuple-element.6), channel_id=1, source_target_pairs={{0,16},{16,0},{1,17},{17,1},{2,18},{18,2},{3,19},{19,3},{4,20},{20... | collective-permute-start | bytes 786440 | tf_op jit(solution)/shard_map/ppermute | solution.py:129
  12.6 0.0 copy-start.5
  12.6 0.7 %copy-done.5 = s32[48]{0:T(128)S(1)} copy-done((s32[48]{0:T(128)S(1)}, s32[48]{0:T(128)}, u32[]{:S(2)}) %copy-start.5) | copy-done | bytes 216
  13.2 0.2 select_reduce_fusion.2
  13.4 0.0 copy-done.1
  13.4 0.1 reshape.212
  13.5 0.3 fusion.2
  13.8 0.1 select_bitcast_fusion
  13.9 2.8 %all-to-all-done = s32[16,8,128]{2,1,0:T(8,128)S(1)} async-done(((s32[16,8,128]{2,1,0:T(8,128)}), s32[16,8,128]{2,1,0:T(8,128)S(1)}, u32[]{:S(2)}, u32[]{:S(2)}) %all-to-all-start) | async-done | bytes 65568 | tf_op jit(solution)/shard_map/all_to_all | solution.py:108
  16.8 0.1 slice_compare_fusion
  16.8 0.1 copy.25
  16.9 1.0 %select_select_fusion = bf16[16,64,256]{2,1,0:T(8,128)(2,1)} fusion(pred[16]{0:T(512)(128)(4,1)S(1)} %get-tuple-element.16, pred[16]{0:T(512)(128)(4,1)S(1)} %get-tuple-element.15, pred[16,64]{1,0:T(8,128)(4,1)S(1)} %slice_compare_fusion, bf16[64,256]{1,0:T(8,128)(2,1)S(1)} %get-tuple-element.21, bf16[64,256]{1,0:T(8,128)(2,1)S(1)} %get-tuple-element.22, ...), kind=kLoop, calls=%fused_computation.1 | loop fusion | flops 1310720 | bytes 721952 | tf_op jit(solution)/shard_map/jit(_where)/select_n | solution.py:116
  18.0 3.6 %all-to-all-start.1 = ((bf16[16,64,256]{2,1,0:T(8,128)(2,1)}), bf16[16,64,256]{2,1,0:T(8,128)(2,1)S(1)}, u32[]{:S(2)}, u32[]{:S(2)}) async-start(bf16[16,64,256]{2,1,0:T(8,128)(2,1)} %select_select_fusion), calls=%async_computation.1 | async-start | bytes 1048576 | tf_op jit(solution)/shard_map/all_to_all | solution.py:117
  21.6 0.1 dynamic-slice_bitcast_fusion.3
  21.6 0.1 select_reduce_fusion.1
  21.8 0.1 broadcast_select_fusion
  21.8 0.1 fusion
  21.9 0.1 select_n.109
  22.0 0.1 select_n.113
  22.1 0.6 %pad_maximum_fusion.1.bias_ref = f32[1,2048]{1,0:T(1,128)} fusion(f32[1,1024]{1,0:T(1,128)S(1)} %select_n.113, f32[1,1024]{1,0:T(1,128)S(1)} %select_n.109), kind=kLoop, calls=%fused_computation.16 | loop fusion | flops 2048 | bytes 16384 | tf_op jit(solution)/shard_map/concatenate | solution.py:141
  22.7 0.0 collective-permute-done
  22.7 0.8 %pad_maximum_fusion = bf16[16,64,256]{2,1,0:T(8,128)(2,1)} fusion(bf16[16,32,256]{2,1,0:T(8,128)(2,1)S(1)} %collective-permute-done, bf16[16,32,256]{2,1,0:T(8,128)(2,1)S(1)} %get-tuple-element.5), kind=kLoop, calls=%fused_computation | loop fusion | flops 1048576 | bytes 1048576 | tf_op jit(solution)/shard_map/concatenate | solution.py:132
  23.5 12.5 %all-to-all-done.1 = bf16[16,64,256]{2,1,0:T(8,128)(2,1)S(1)} async-done(((bf16[16,64,256]{2,1,0:T(8,128)(2,1)}), bf16[16,64,256]{2,1,0:T(8,128)(2,1)S(1)}, u32[]{:S(2)}, u32[]{:S(2)}) %all-to-all-start.1) | async-done | bytes 524320 | tf_op jit(solution)/shard_map/all_to_all | solution.py:117
  36.0 0.0 copy-start
  36.0 0.8 %copy-done = bf16[16,64,256]{2,1,0:T(8,128)(2,1)} copy-done((bf16[16,64,256]{2,1,0:T(8,128)(2,1)}, bf16[16,64,256]{2,1,0:T(8,128)(2,1)S(1)}, u32[]{:S(2)}) %copy-start) | copy-done | bytes 524312
  36.8 13.7 %shard_map.82 = bf16[384,1024]{1,0:T(8,128)(2,1)} custom-call(f32[1,2048]{1,0:T(1,128)} %pad_maximum_fusion.1.bias_ref, bf16[1024,256]{1,0:T(8,128)(2,1)} %bitcast.40, bf16[1024,256]{1,0:T(8,128)(2,1)} %bitcast.41, bf16[384,256]{1,0:T(8,128)(2,1)} %own_ref.1, bf16[384,1024]{1,0:T(8,128)(2,1)} %q_ref.1), custom_call_target="tpu_custom_call" | custom-call | flops 3825205248 | bytes 2826240 | tf_op jit(solution)/shard_map/pallas_call | solution.py:71
  (11 shorter events, 0.1 us)
Async XLA Ops:
  0.0 0.7 %copy-start.3 = (s32[48]{0:T(128)S(1)}, s32[48]{0:T(128)}, u32[]{:S(2)}) copy-start(s32[48]{0:T(128)} %param.13) | copy-start | bytes 580
  0.0 0.7 %copy-start.4 = (s32[1,16]{1,0:T(1,128)S(1)}, s32[1,16]{1,0:T(1,128)}, u32[]{:S(2)}) copy-start(s32[1,16]{1,0:T(1,128)} %param.12) | copy-start | bytes 196
  0.9 0.7 %copy-start.2 = (s32[1,16,64]{2,1,0:T(8,128)S(1)}, s32[1,16,64]{2,1,0:T(8,128)}, u32[]{:S(2)}) copy-start(s32[1,16,64]{2,1,0:T(8,128)} %param.15) | copy-start | bytes 12292
  2.4 14.3 %all-to-all-start = ((s32[16,8,128]{2,1,0:T(8,128)}), s32[16,8,128]{2,1,0:T(8,128)S(1)}, u32[]{:S(2)}, u32[]{:S(2)}) async-start(s32[16,8,128]{2,1,0:T(8,128)} %bitcast.19), calls=%async_computation | async-start | bytes 131072 | tf_op jit(solution)/shard_map/all_to_all | solution.py:108
  9.9 3.5 %copy-start.1 = (bf16[3,128,256]{2,1,0:T(8,128)(2,1)S(1)}, bf16[3,128,256]{2,1,0:T(8,128)(2,1)}, u32[]{:S(2)}) copy-start(bf16[3,128,256]{2,1,0:T(8,128)(2,1)} %param.10) | copy-start | bytes 589828
  11.0 11.7 %collective-permute-start = (bf16[16,32,256]{2,1,0:T(8,128)(2,1)S(1)}, bf16[16,32,256]{2,1,0:T(8,128)(2,1)S(1)}, u32[]{:S(2)}, u32[]{:S(2)}) collective-permute-start(bf16[16,32,256]{2,1,0:T(8,128)(2,1)S(1)} %get-tuple-element.6), channel_id=1, source_target_pairs={{0,16},{16,0},{1,17},{17,1},{2,18},{18,2},{3,19},{19,3},{4,20},{20... | collective-permute-start | bytes 786440 | tf_op jit(solution)/shard_map/ppermute | solution.py:129
  12.6 0.7 %copy-start.5 = (s32[48]{0:T(128)S(1)}, s32[48]{0:T(128)}, u32[]{:S(2)}) copy-start(s32[48]{0:T(128)} %param.14) | copy-start | bytes 580
  18.0 18.0 %all-to-all-start.1 = ((bf16[16,64,256]{2,1,0:T(8,128)(2,1)}), bf16[16,64,256]{2,1,0:T(8,128)(2,1)S(1)}, u32[]{:S(2)}, u32[]{:S(2)}) async-start(bf16[16,64,256]{2,1,0:T(8,128)(2,1)} %select_select_fusion), calls=%async_computation.1 | async-start | bytes 1048576 | tf_op jit(solution)/shard_map/all_to_all | solution.py:117
  36.0 0.8 %copy-start = (bf16[16,64,256]{2,1,0:T(8,128)(2,1)}, bf16[16,64,256]{2,1,0:T(8,128)(2,1)S(1)}, u32[]{:S(2)}) copy-start(bf16[16,64,256]{2,1,0:T(8,128)(2,1)S(1)} %all-to-all-done.1) | copy-start | bytes 1572868

commit v13 on v7

--- a/solution.py
+++ b/solution.py
@@ -106,10 +106,10 @@
     asked = lax.all_to_all(request, "seq", 0, 0, tiled=True)
     which = asked[:, :1, None]
     odd_given = asked[:, 1:, None]
-    halves = library.reshape(per_owner, -1, 2, library.shape[2])
+    halves = jnp.swapaxes(library.reshape(per_owner, -1, 2, library.shape[2]), 1, 2)
     send = None
     for k in range(per_owner):
-        kept = jnp.where(odd_given == 0, halves[k, :, 1][None], halves[k, :, 0][None])
+        kept = jnp.where(odd_given == 0, halves[k, 1][None], halves[k, 0][None])
         send = kept if send is None else jnp.where(which == k, kept, send)
     recv = lax.all_to_all(send, "seq", 0, 0, tiled=True)
 

time: 50.1 us -> 50.1 us (level)
  no operation moved by 1% of the time
where the time goes in v13:
time: 50.1 us; the launch traced here: 49.8 us
  waiting for transfers between devices  15.4 us (31%)
  Pallas kernels  13.7 us (27%)
  starting transfers between devices  12.5 us (25%)
  other arithmetic  4.33 us (9%)
  local copies, waits for them, and re-layouts  3.76 us (8%)
    pallas_call x1, Pallas kernels, attend(): pl.pallas_call(attend_kernel, grid=(heads // step,), in_specs=[full(bias....  13.7 us
    all_to_all x1, waiting for transfers between devices, per_device(): recv = lax.all_to_all(send, 'seq', 0, 0, tiled=True)  12.5 us
    all_to_all x1, starting transfers between devices, per_device(): asked = lax.all_to_all(request, 'seq', 0, 0, tiled=True)  7.39 us
    all_to_all x1, starting transfers between devices, per_device(): recv = lax.all_to_all(send, 'seq', 0, 0, tiled=True)  3.57 us
    all_to_all x1, waiting for transfers between devices, per_device(): asked = lax.all_to_all(request, 'seq', 0, 0, tiled=True)  2.91 us
    unnamed x15, local copies, waits for them, and re-layouts  1.98 us
    ppermute x1, starting transfers between devices, per_device(): pieces.append(lax.ppermute(piece, 'kvh', pairs))  1.59 us
    dynamic_slice x1, local copies, waits for them, and re-layouts, per_device(): pieces = [lax.dynamic_slice_in_dim(fresh_local, me * width, width, 2)]  1.11 us
  transfers between devices with their start and end apart: 3, of which 2 were waited for; matrix products, arithmetic and copies ran while one was open for 10% of the time, Pallas kernels for 0%

profile of v13, /device:TPU:0, one launch (start us, length us, event | category | flops | bytes accessed | tf_op | source)
XLA Modules:
  0.0 49.8 jit_solution(4246491966223571015)
XLA Ops:
  0.0 0.0 copy-start.3
  0.0 0.0 copy-start.4
  0.0 0.7 %copy-done.3 = s32[48]{0:T(128)S(1)} copy-done((s32[48]{0:T(128)S(1)}, s32[48]{0:T(128)}, u32[]{:S(2)}) %copy-start.3) | copy-done | bytes 216
  0.7 0.0 copy-done.4
  0.7 0.2 select_reduce_fusion.3
  0.9 0.0 copy-start.2
  0.9 0.1 fusion.1
  1.0 0.1 copy.17
  1.1 0.5 copy-done.2
  1.6 0.1 pad_add_fusion
  1.7 0.7 %select_reduce_fusion = s32[16,65]{1,0:T(8,128)} fusion(s32[16,65]{1,0:T(8,128)S(1)} %pad_add_fusion, pred[16,16]{1,0:T(8,128)(4,1)S(1)} %get-tuple-element.18), kind=kLoop, calls=%fused_computation.4 | loop fusion | flops 32240 | bytes 8576 | tf_op jit(solution)/shard_map/reduce_sum | solution.py:105
  2.4 7.4 %all-to-all-start = ((s32[16,1,65]{2,1,0:T(1,128)}), s32[16,1,65]{2,1,0:T(1,128)S(1)}, u32[]{:S(2)}, u32[]{:S(2)}) async-start(s32[16,1,65]{2,1,0:T(1,128)} %bitcast.7), calls=%async_computation | async-start | bytes 16384 | tf_op jit(solution)/shard_map/all_to_all | solution.py:106
  9.8 0.0 copy-start.1
  9.8 1.1 %dynamic-slice_bitcast_fusion.1 = (bf16[16,32,256]{2,1,0:T(8,128)(2,1)S(1)}, bf16[16,32,256]{2,1,0:T(8,128)(2,1)S(1)}) fusion(bf16[1,16,32,512]{3,2,1,0:T(8,128)(2,1)} %param.11, s32[]{:T(128)S(6)} %select_n.121, s32[]{:T(128)S(6)} %select_n.122), kind=kLoop, calls=%fused_computation.3 | loop fusion | bytes 1048584 | tf_op jit(solution)/shard_map/dynamic_slice | solution.py:120
  10.9 0.0 copy-start.5
  10.9 1.6 %collective-permute-start = (bf16[16,32,256]{2,1,0:T(8,128)(2,1)S(1)}, bf16[16,32,256]{2,1,0:T(8,128)(2,1)S(1)}, u32[]{:S(2)}, u32[]{:S(2)}) collective-permute-start(bf16[16,32,256]{2,1,0:T(8,128)(2,1)S(1)} %get-tuple-element.8), channel_id=1, source_target_pairs={{0,16},{16,0},{1,17},{17,1},{2,18},{18,2},{3,19},{19,3},{4,20},{20... | collective-permute-start | bytes 786440 | tf_op jit(solution)/shard_map/ppermute | solution.py:126
  12.5 0.0 copy-done.5
  12.5 0.2 select_reduce_fusion.2
  12.7 0.0 copy-done.1
  12.7 0.1 reshape.206
  12.8 0.3 fusion.2
  13.1 0.1 select_bitcast_fusion
  13.2 2.9 %all-to-all-done = s32[16,1,65]{2,1,0:T(1,128)S(1)} async-done(((s32[16,1,65]{2,1,0:T(1,128)}), s32[16,1,65]{2,1,0:T(1,128)S(1)}, u32[]{:S(2)}, u32[]{:S(2)}) %all-to-all-start) | async-done | bytes 4192 | tf_op jit(solution)/shard_map/all_to_all | solution.py:106
  16.1 0.1 compare_reduce_fusion.1
  16.2 0.1 slice_compare_fusion
  16.3 1.0 %select_select_fusion = bf16[16,64,256]{2,1,0:T(8,128)(2,1)} fusion(pred[16]{0:T(512)(128)(4,1)S(1)} %get-tuple-element.6, pred[16]{0:T(512)(128)(4,1)S(1)} %get-tuple-element.5, pred[16,64]{1,0:T(8,128)(4,1)S(1)} %slice_compare_fusion, bf16[64,256]{1,0:T(8,128)(2,1)S(1)} %get-tuple-element.21, bf16[64,256]{1,0:T(8,128)(2,1)S(1)} %get-tuple-element.22, ...), kind=kLoop, calls=%fused_computation.1 | loop fusion | flops 1310720 | bytes 721952 | tf_op jit(solution)/shard_map/jit(_where)/select_n | solution.py:113
  17.3 3.6 %all-to-all-start.1 = ((bf16[16,64,256]{2,1,0:T(8,128)(2,1)}), bf16[16,64,256]{2,1,0:T(8,128)(2,1)S(1)}, u32[]{:S(2)}, u32[]{:S(2)}) async-start(bf16[16,64,256]{2,1,0:T(8,128)(2,1)} %select_select_fusion), calls=%async_computation.1 | async-start | bytes 1048576 | tf_op jit(solution)/shard_map/all_to_all | solution.py:114
  20.9 0.1 dynamic-slice_bitcast_fusion.3
  21.0 0.1 select_reduce_fusion.1
  21.1 0.1 broadcast_select_fusion
  21.2 0.1 fusion
  21.3 0.1 select_n.109
  21.4 0.1 select_n.113
  21.4 0.6 %pad_maximum_fusion.1.bias_ref = f32[1,2048]{1,0:T(1,128)} fusion(f32[1,1024]{1,0:T(1,128)S(1)} %select_n.113, f32[1,1024]{1,0:T(1,128)S(1)} %select_n.109), kind=kLoop, calls=%fused_computation.14 | loop fusion | flops 2048 | bytes 16384 | tf_op jit(solution)/shard_map/concatenate | solution.py:138
  22.0 0.0 collective-permute-done
  22.0 0.8 %pad_maximum_fusion = bf16[16,64,256]{2,1,0:T(8,128)(2,1)} fusion(bf16[16,32,256]{2,1,0:T(8,128)(2,1)S(1)} %collective-permute-done, bf16[16,32,256]{2,1,0:T(8,128)(2,1)S(1)} %get-tuple-element.7), kind=kLoop, calls=%fused_computation | loop fusion | flops 1048576 | bytes 1048576 | tf_op jit(solution)/shard_map/concatenate | solution.py:129
  22.9 12.5 %all-to-all-done.1 = bf16[16,64,256]{2,1,0:T(8,128)(2,1)S(1)} async-done(((bf16[16,64,256]{2,1,0:T(8,128)(2,1)}), bf16[16,64,256]{2,1,0:T(8,128)(2,1)S(1)}, u32[]{:S(2)}, u32[]{:S(2)}) %all-to-all-start.1) | async-done | bytes 524320 | tf_op jit(solution)/shard_map/all_to_all | solution.py:114
  35.3 0.0 copy-start
  35.4 0.8 %copy-done = bf16[16,64,256]{2,1,0:T(8,128)(2,1)} copy-done((bf16[16,64,256]{2,1,0:T(8,128)(2,1)}, bf16[16,64,256]{2,1,0:T(8,128)(2,1)S(1)}, u32[]{:S(2)}) %copy-start) | copy-done | bytes 524312
  36.1 13.7 %shard_map.82 = bf16[384,1024]{1,0:T(8,128)(2,1)} custom-call(f32[1,2048]{1,0:T(1,128)} %pad_maximum_fusion.1.bias_ref, bf16[1024,256]{1,0:T(8,128)(2,1)} %bitcast.35, bf16[1024,256]{1,0:T(8,128)(2,1)} %bitcast.36, bf16[384,256]{1,0:T(8,128)(2,1)} %own_ref.1, bf16[384,1024]{1,0:T(8,128)(2,1)} %q_ref.1), custom_call_target="tpu_custom_call" | custom-call | flops 3825205248 | bytes 2826240 | tf_op jit(solution)/shard_map/pallas_call | solution.py:71
  (7 shorter events, 0.1 us)
Async XLA Ops:
  0.0 0.7 %copy-start.3 = (s32[48]{0:T(128)S(1)}, s32[48]{0:T(128)}, u32[]{:S(2)}) copy-start(s32[48]{0:T(128)} %param.13) | copy-start | bytes 580
  0.0 0.7 %copy-start.4 = (s32[1,16]{1,0:T(1,128)S(1)}, s32[1,16]{1,0:T(1,128)}, u32[]{:S(2)}) copy-start(s32[1,16]{1,0:T(1,128)} %param.12) | copy-start | bytes 196
  0.9 0.7 %copy-start.2 = (s32[1,16,64]{2,1,0:T(8,128)S(1)}, s32[1,16,64]{2,1,0:T(8,128)}, u32[]{:S(2)}) copy-start(s32[1,16,64]{2,1,0:T(8,128)} %param.15) | copy-start | bytes 12292
  2.4 13.7 %all-to-all-start = ((s32[16,1,65]{2,1,0:T(1,128)}), s32[16,1,65]{2,1,0:T(1,128)S(1)}, u32[]{:S(2)}, u32[]{:S(2)}) async-start(s32[16,1,65]{2,1,0:T(1,128)} %bitcast.7), calls=%async_computation | async-start | bytes 16384 | tf_op jit(solution)/shard_map/all_to_all | solution.py:106
  9.8 2.9 %copy-start.1 = (bf16[3,128,256]{2,1,0:T(8,128)(2,1)S(1)}, bf16[3,128,256]{2,1,0:T(8,128)(2,1)}, u32[]{:S(2)}) copy-start(bf16[3,128,256]{2,1,0:T(8,128)(2,1)} %param.10) | copy-start | bytes 589828
  10.9 1.6 %copy-start.5 = (s32[48]{0:T(128)S(1)}, s32[48]{0:T(128)}, u32[]{:S(2)}) copy-start(s32[48]{0:T(128)} %param.14) | copy-start | bytes 580
  10.9 11.1 %collective-permute-start = (bf16[16,32,256]{2,1,0:T(8,128)(2,1)S(1)}, bf16[16,32,256]{2,1,0:T(8,128)(2,1)S(1)}, u32[]{:S(2)}, u32[]{:S(2)}) collective-permute-start(bf16[16,32,256]{2,1,0:T(8,128)(2,1)S(1)} %get-tuple-element.8), channel_id=1, source_target_pairs={{0,16},{16,0},{1,17},{17,1},{2,18},{18,2},{3,19},{19,3},{4,20},{20... | collective-permute-start | bytes 786440 | tf_op jit(solution)/shard_map/ppermute | solution.py:126
  17.3 18.0 %all-to-all-start.1 = ((bf16[16,64,256]{2,1,0:T(8,128)(2,1)}), bf16[16,64,256]{2,1,0:T(8,128)(2,1)S(1)}, u32[]{:S(2)}, u32[]{:S(2)}) async-start(bf16[16,64,256]{2,1,0:T(8,128)(2,1)} %select_select_fusion), calls=%async_computation.1 | async-start | bytes 1048576 | tf_op jit(solution)/shard_map/all_to_all | solution.py:114
  35.3 0.8 %copy-start = (bf16[16,64,256]{2,1,0:T(8,128)(2,1)}, bf16[16,64,256]{2,1,0:T(8,128)(2,1)S(1)}, u32[]{:S(2)}) copy-start(bf16[16,64,256]{2,1,0:T(8,128)(2,1)S(1)} %all-to-all-done.1) | copy-start | bytes 1572868
